TPU v7x, 512 devices: a whole 4x4x16 slice. The times are simulated.
512 devices in a mesh: ctx: 16 (over z), ep: 32 (over y, x, core).
Axes of the slice: x: 4, y: 4, z: 16, core: 2. Of those that a mesh axis runs over, the one named last changes fastest.
Arguments:
- query_act: bfloat16 [2048, 8192], P('ctx', 'ep'), may hold values from -6 to 6
- key_act: bfloat16 [2048, 8192], P('ctx', 'ep'), may hold values from -6 to 6
- value_act: bfloat16 [2048, 8192], P('ctx', 'ep'), may hold values from -6 to 6
- state_init: float32 [64, 128, 128], P('ep'), may hold values from -128 to 128
- head_gain: float32 [8192], P('ep'), may hold values from 0.25 to 1.75
- out_weight: bfloat16 [8192, 3072], P('ctx', 'ep'), may hold values from -0.0625 to 0.0625
- stream_in: bfloat16 [2048, 3072], P('ctx', 'ep'), may hold values from -150 to 150
- model_gain: float32 [3072], replicated, may hold values from 0.25 to 1.75
- expert_ids: int32 [2048, 2], P('ctx'), may hold values from 0 to 15, as said below
- expert_slots: int32 [2048, 2], P('ctx'), may hold values from 0 to 19, as said below
- route_gates: float32 [2048, 2], P('ctx'), may hold values from 0.2 to 1
- gate_weight: bfloat16 [32, 3072, 3072], P('ep', 'ctx'), may hold values from -0.109375 to 0.109375
- up_weight: bfloat16 [32, 3072, 3072], P('ep', 'ctx'), may hold values from -0.109375 to 0.109375
- down_weight: bfloat16 [32, 3072, 3072], P('ep', 'ctx'), may hold values from -0.078125 to 0.078125
- out_grad: bfloat16 [2048, 3072], P('ctx', 'ep'), may hold values from -6 to 6
Outputs:
- layer_out: bfloat16 [2048, 3072], P('ctx', 'ep')
- grad_query: bfloat16 [2048, 8192], P('ctx', 'ep')
- grad_key: bfloat16 [2048, 8192], P('ctx', 'ep')
- grad_value: bfloat16 [2048, 8192], P('ctx', 'ep')
- grad_state: float32 [64, 128, 128], P('ep')
- grad_stream: bfloat16 [2048, 3072], P('ctx', 'ep')
Inputs may be any that keep to these rules, and one draw needn't show every extreme that they name: `expert_ids`: within each block of 128 tokens a token's two experts differ; the tokens naming expert e hold the slots 0 to n - 1 of e once each, n being their number; no expert is named by more than 20 tokens of a block, and in every block some expert by exactly 20. `expert_slots`: see expert_ids.
All inputs are finite; a program needn't handle non-finite values.
Results may differ from a plain program's by a relative error of at most 0.02.
Values may be sent and summed in bfloat16 or wider, within the bound.
No kernel may reach another device: no remote copies, remote signals or barrier semaphores. Data moves between devices by JAX's collectives and lax.ppermute only.
A program may use at most 64 MiB of HBM per device.

v0:
```python
import jax
import jax.numpy as jnp
from jax import lax
from jax.sharding import PartitionSpec as P


def carried_in(value, axis, join, neutral, backward):
    count = lax.axis_size(axis)
    place = lax.axis_index(axis)
    ahead = count - 1 - place if backward else place
    gathered = lax.all_gather(value.astype(jnp.bfloat16), axis)
    state = jnp.zeros_like(value) + jnp.asarray(neutral, value.dtype)

    def one(turn, state):
        source = count - 1 - turn if backward else turn
        return join(state, lax.dynamic_index_in_dim(gathered, source, 0, False).astype(value.dtype))

    return lax.fori_loop(0, ahead, one, state)


def head_normalize(attended, gain):
    factor = lax.rsqrt(jnp.mean(attended * attended, -1, keepdims=True) + 1e-06)
    return attended * factor * gain


def add_states(earlier, later_one):
    return earlier + later_one


def contract_last(left, right):
    return lax.dot_general(
        left, right, (((1,), (1,)), ((), ())), preferred_element_type=jnp.float32
    )


def local(
    query_act,
    key_act,
    value_act,
    state_init,
    head_gain,
    out_weight,
    stream_in,
    model_gain,
    expert_ids,
    expert_slots,
    route_gates,
    gate_weight,
    up_weight,
    down_weight,
    out_grad,
):
    f32 = jnp.float32
    high = lax.Precision.HIGHEST
    ep_count = lax.axis_size("ep")
    expert_count = ep_count // 2
    my_ep = lax.axis_index("ep")
    tokens_here = query_act.shape[0]
    head_count = state_init.shape[0]
    head_size = state_init.shape[1]
    model_width = model_gain.shape[0]
    columns = stream_in.shape[1]
    capacity = 5 * tokens_here // (2 * expert_count)
    query3 = query_act.reshape(tokens_here, head_count, head_size)
    key3 = key_act.reshape(tokens_here, head_count, head_size)
    value3 = value_act.reshape(tokens_here, head_count, head_size)
    kv_own = jnp.einsum("thd,the->hde", key3, value3, preferred_element_type=f32)
    zero_state = jnp.zeros_like(kv_own)
    before = carried_in(kv_own, "ctx", add_states, zero_state, False)
    prefix = state_init + before
    causal = jnp.arange(tokens_here)[:, None] >= jnp.arange(tokens_here)[None, :]
    scores = jnp.einsum("thd,shd->hts", query3, key3, preferred_element_type=f32)
    scores_bf = jnp.where(causal[None], scores, 0.0).astype(jnp.bfloat16)
    inside = jnp.einsum("hts,she->the", scores_bf, value3, preferred_element_type=f32)
    from_state = jnp.einsum("thd,hde->the", query3.astype(f32), prefix, precision=high)
    attended = from_state + inside
    gain_heads = head_gain.reshape(head_count, head_size)
    normed_heads = (
        head_normalize(attended, gain_heads)
        .astype(jnp.bfloat16)
        .reshape(tokens_here, head_count * head_size)
    )
    w_cols = lax.all_gather(out_weight, "ctx", axis=0, tiled=True)
    attn_proj = jnp.dot(
        lax.all_gather(normed_heads, "ep", axis=1, tiled=True), w_cols, preferred_element_type=f32
    )
    stream = (stream_in.astype(f32) + attn_proj).astype(jnp.bfloat16)
    stream_f = stream.astype(f32)
    gain_cols = lax.dynamic_slice_in_dim(model_gain, my_ep * columns, columns, 0)
    dest_expert = jnp.arange(ep_count) % expert_count
    slot_iota = jnp.arange(capacity)
    hits = (expert_ids[:, :, None, None] == dest_expert[None, None, :, None]) & (
        expert_slots[:, :, None, None] == slot_iota[None, None, None, :]
    )
    hits_f = hits.astype(f32)
    dest_picks = jnp.sum(hits_f, 1).reshape(tokens_here, ep_count * capacity)
    dest_weights = jnp.sum(hits_f * route_gates[:, :, None, None], 1).reshape(
        tokens_here, ep_count * capacity
    )
    whole_rows = lax.all_gather(stream, "ep", axis=1, tiled=True).astype(f32)
    row_scale = lax.rsqrt(jnp.mean(whole_rows * whole_rows, -1, keepdims=True) + 1e-05)
    model_in = (whole_rows * row_scale * model_gain).astype(jnp.bfloat16)
    own_select = lax.dynamic_slice_in_dim(dest_picks, my_ep * capacity, capacity, 1).T.astype(
        jnp.bfloat16
    )
    expert_in = jnp.dot(own_select, model_in, preferred_element_type=f32).astype(jnp.bfloat16)
    w_gate = gate_weight[0]
    w_up = up_weight[0]
    w_down = down_weight[0]
    hidden_block = w_gate.shape[0]
    portion = lax.all_gather(expert_in, "ctx", axis=0, tiled=True)
    projected = jnp.concatenate([contract_last(portion, w_gate), contract_last(portion, w_up)], 1)
    pre_gate = projected[:, :hidden_block]
    pre_up = projected[:, hidden_block:]
    gate_sig = jax.nn.sigmoid(pre_gate)
    activated = (pre_gate * gate_sig * pre_up).astype(jnp.bfloat16)
    half_out = lax.psum_scatter(
        jnp.dot(activated, w_down, preferred_element_type=f32).astype(jnp.bfloat16),
        "ctx",
        scatter_dimension=0,
        tiled=True,
    )
    returned = lax.all_to_all(half_out, "ep", split_axis=1, concat_axis=0, tiled=True)
    expert_mix = jnp.dot(dest_weights, returned.astype(f32), precision=high)
    layer_out = (stream_f + expert_mix).astype(jnp.bfloat16)
    grad_out = out_grad.astype(f32)
    grad_send = jnp.dot(dest_weights.T, grad_out, precision=high).astype(jnp.bfloat16)
    grad_in = lax.all_to_all(grad_send, "ep", split_axis=0, concat_axis=1, tiled=True)
    grad_act = contract_last(lax.all_gather(grad_in, "ctx", axis=0, tiled=True), w_down)
    grad_gate_pre = (grad_act * pre_up * gate_sig * (1.0 + pre_gate * (1.0 - gate_sig))).astype(
        jnp.bfloat16
    )
    grad_up_pre = (grad_act * pre_gate * gate_sig).astype(jnp.bfloat16)
    grad_half = lax.psum_scatter(
        (
            jnp.dot(grad_gate_pre, w_gate, preferred_element_type=f32)
            + jnp.dot(grad_up_pre, w_up, preferred_element_type=f32)
        ).astype(jnp.bfloat16),
        "ctx",
        scatter_dimension=0,
        tiled=True,
    )
    grad_back = lax.all_to_all(grad_half, "ep", split_axis=1, concat_axis=0, tiled=True)
    grad_model_in = jnp.dot(dest_picks, grad_back.astype(f32), precision=high)
    scaled_grad = grad_model_in * gain_cols
    inner_sum = lax.psum(jnp.sum(stream_f * scaled_grad, -1), "ep")
    grad_stream = (
        grad_out
        + row_scale * scaled_grad
        - stream_f * row_scale**3 * inner_sum[:, None] / model_width
    ).astype(jnp.bfloat16)
    w_rows = lax.all_to_all(w_cols, "ep", split_axis=0, concat_axis=1, tiled=True)
    grad_heads = contract_last(lax.all_gather(grad_stream, "ep", axis=1, tiled=True), w_rows)
    head_pull = jax.vjp(lambda value: head_normalize(value, gain_heads), attended)[1]
    grad_attended = head_pull(grad_heads.reshape(tokens_here, head_count, head_size))[0].astype(
        jnp.bfloat16
    )
    state_part = jnp.einsum("thd,the->hde", query3, grad_attended, preferred_element_type=f32)
    later_sum = carried_in(state_part, "ctx", add_states, zero_state, True)
    state_total = lax.psum(state_part.astype(jnp.bfloat16), "ctx").astype(jnp.float32)
    grad_scores = jnp.einsum("the,she->hts", grad_attended, value3, preferred_element_type=f32)
    grad_masked = jnp.where(causal[None], grad_scores, 0.0).astype(jnp.bfloat16)
    grad_att_f = grad_attended.astype(f32)
    grad_query = jnp.einsum("the,hde->thd", grad_att_f, prefix, precision=high) + jnp.einsum(
        "hts,shd->thd", grad_masked, key3, preferred_element_type=f32
    )
    grad_key = jnp.einsum(
        "the,hde->thd", value3.astype(f32), later_sum, precision=high
    ) + jnp.einsum("hts,thd->shd", grad_masked, query3, preferred_element_type=f32)
    grad_value = jnp.einsum(
        "thd,hde->the", key3.astype(f32), later_sum, precision=high
    ) + jnp.einsum("hts,the->she", scores_bf, grad_attended, preferred_element_type=f32)
    flat_shape = (tokens_here, head_count * head_size)
    return (
        layer_out,
        grad_query.astype(jnp.bfloat16).reshape(flat_shape),
        grad_key.astype(jnp.bfloat16).reshape(flat_shape),
        grad_value.astype(jnp.bfloat16).reshape(flat_shape),
        state_total,
        grad_stream,
    )


def solution(mesh):
    return jax.shard_map(
        local,
        mesh=mesh,
        in_specs=(
            P("ctx", "ep"),
            P("ctx", "ep"),
            P("ctx", "ep"),
            P("ep", None, None),
            P("ep"),
            P("ctx", "ep"),
            P("ctx", "ep"),
            P(),
            P("ctx", None),
            P("ctx", None),
            P("ctx", None),
            P("ep", "ctx", None),
            P("ep", "ctx", None),
            P("ep", "ctx", None),
            P("ctx", "ep"),
        ),
        out_specs=(
            P("ctx", "ep"),
            P("ctx", "ep"),
            P("ctx", "ep"),
            P("ctx", "ep"),
            P("ep", None, None),
            P("ctx", "ep"),
        ),
        check_vma=False,
    )
```

profile of v0, /device:TPU:1, one launch (start us, length us, event | category | flops | bytes accessed | tf_op | source)
XLA Modules:
  0.0 788.4 jit_solution(11163868636489932232)
XLA Ops:
  7.2 1.1 copy.182
  8.3 1.6 convolution_convert_fusion.4
  10.8 1.0 copy.145
  11.8 1.1 fusion.25
  12.9 63.4 %all-gather.15.cloned.1.call-done = bf16[32,128,128]{2,1,0:T(8,128)(2,1)} async-done(((bf16[2,128,128]{2,1,0:T(8,128)(2,1)}), bf16[32,128,128]{2,1,0:T(8,128)(2,1)}) %all-gather.15.cloned.1.call-update) | async-done | bytes 1048592 | tf_op jit(solution)/shard_map/all_gather | solution.py:11
  79.0 25.9 %all_to_all.67 = bf16[32,20,96]{2,1,0:T(8,128)(2,1)S(1)} all-to-all(bf16[32,20,96]{2,1,0:T(8,128)(2,1)S(1)} %all_to_all.53), channel_id=1, replica_groups=mesh['ctx'=16,'ep'=32] {'ep'}, dimensions={0} | all-to-all | bytes 245760 | tf_op jit(solution)/shard_map/all_to_all | solution.py:128
  106.2 41.4 %all-gather.13.cloned.1.call-done = bf16[8192,96]{0,1:T(8,128)(2,1)} async-done(((bf16[512,96]{0,1:T(8,128)(2,1)}), bf16[8192,96]{0,1:T(8,128)(2,1)}) %all-gather.13.cloned.1.call-update) | async-done | bytes 1572880 | tf_op jit(solution)/shard_map/all_gather | solution.py:83
  147.6 70.2 %all-gather.11.cloned.1.call-done = bf16[128,8192]{0,1:T(8,128)(2,1)} async-done(((bf16[128,256]{0,1:T(8,128)(2,1)}), bf16[128,8192]{0,1:T(8,128)(2,1)}) %all-gather.11.cloned.1.call-update) | async-done | bytes 2097168 | tf_op jit(solution)/shard_map/all_gather | solution.py:85
  217.8 2.6 fusion.33
  221.1 24.4 %all_gather.34 = bf16[128,3072]{0,1:T(8,128)(2,1)S(1)} all-gather(bf16[128,96]{0,1:T(8,128)(2,1)S(1)} %fusion.33), channel_id=1, replica_groups=mesh['ctx'=16,'ep'=32] {'ep'}, dimensions={1}, use_global_device_ids=true | all-gather | bytes 811008 | tf_op jit(solution)/shard_map/all_gather | solution.py:100
  246.4 1.3 fusion.3
  247.7 1.4 copy.189
  249.1 4.5 all-to-all-start.3
  253.6 30.3 %all-gather.21.cloned.1.call-done = bf16[16,20,3072]{2,1,0:T(8,128)(2,1)} async-done(((bf16[1,20,3072]{2,1,0:T(8,128)(2,1)}), bf16[16,20,3072]{2,1,0:T(8,128)(2,1)}) %all-gather.21.cloned.1.call-update) | async-done | bytes 1966096 | tf_op jit(solution)/shard_map/all_gather | solution.py:129
  284.0 2.6 reshape.145
  286.5 1.6 fusion.9
  288.2 66.8 %all-gather.19.cloned.1.call-done = bf16[16,20,3072]{2,1,0:T(8,128)(2,1)} async-done(((bf16[1,20,3072]{2,1,0:T(8,128)(2,1)}), bf16[16,20,3072]{2,1,0:T(8,128)(2,1)}) %all-gather.19.cloned.1.call-update) | async-done | bytes 1966096 | tf_op jit(solution)/shard_map/all_gather | solution.py:111
  355.0 2.6 reshape.143
  357.6 2.3 fusion.17
  359.9 0.9 fusion.13
  363.0 2.0 fusion.2
  365.0 49.0 %fusion.70 = (bf16[24,3072]{1,0:T(8,128)(2,1)}, bf16[24,3072]{1,0:T(8,128)(2,1)}) fusion(bf16[320,3072]{1,0:T(8,128)(2,1)S(1)} %convolution_convert_fusion, bf16[320,3072]{1,0:T(8,128)(2,1)} %fusion.2), kind=kCustom, calls=%all-reduce-scatter.2 | all-reduce-scatter fusion | flops 2359297 | bytes 4229120
  414.0 1.0 slice
  415.0 3.0 collective-permute-start
  417.9 4.3 collective-permute-start.1
  422.2 4.1 collective-permute-start.2
  426.3 2.2 collective-permute-start.3
  428.5 3.8 collective-permute-start.4
  432.3 0.9 slice.1
  433.2 4.5 collective-permute-start.5
  437.7 1.3 dynamic-slice.6
  439.7 2.5 concatenate
  442.2 1.0 concatenate.1
  444.9 27.2 %all-to-all-start.2 = ((bf16[20,32,96]{2,0,1:T(8,128)(2,1)}), bf16[20,32,96]{2,0,1:T(8,128)(2,1)}, u32[]{:S(2)}, u32[]{:S(2)}) async-start(bf16[20,32,96]{2,0,1:T(8,128)(2,1)} %copy.119), calls=%async_computation.2 | async-start | bytes 393216 | tf_op jit(solution)/shard_map/all_to_all | solution.py:143
  472.6 2.4 dot_general.89
  475.1 5.3 all-to-all-done.2
  480.4 2.5 fusion.60
  482.9 62.2 %psum.14 = f32[128]{0:T(128)S(1)} all-reduce(f32[128]{0:T(128)} %get-tuple-element.145), channel_id=1, replica_groups=mesh['ctx'=16,'ep'=32] {'ep'}, use_global_device_ids=true, to_apply=%region_9.10 | all-reduce | flops 128 | bytes 1024 | tf_op jit(solution)/shard_map/psum | solution.py:146
  546.5 24.2 %all_gather.37 = bf16[128,3072]{0,1:T(8,128)(2,1)S(1)} all-gather(bf16[128,96]{0,1:T(8,128)(2,1)S(1)} %fusion.59), channel_id=1, replica_groups=mesh['ctx'=16,'ep'=32] {'ep'}, dimensions={1}, use_global_device_ids=true | all-gather | bytes 811008 | tf_op jit(solution)/shard_map/all_gather | solution.py:153
  570.7 1.5 multiply_reduce_fusion
  574.6 1.1 all_to_all.50
  576.4 5.6 all-to-all-start
  583.5 6.8 all-to-all-done
  590.3 1.0 fusion.34
  591.3 104.4 %all-reduce.7.cloned.1.call-done = bf16[2,128,128]{1,2,0:T(8,128)(2,1)} async-done(((bf16[2,128,128]{1,2,0:T(8,128)(2,1)}), bf16[2,128,128]{1,2,0:T(8,128)(2,1)}) %all-reduce.7.cloned.1.call-update) | async-done | bytes 65552 | tf_op jit(solution)/shard_map/psum | solution.py:160
  695.7 1.6 copy.136
  697.3 68.5 %all-gather.17.cloned.1.call-done = bf16[32,128,128]{2,1,0:T(8,128)(2,1)} async-done(((bf16[2,128,128]{2,1,0:T(8,128)(2,1)}), bf16[32,128,128]{2,1,0:T(8,128)(2,1)}) %all-gather.17.cloned.1.call-update) | async-done | bytes 1048592 | tf_op jit(solution)/shard_map/all_gather | solution.py:11
  765.8 13.4 %while.23 = (s32[]{:T(128)}, f32[2,128,128]{2,1,0:T(8,128)S(1)}, s32[]{:T(128)}, bf16[16,2,128,128]{3,2,1,0:T(8,128)(2,1)}, s32[]{:T(128)}, /*index=5*/s32[]{:T(128)}, s32[]{:T(128)}, s32[]{:T(128)}) while((s32[]{:T(128)}, f32[2,128,128]{2,1,0:T(8,128)S(1)}, s32[]{:T(128)}, bf16[16,2,128,128]{3,2,1,0:T(8,128)(2,1)}, s32[]{:T(128)}, ...), condition=%wide.region_12.13_spmd, body=%wide.region_11.12_spmd.sunk | while | flops 65542 | bytes 327815 | solution.py:18
  (158 shorter events, 31.5 us)
Async XLA Ops:
  7.2 279.4 %copy-start = (bf16[1,192,3072]{2,1,0:T(8,128)(2,1)S(1)}, bf16[1,192,3072]{2,1,0:T(8,128)(2,1)}, u32[]{:S(2)}) copy-start(bf16[1,192,3072]{2,1,0:T(8,128)(2,1)} %param.32) | copy-start | bytes 3538948
  7.2 69.2 %copy-start.24 = (f32[2,128,128]{2,1,0:T(8,128)S(1)}, f32[2,128,128]{2,1,0:T(8,128)}, u32[]{:S(2)}) copy-start(f32[2,128,128]{2,1,0:T(8,128)} %param.22) | copy-start | bytes 393220
  7.2 69.1 %all-gather.15.cloned.1.call-start = ((), (), s32[]{:S(2)}) async-start(), calls=%async_computation.7 | async-start | bytes 1114112 | tf_op jit(solution)/shard_map/all_gather | solution.py:11
  8.3 68.0 %copy-start.16 = (bf16[128,256]{0,1:T(8,128)(2,1)}, bf16[128,256]{0,1:T(8,128)(2,1)S(1)}, u32[]{:S(2)}) copy-start(bf16[128,256]{0,1:T(8,128)(2,1)S(1)} %copy.182) | copy-start | bytes 196612
  10.0 66.8 %copy-start.18 = (bf16[128,256]{1,0:T(8,128)(2,1)S(1)}, bf16[128,256]{1,0:T(8,128)(2,1)}, u32[]{:S(2)}) copy-start(bf16[128,256]{1,0:T(8,128)(2,1)} %param.21) | copy-start | bytes 196612
  10.0 137.6 %all-gather.13.cloned.1.call-start = ((), (), s32[]{:S(2)}) async-start(), calls=%async_computation.5 | async-start | bytes 1671168 | tf_op jit(solution)/shard_map/all_gather | solution.py:83
  10.7 207.1 %all-gather.11.cloned.1.call-start = ((), (), s32[]{:S(2)}) async-start(), calls=%async_computation.4 | async-start | bytes 2162688 | tf_op jit(solution)/shard_map/all_gather | solution.py:85
  11.7 65.2 %copy-start.12 = (bf16[128,256]{0,1:T(8,128)(2,1)}, bf16[128,256]{0,1:T(8,128)(2,1)S(1)}, u32[]{:S(2)}) copy-start(bf16[128,256]{0,1:T(8,128)(2,1)S(1)} %copy.145) | copy-start | bytes 196612
  12.9 64.9 %copy-start.22 = (bf16[2,128,128]{2,1,0:T(8,128)(2,1)}, bf16[2,128,128]{2,1,0:T(8,128)(2,1)S(1)}, u32[]{:S(2)}) copy-start(bf16[2,128,128]{2,1,0:T(8,128)(2,1)S(1)} %fusion.25) | copy-start | bytes 196612
  12.9 64.2 %copy-start.33 = (f32[256]{0:T(256)S(1)}, f32[256]{0:T(256)}, u32[]{:S(2)}) copy-start(f32[256]{0:T(256)} %param.23) | copy-start | bytes 3076
  76.3 1.5 copy-start.34
  76.3 1.6 copy-start.35
  76.4 1.7 copy-start.32
  76.4 1.5 copy-start.5
  76.4 2.0 copy-start.26
  77.8 206.2 %all-gather.21.cloned.1.call-start = ((), (), s32[]{:S(2)}) async-start(), calls=%async_computation.10 | async-start | bytes 2506752 | tf_op jit(solution)/shard_map/all_gather | solution.py:129
  78.2 27.8 %copy-start.2 = (f32[128,32,20]{0,1,2:T(8,128)}, f32[128,32,20]{0,1,2:T(8,128)S(1)}, u32[]{:S(2)}) copy-start(f32[128,32,20]{0,1,2:T(8,128)S(1)} %get-tuple-element.119) | copy-start | bytes 983044
  78.4 139.4 %copy-start.27 = (bf16[128,96]{0,1:T(8,128)(2,1)S(1)}, bf16[128,96]{0,1:T(8,128)(2,1)}, u32[]{:S(2)}) copy-start(bf16[128,96]{0,1:T(8,128)(2,1)} %param.25) | copy-start | bytes 73732
  105.9 249.1 %all-gather.19.cloned.1.call-start = ((), (), s32[]{:S(2)}) async-start(), calls=%async_computation.9 | async-start | bytes 2506752 | tf_op jit(solution)/shard_map/all_gather | solution.py:111
  221.1 25.4 %copy-start.37 = (f32[3072]{0:T(1024)S(1)}, f32[3072]{0:T(1024)}, u32[]{:S(2)}) copy-start(f32[3072]{0:T(1024)} %param.26) | copy-start | bytes 36868
  221.1 26.7 %copy-start.1 = (bf16[8192,96]{0,1:T(8,128)(2,1)S(1)}, bf16[8192,96]{0,1:T(8,128)(2,1)}, u32[]{:S(2)}) copy-start(bf16[8192,96]{0,1:T(8,128)(2,1)} %all-gather.13.cloned.1.call-done) | copy-start | bytes 4718596
  246.4 2.7 copy-start.36
  249.1 195.8 %all-to-all-start.3 = ((bf16[32,256,96]{1,2,0:T(8,128)(2,1)}), bf16[32,256,96]{1,2,0:T(8,128)(2,1)}, u32[]{:S(2)}, u32[]{:S(2)}) async-start(bf16[32,256,96]{1,2,0:T(8,128)(2,1)} %bitcast.161), calls=%async_computation.3 | async-start | bytes 3145728 | tf_op jit(solution)/shard_map/all_to_all | solution.py:152
  357.6 2.3 copy-start.10
  360.8 1.0 copy-start.4
  360.9 1.4 copy-start.9
  414.0 28.2 %copy-start.11 = (bf16[24,3072]{1,0:T(8,128)(2,1)S(1)}, bf16[24,3072]{1,0:T(8,128)(2,1)}, u32[]{:S(2)}) copy-start(bf16[24,3072]{1,0:T(8,128)(2,1)} %get-tuple-element.140) | copy-start | bytes 442372
  415.0 24.7 %collective-permute-start = (bf16[24,3072]{1,0:T(8,128)(2,1)}, bf16[24,3072]{1,0:T(8,128)(2,1)S(1)}, u32[]{:S(2)}, u32[]{:S(2)}) collective-permute-start(bf16[24,3072]{1,0:T(8,128)(2,1)} %get-tuple-element.139), channel_id=1, source_target_pairs={{0,32},{32,64},{64,96},{96,128},{128,160},{160,192},{192,224},{224... | collective-permute-start | bytes 442376
  417.9 21.7 %collective-permute-start.1 = (bf16[24,3072]{1,0:T(8,128)(2,1)}, bf16[24,3072]{1,0:T(8,128)(2,1)S(1)}, u32[]{:S(2)}, u32[]{:S(2)}) collective-permute-start(bf16[24,3072]{1,0:T(8,128)(2,1)} %get-tuple-element.139), channel_id=1, source_target_pairs={{0,64},{32,96},{64,128},{96,160},{128,192},{160,224},{192,256},{22... | collective-permute-start | bytes 442376
  422.2 11.0 %collective-permute-start.2 = (bf16[12,3072]{1,0:T(8,128)(2,1)S(1)}, bf16[12,3072]{1,0:T(8,128)(2,1)S(1)}, u32[]{:S(2)}, u32[]{:S(2)}) collective-permute-start(bf16[12,3072]{1,0:T(8,128)(2,1)S(1)} %slice), channel_id=1, source_target_pairs={{0,96},{32,128},{64,160},{96,192},{128,224},{160,256},{192,288},{2... | collective-permute-start | bytes 221192
  426.3 15.8 %collective-permute-start.3 = (bf16[24,3072]{1,0:T(8,128)(2,1)}, bf16[24,3072]{1,0:T(8,128)(2,1)S(1)}, u32[]{:S(2)}, u32[]{:S(2)}) collective-permute-start(bf16[24,3072]{1,0:T(8,128)(2,1)} %get-tuple-element.140), channel_id=1, source_target_pairs={{0,32},{32,64},{64,96},{96,128},{128,160},{160,192},{192,224},{224... | collective-permute-start | bytes 442376
  428.5 13.7 %collective-permute-start.4 = (bf16[24,3072]{1,0:T(8,128)(2,1)}, bf16[24,3072]{1,0:T(8,128)(2,1)S(1)}, u32[]{:S(2)}, u32[]{:S(2)}) collective-permute-start(bf16[24,3072]{1,0:T(8,128)(2,1)} %get-tuple-element.140), channel_id=1, source_target_pairs={{0,64},{32,96},{64,128},{96,160},{128,192},{160,224},{192,256},{22... | collective-permute-start | bytes 442376
  433.2 8.9 %collective-permute-start.5 = (bf16[12,3072]{1,0:T(8,128)(2,1)S(1)}, bf16[12,3072]{1,0:T(8,128)(2,1)S(1)}, u32[]{:S(2)}, u32[]{:S(2)}) collective-permute-start(bf16[12,3072]{1,0:T(8,128)(2,1)S(1)} %slice.1), channel_id=1, source_target_pairs={{0,96},{32,128},{64,160},{96,192},{128,224},{160,256},{192,288},{2... | collective-permute-start | bytes 221192
  444.9 35.5 %all-to-all-start.2 = ((bf16[20,32,96]{2,0,1:T(8,128)(2,1)}), bf16[20,32,96]{2,0,1:T(8,128)(2,1)}, u32[]{:S(2)}, u32[]{:S(2)}) async-start(bf16[20,32,96]{2,0,1:T(8,128)(2,1)} %copy.119), calls=%async_computation.2 | async-start | bytes 393216 | tf_op jit(solution)/shard_map/all_to_all | solution.py:143
  472.6 7.7 copy-start.3
  472.6 98.1 %copy-start.8 = (f32[128,2,128]{0,2,1:T(8,128)S(1)}, f32[128,2,128]{0,2,1:T(8,128)}, u32[]{:S(2)}) copy-start(f32[128,2,128]{0,2,1:T(8,128)} %copy-done.7) | copy-start | bytes 393220
  570.7 1.6 copy-start.31
  570.7 1.6 copy-start.29
  570.7 1.6 copy-start.13
  572.2 9.9 %copy-start.19 = (bf16[128,256]{1,0:T(8,128)(2,1)S(1)}, bf16[128,256]{1,0:T(8,128)(2,1)}, u32[]{:S(2)}) copy-start(bf16[128,256]{1,0:T(8,128)(2,1)} %param.21) | copy-start | bytes 196612
  572.2 10.1 %copy-start.6 = (f32[2,128,128]{2,1,0:T(8,128)S(1)}, f32[2,128,128]{2,1,0:T(8,128)}, u32[]{:S(2)}) copy-start(f32[2,128,128]{2,1,0:T(8,128)} %copy-done.5) | copy-start | bytes 393220
  572.2 10.3 %copy-start.17 = (bf16[128,256]{0,1:T(8,128)(2,1)S(1)}, bf16[128,256]{0,1:T(8,128)(2,1)}, u32[]{:S(2)}) copy-start(bf16[128,256]{0,1:T(8,128)(2,1)} %copy-done.16) | copy-start | bytes 196612
  572.3 18.1 %copy-start.15 = (bf16[128,96]{0,1:T(8,128)(2,1)S(1)}, bf16[128,96]{0,1:T(8,128)(2,1)}, u32[]{:S(2)}) copy-start(bf16[128,96]{0,1:T(8,128)(2,1)} %copy-done.14) | copy-start | bytes 73732
  573.3 122.4 %all-reduce.7.cloned.1.call-start = ((), (), s32[]{:S(2)}) async-start(), calls=%async_computation.6 | async-start | bytes 131072 | tf_op jit(solution)/shard_map/psum | solution.py:160
  573.8 192.0 %all-gather.17.cloned.1.call-start = ((), (), s32[]{:S(2)}) async-start(), calls=%async_computation.8 | async-start | bytes 1114112 | tf_op jit(solution)/shard_map/all_gather | solution.py:11
  576.4 13.9 %all-to-all-start = ((bf16[20,32,96]{2,0,1:T(8,128)(2,1)}), bf16[20,32,96]{2,0,1:T(8,128)(2,1)S(1)}, u32[]{:S(2)}, u32[]{:S(2)}) async-start(bf16[20,32,96]{2,0,1:T(8,128)(2,1)} %copy.114), calls=%async_computation | async-start | bytes 393216 | tf_op jit(solution)/shard_map/all_to_all | solution.py:123
  582.5 196.7 %copy-start.21 = (bf16[128,256]{1,0:T(8,128)(2,1)S(1)}, bf16[128,256]{1,0:T(8,128)(2,1)}, u32[]{:S(2)}) copy-start(bf16[128,256]{1,0:T(8,128)(2,1)} %param.20) | copy-start | bytes 196612
  590.3 189.4 %copy-start.23 = (bf16[2,128,128]{2,1,0:T(8,128)(2,1)S(1)}, bf16[2,128,128]{2,1,0:T(8,128)(2,1)}, u32[]{:S(2)}) copy-start(bf16[2,128,128]{2,1,0:T(8,128)(2,1)} %copy-done.22) | copy-start | bytes 196612
  (6 other events, 4.7 us)
Sparse Core Ops, SparseCore 0:
  10.7 65.6 all-gather.14
  78.4 69.1 all-gather.12
  151.3 66.4 all-gather.10
  219.7 64.1 all-gather.20
  285.9 69.0 all-gather.18
  576.1 119.5 all-reduce.6
  698.3 67.4 all-gather.16
where the time goes:
time: 800 us; the launch traced here: 788 us
  waiting for transfers between devices  459 us (57%)
  blocking collectives  186 us (23%)
  starting transfers between devices  59.3 us (7%)
  local copies, waits for them, and re-layouts  29.8 us (4%)
  matrix products  22.4 us (3%)
  other arithmetic  15.8 us (2%)
  between operations  15.6 us (2%)
    all_gather x2, waiting for transfers between devices, carried_in(): gathered = lax.all_gather(value.astype(jnp.bfloat16), axis)  132 us
    psum x1, waiting for transfers between devices, local(): lax.psum(state_part.astype(jnp.bfloat16), 'ctx').astype(jnp.float32)  104 us
    all_gather x1, waiting for transfers between devices, local(): lax.all_gather(normed_heads, 'ep', axis=1, tiled=True)  70.2 us
    all_gather x1, waiting for transfers between devices, local(): portion = lax.all_gather(expert_in, 'ctx', axis=0, tiled=True)  66.8 us
    psum x1, blocking collectives, local(): inner_sum = lax.psum(jnp.sum(stream_f * scaled_grad, -1), 'ep')  62.2 us
    unnamed x1, blocking collectives  49 us
    all_gather x1, waiting for transfers between devices, local(): w_cols = lax.all_gather(out_weight, 'ctx', axis=0, tiled=True)  41.4 us
    all_gather x1, waiting for transfers between devices, local(): lax.all_gather(grad_in, 'ctx', axis=0, tiled=True)  30.3 us
  transfers between devices with their start and end apart: 16, of which 9 were waited for; matrix products, arithmetic and copies ran while one was open for 11% of the time, Pallas kernels for 0%

commit v1 on v0

--- a/solution.py
+++ b/solution.py
@@ -4,27 +4,31 @@
 from jax.sharding import PartitionSpec as P
 
 
-def carried_in(value, axis, join, neutral, backward):
+def butterfly_sums(value, axis, backward):
     count = lax.axis_size(axis)
     place = lax.axis_index(axis)
-    ahead = count - 1 - place if backward else place
-    gathered = lax.all_gather(value.astype(jnp.bfloat16), axis)
-    state = jnp.zeros_like(value) + jnp.asarray(neutral, value.dtype)
-
-    def one(turn, state):
-        source = count - 1 - turn if backward else turn
-        return join(state, lax.dynamic_index_in_dim(gathered, source, 0, False).astype(value.dtype))
-
-    return lax.fori_loop(0, ahead, one, state)
+    total = value
+    carried = jnp.zeros_like(value)
+    step = 1
+    while step < count:
+        other = lax.ppermute(total, axis, [(i, i ^ step) for i in range(count)])
+        upper = (place & step) != 0
+        take = jnp.logical_not(upper) if backward else upper
+        carried = carried + jnp.where(take, other, jnp.zeros_like(other))
+        total = total + other
+        step *= 2
+    return carried, total
+
+
+def gather_blocks(value, axis):
+    count = lax.axis_size(axis)
+    spread = jnp.broadcast_to(value[None], (count,) + value.shape)
+    return lax.all_to_all(spread, axis, 0, 0, tiled=True)
 
 
 def head_normalize(attended, gain):
     factor = lax.rsqrt(jnp.mean(attended * attended, -1, keepdims=True) + 1e-06)
     return attended * factor * gain
-
-
-def add_states(earlier, later_one):
-    return earlier + later_one
 
 
 def contract_last(left, right):
@@ -61,12 +65,12 @@
     model_width = model_gain.shape[0]
     columns = stream_in.shape[1]
     capacity = 5 * tokens_here // (2 * expert_count)
+    w_cols = lax.all_gather(out_weight, "ctx", axis=0, tiled=True)
     query3 = query_act.reshape(tokens_here, head_count, head_size)
     key3 = key_act.reshape(tokens_here, head_count, head_size)
     value3 = value_act.reshape(tokens_here, head_count, head_size)
     kv_own = jnp.einsum("thd,the->hde", key3, value3, preferred_element_type=f32)
-    zero_state = jnp.zeros_like(kv_own)
-    before = carried_in(kv_own, "ctx", add_states, zero_state, False)
+    before, _ = butterfly_sums(kv_own, "ctx", False)
     prefix = state_init + before
     causal = jnp.arange(tokens_here)[:, None] >= jnp.arange(tokens_here)[None, :]
     scores = jnp.einsum("thd,shd->hts", query3, key3, preferred_element_type=f32)
@@ -80,9 +84,9 @@
         .astype(jnp.bfloat16)
         .reshape(tokens_here, head_count * head_size)
     )
-    w_cols = lax.all_gather(out_weight, "ctx", axis=0, tiled=True)
-    attn_proj = jnp.dot(
-        lax.all_gather(normed_heads, "ep", axis=1, tiled=True), w_cols, preferred_element_type=f32
+    w_blocks = w_cols.reshape(ep_count, head_count * head_size, columns)
+    attn_proj = jnp.einsum(
+        "ith,ihf->tf", gather_blocks(normed_heads, "ep"), w_blocks, preferred_element_type=f32
     )
     stream = (stream_in.astype(f32) + attn_proj).astype(jnp.bfloat16)
     stream_f = stream.astype(f32)
@@ -97,18 +101,22 @@
     dest_weights = jnp.sum(hits_f * route_gates[:, :, None, None], 1).reshape(
         tokens_here, ep_count * capacity
     )
-    whole_rows = lax.all_gather(stream, "ep", axis=1, tiled=True).astype(f32)
-    row_scale = lax.rsqrt(jnp.mean(whole_rows * whole_rows, -1, keepdims=True) + 1e-05)
-    model_in = (whole_rows * row_scale * model_gain).astype(jnp.bfloat16)
-    own_select = lax.dynamic_slice_in_dim(dest_picks, my_ep * capacity, capacity, 1).T.astype(
-        jnp.bfloat16
-    )
-    expert_in = jnp.dot(own_select, model_in, preferred_element_type=f32).astype(jnp.bfloat16)
+    picked = jnp.dot(
+        dest_picks.T.astype(jnp.bfloat16), stream, preferred_element_type=f32
+    ).astype(jnp.bfloat16)
+    arrived = lax.all_to_all(
+        picked.reshape(ep_count, capacity, columns), "ep", 0, 0, tiled=True
+    )
+    slot_rows = arrived.transpose(1, 0, 2).reshape(capacity, model_width).astype(f32)
+    slot_scale = lax.rsqrt(jnp.mean(slot_rows * slot_rows, -1, keepdims=True) + 1e-05)
+    expert_in = (slot_rows * slot_scale * model_gain).astype(jnp.bfloat16)
     w_gate = gate_weight[0]
     w_up = up_weight[0]
     w_down = down_weight[0]
     hidden_block = w_gate.shape[0]
+    w_rows = lax.all_to_all(w_blocks, "ep", 0, 0, tiled=True)
     portion = lax.all_gather(expert_in, "ctx", axis=0, tiled=True)
+    portion, w_rows = lax.optimization_barrier((portion, w_rows))
     projected = jnp.concatenate([contract_last(portion, w_gate), contract_last(portion, w_up)], 1)
     pre_gate = projected[:, :hidden_block]
     pre_up = projected[:, hidden_block:]
@@ -120,9 +128,6 @@
         scatter_dimension=0,
         tiled=True,
     )
-    returned = lax.all_to_all(half_out, "ep", split_axis=1, concat_axis=0, tiled=True)
-    expert_mix = jnp.dot(dest_weights, returned.astype(f32), precision=high)
-    layer_out = (stream_f + expert_mix).astype(jnp.bfloat16)
     grad_out = out_grad.astype(f32)
     grad_send = jnp.dot(dest_weights.T, grad_out, precision=high).astype(jnp.bfloat16)
     grad_in = lax.all_to_all(grad_send, "ep", split_axis=0, concat_axis=1, tiled=True)
@@ -143,21 +148,30 @@
     grad_back = lax.all_to_all(grad_half, "ep", split_axis=1, concat_axis=0, tiled=True)
     grad_model_in = jnp.dot(dest_picks, grad_back.astype(f32), precision=high)
     scaled_grad = grad_model_in * gain_cols
-    inner_sum = lax.psum(jnp.sum(stream_f * scaled_grad, -1), "ep")
+    row_parts = jnp.stack(
+        [jnp.sum(stream_f * stream_f, -1), jnp.sum(stream_f * scaled_grad, -1)], -1
+    )
+    row_sums = jnp.sum(gather_blocks(row_parts, "ep"), 0)
+    row_scale = lax.rsqrt(row_sums[:, :1] / model_width + 1e-05)
+    inner_sum = row_sums[:, 1:]
     grad_stream = (
         grad_out
         + row_scale * scaled_grad
-        - stream_f * row_scale**3 * inner_sum[:, None] / model_width
+        - stream_f * row_scale**3 * inner_sum / model_width
     ).astype(jnp.bfloat16)
-    w_rows = lax.all_to_all(w_cols, "ep", split_axis=0, concat_axis=1, tiled=True)
-    grad_heads = contract_last(lax.all_gather(grad_stream, "ep", axis=1, tiled=True), w_rows)
+    grad_heads = jnp.einsum(
+        "itf,ihf->th", gather_blocks(grad_stream, "ep"), w_rows, preferred_element_type=f32
+    )
     head_pull = jax.vjp(lambda value: head_normalize(value, gain_heads), attended)[1]
     grad_attended = head_pull(grad_heads.reshape(tokens_here, head_count, head_size))[0].astype(
         jnp.bfloat16
     )
     state_part = jnp.einsum("thd,the->hde", query3, grad_attended, preferred_element_type=f32)
-    later_sum = carried_in(state_part, "ctx", add_states, zero_state, True)
-    state_total = lax.psum(state_part.astype(jnp.bfloat16), "ctx").astype(jnp.float32)
+    half_out, state_part = lax.optimization_barrier((half_out, state_part))
+    returned = lax.all_to_all(half_out, "ep", split_axis=1, concat_axis=0, tiled=True)
+    expert_mix = jnp.dot(dest_weights, returned.astype(f32), precision=high)
+    layer_out = (stream_f + expert_mix).astype(jnp.bfloat16)
+    later_sum, state_total = butterfly_sums(state_part, "ctx", True)
     grad_scores = jnp.einsum("the,she->hts", grad_attended, value3, preferred_element_type=f32)
     grad_masked = jnp.where(causal[None], grad_scores, 0.0).astype(jnp.bfloat16)
     grad_att_f = grad_attended.astype(f32)

time: 800 us -> 469 us (0.59); the launches traced: 788 us -> 467 us
  waiting for transfers between devices: 459 us -> 187 us
  blocking collectives: 186 us -> 72.6 us
  starting transfers between devices: 59.3 us -> 133 us
  other arithmetic: 15.8 us -> 5.61 us
    all_gather x3 -> x0, waiting for transfers between devices: 202 us -> none  [the longest x2 132 us: carried_in(): gathered = lax.all_gather(value.astype(jnp.bfloat16), axis)]
    psum x1 -> x0, waiting for transfers between devices: 104 us -> none  [local(): lax.psum(state_part.astype(jnp.bfloat16), 'ctx').astype(jnp.float32)]
    psum x1 -> x0, blocking collectives: 62.2 us -> none  [local(): inner_sum = lax.psum(jnp.sum(stream_f * scaled_grad, -1), 'ep')]
    ppermute x0 -> x8, starting transfers between devices: none -> 51.3 us  [butterfly_sums(): other = lax.ppermute(total, axis, [(i, i ^ step) for i in range(count)])]
    all_gather x2 -> x0, blocking collectives: 48.7 us -> none  [the longest x1 24.4 us: local(): whole_rows = lax.all_gather(stream, 'ep', axis=1, tiled=True).astype(f32)]
    ppermute x0 -> x8, waiting for transfers between devices: none -> 48.1 us  [butterfly_sums(): other = lax.ppermute(total, axis, [(i, i ^ step) for i in range(count)])]
    all_to_all x1 -> x4, waiting for transfers between devices: 0.01 us -> 41.9 us  [the longest x2 41.9 us: gather_blocks(): return lax.all_to_all(spread, axis, 0, 0, tiled=True)]
    all_gather x1, waiting for transfers between devices: 41.4 us -> 0.01 us  [local(): w_cols = lax.all_gather(out_weight, 'ctx', axis=0, tiled=True)]
  transfers between devices with their start and end apart: 16 -> 23, of which waited for: 9 -> 10; matrix products, arithmetic and copies ran while one was open for 11% -> 8% of each run, Pallas kernels for 0% -> 0%
where the time goes in v1:
time: 469 us; the launch traced here: 467 us
  waiting for transfers between devices  187 us (40%)
  starting transfers between devices  133 us (28%)
  blocking collectives  72.6 us (15%)
  local copies, waits for them, and re-layouts  33.3 us (7%)
  matrix products  19.9 us (4%)
  between operations  15.4 us (3%)
  other arithmetic  5.61 us (1%)
    all_gather x1, waiting for transfers between devices, local(): portion = lax.all_gather(expert_in, 'ctx', axis=0, tiled=True)  65 us
    ppermute x8, starting transfers between devices, butterfly_sums(): other = lax.ppermute(total, axis, [(i, i ^ step) for i in range(count)])  51.3 us
    unnamed x1, blocking collectives  49 us
    ppermute x8, waiting for transfers between devices, butterfly_sums(): other = lax.ppermute(total, axis, [(i, i ^ step) for i in range(count)])  48.1 us
    all_to_all x2, waiting for transfers between devices, gather_blocks(): return lax.all_to_all(spread, axis, 0, 0, tiled=True)  41.9 us
    all_to_all x1, starting transfers between devices, local(): lax.all_to_all(grad_half, 'ep', split_axis=1, concat_axis=0, tiled=True)  27.2 us
    all_gather x1, waiting for transfers between devices, local(): lax.all_gather(grad_in, 'ctx', axis=0, tiled=True)  23 us
    unnamed x6, starting transfers between devices  21.8 us
  transfers between devices with their start and end apart: 23, of which 10 were waited for; matrix products, arithmetic and copies ran while one was open for 8% of the time, Pallas kernels for 0%

profile of v1, /device:TPU:1, one launch (start us, length us, event | category | flops | bytes accessed | tf_op | source)
XLA Modules:
  0.0 466.6 jit_solution(1889732144079362567)
XLA Ops:
  8.9 1.0 fusion.41
  9.9 4.4 collective-permute-start
  17.7 4.9 %collective-permute-start.1 = (f32[2,128,128]{2,1,0:T(8,128)S(1)}, f32[2,128,128]{2,1,0:T(8,128)S(1)}, u32[]{:S(2)}, u32[]{:S(2)}) collective-permute-start(f32[2,128,128]{2,1,0:T(8,128)S(1)} %add.115), channel_id=1, source_target_pairs={{0,64},{32,96},{64,0},{96,32},{128,192},{160,224},{192,128},{224,1... | collective-permute-start | bytes 393224 | tf_op jit(solution)/shard_map/ppermute | solution.py:14
  23.9 8.4 %all-to-all-start.3 = ((bf16[32,20,96]{2,1,0:T(8,128)(2,1)}), bf16[32,20,96]{2,1,0:T(8,128)(2,1)S(1)}, u32[]{:S(2)}, u32[]{:S(2)}) async-start(bf16[32,20,96]{2,1,0:T(8,128)(2,1)} %all_to_all.56), calls=%async_computation.3 | async-start | bytes 393216 | tf_op jit(solution)/shard_map/all_to_all | solution.py:133
  32.5 8.8 %collective-permute-start.2 = (f32[2,128,128]{2,1,0:T(8,128)S(1)}, f32[2,128,128]{2,1,0:T(8,128)S(1)}, u32[]{:S(2)}, u32[]{:S(2)}) collective-permute-start(f32[2,128,128]{2,1,0:T(8,128)S(1)} %add.117), channel_id=1, source_target_pairs={{0,128},{32,160},{64,192},{96,224},{128,0},{160,32},{192,64},{224,... | collective-permute-start | bytes 393224 | tf_op jit(solution)/shard_map/ppermute | solution.py:14
  41.6 14.2 %collective-permute-done.2 = f32[2,128,128]{2,1,0:T(8,128)S(1)} collective-permute-done((f32[2,128,128]{2,1,0:T(8,128)S(1)}, f32[2,128,128]{2,1,0:T(8,128)S(1)}, u32[]{:S(2)}, u32[]{:S(2)}) %collective-permute-start.2) | collective-permute-done | bytes 131104 | tf_op jit(solution)/shard_map/ppermute | solution.py:14
  55.8 11.3 %collective-permute-start.3 = (f32[2,128,128]{2,1,0:T(8,128)S(1)}, f32[2,128,128]{2,1,0:T(8,128)S(1)}, u32[]{:S(2)}, u32[]{:S(2)}) collective-permute-start(f32[2,128,128]{2,1,0:T(8,128)S(1)} %add.119), channel_id=1, source_target_pairs={{0,256},{32,288},{64,320},{96,352},{128,384},{160,416},{192,448},{... | collective-permute-start | bytes 393224 | tf_op jit(solution)/shard_map/ppermute | solution.py:14
  67.4 4.5 collective-permute-done.3
  73.1 1.6 broadcast_in_dim.28
  74.8 12.2 %all-to-all-start = ((bf16[32,128,256]{2,1,0:T(8,128)(2,1)}), bf16[32,128,256]{2,1,0:T(8,128)(2,1)}, u32[]{:S(2)}, u32[]{:S(2)}) async-start(bf16[32,128,256]{2,1,0:T(8,128)(2,1)} %broadcast_in_dim.28), calls=%async_computation | async-start | bytes 4194304 | tf_op jit(solution)/shard_map/all_to_all | solution.py:26
  88.2 27.5 %all-to-all-done = bf16[32,128,256]{2,1,0:T(8,128)(2,1)} async-done(((bf16[32,128,256]{2,1,0:T(8,128)(2,1)}), bf16[32,128,256]{2,1,0:T(8,128)(2,1)}, u32[]{:S(2)}, u32[]{:S(2)}) %all-to-all-start) | async-done | bytes 2097184 | tf_op jit(solution)/shard_map/all_to_all | solution.py:26
  115.8 2.9 fusion.24
  119.1 12.7 %all_to_all.76 = bf16[32,20,96]{2,1,0:T(8,128)(2,1)S(1)} all-to-all(bf16[32,20,96]{2,1,0:T(8,128)(2,1)S(1)} %reshape.127), channel_id=1, replica_groups=mesh['ctx'=16,'ep'=32] {'ep'}, dimensions={0} | all-to-all | bytes 245760 | tf_op jit(solution)/shard_map/all_to_all | solution.py:107
  132.7 1.9 reshape.133
  134.8 1.7 fusion.31
  136.5 1.3 copy.196
  137.9 3.8 all-to-all-start.2
  141.7 23.0 %all-gather.10.cloned.1.call-done = bf16[16,20,3072]{2,1,0:T(8,128)(2,1)} async-done(((bf16[1,20,3072]{2,1,0:T(8,128)(2,1)}), bf16[16,20,3072]{2,1,0:T(8,128)(2,1)}) %all-gather.10.cloned.1.call-update) | async-done | bytes 1966096 | tf_op jit(solution)/shard_map/all_gather | solution.py:134
  164.7 4.0 reshape.137
  168.6 3.2 fusion.3
  171.9 65.0 %all-gather.8.cloned.1.call-done = bf16[16,20,3072]{2,1,0:T(8,128)(2,1)} async-done(((bf16[1,20,3072]{2,1,0:T(8,128)(2,1)}), bf16[16,20,3072]{2,1,0:T(8,128)(2,1)}) %all-gather.8.cloned.1.call-update) | async-done | bytes 1966096 | tf_op jit(solution)/shard_map/all_gather | solution.py:118
  236.8 4.0 reshape.135
  240.8 3.4 fusion.11
  247.4 2.0 fusion.2
  249.4 49.0 %fusion.61 = (bf16[24,3072]{1,0:T(8,128)(2,1)}, bf16[24,3072]{1,0:T(8,128)(2,1)}) fusion(bf16[320,3072]{1,0:T(8,128)(2,1)S(1)} %convolution_convert_fusion, bf16[320,3072]{1,0:T(8,128)(2,1)} %fusion.2), kind=kCustom, calls=%all-reduce-scatter.2 | all-reduce-scatter fusion | flops 2359297 | bytes 4229120
  299.3 3.0 collective-permute-start.8
  302.3 4.3 collective-permute-start.9
  306.5 4.1 collective-permute-start.10
  310.6 2.2 collective-permute-start.11
  312.8 3.8 collective-permute-start.12
  317.6 4.5 collective-permute-start.13
  322.1 1.3 dynamic-slice.6
  324.0 2.5 concatenate
  326.5 2.5 concatenate.1
  330.6 27.2 %all-to-all-start.4 = ((bf16[20,32,96]{2,0,1:T(8,128)(2,1)}), bf16[20,32,96]{2,0,1:T(8,128)(2,1)S(1)}, u32[]{:S(2)}, u32[]{:S(2)}) async-start(bf16[20,32,96]{2,0,1:T(8,128)(2,1)} %copy.130), calls=%async_computation.4 | async-start | bytes 393216 | tf_op jit(solution)/shard_map/all_to_all | solution.py:148
  358.0 8.2 %all-to-all-done.4 = bf16[20,32,96]{2,0,1:T(8,128)(2,1)S(1)} async-done(((bf16[20,32,96]{2,0,1:T(8,128)(2,1)}), bf16[20,32,96]{2,0,1:T(8,128)(2,1)S(1)}, u32[]{:S(2)}, u32[]{:S(2)}) %all-to-all-start.4) | async-done | bytes 122912 | tf_op jit(solution)/shard_map/all_to_all | solution.py:148
  366.5 10.9 %all_to_all.77 = f32[32,128,2]{1,2,0:T(2,128)S(1)} all-to-all(f32[32,128,2]{1,2,0:T(2,128)S(1)} %broadcast_in_dim.29), channel_id=1, replica_groups=mesh['ctx'=16,'ep'=32] {'ep'}, dimensions={0} | all-to-all | bytes 65536 | tf_op jit(solution)/shard_map/all_to_all | solution.py:26
  377.5 1.0 broadcast_in_dim.30
  378.5 4.0 all-to-all-start.6
  382.5 14.3 %all-to-all-done.6 = bf16[32,128,96]{1,2,0:T(8,128)(2,1)S(1)} async-done(((bf16[32,128,96]{1,2,0:T(8,128)(2,1)}), bf16[32,128,96]{1,2,0:T(8,128)(2,1)S(1)}, u32[]{:S(2)}, u32[]{:S(2)}) %all-to-all-start.6) | async-done | bytes 786464 | tf_op jit(solution)/shard_map/all_to_all | solution.py:26
  398.4 1.9 collective-permute-start.4
  402.4 4.2 all-to-all-start.7
  406.6 5.0 %collective-permute-start.5 = (f32[2,128,128]{2,1,0:T(8,128)S(1)}, f32[2,128,128]{2,1,0:T(8,128)S(1)}, u32[]{:S(2)}, u32[]{:S(2)}) collective-permute-start(f32[2,128,128]{2,1,0:T(8,128)S(1)} %add.136), channel_id=1, source_target_pairs={{0,64},{32,96},{64,0},{96,32},{128,192},{160,224},{192,128},{224,1... | collective-permute-start | bytes 393224 | tf_op jit(solution)/shard_map/ppermute | solution.py:14
  411.8 6.2 %collective-permute-done.5 = f32[2,128,128]{2,1,0:T(8,128)S(1)} collective-permute-done((f32[2,128,128]{2,1,0:T(8,128)S(1)}, f32[2,128,128]{2,1,0:T(8,128)S(1)}, u32[]{:S(2)}, u32[]{:S(2)}) %collective-permute-start.5) | collective-permute-done | bytes 131104 | tf_op jit(solution)/shard_map/ppermute | solution.py:14
  417.9 6.7 %collective-permute-start.6 = (f32[2,128,128]{2,1,0:T(8,128)S(1)}, f32[2,128,128]{2,1,0:T(8,128)S(1)}, u32[]{:S(2)}, u32[]{:S(2)}) collective-permute-start(f32[2,128,128]{2,1,0:T(8,128)S(1)} %add.138), channel_id=1, source_target_pairs={{0,128},{32,160},{64,192},{96,224},{128,0},{160,32},{192,64},{224,... | collective-permute-start | bytes 393224 | tf_op jit(solution)/shard_map/ppermute | solution.py:14
  424.8 11.0 %collective-permute-done.6 = f32[2,128,128]{2,1,0:T(8,128)S(1)} collective-permute-done((f32[2,128,128]{2,1,0:T(8,128)S(1)}, f32[2,128,128]{2,1,0:T(8,128)S(1)}, u32[]{:S(2)}, u32[]{:S(2)}) %collective-permute-start.6) | collective-permute-done | bytes 131104 | tf_op jit(solution)/shard_map/ppermute | solution.py:14
  435.9 8.3 %collective-permute-start.7 = (f32[2,128,128]{2,1,0:T(8,128)S(1)}, f32[2,128,128]{2,1,0:T(8,128)S(1)}, u32[]{:S(2)}, u32[]{:S(2)}) collective-permute-start(f32[2,128,128]{2,1,0:T(8,128)S(1)} %add.140), channel_id=1, source_target_pairs={{0,256},{32,288},{64,320},{96,352},{128,384},{160,416},{192,448},{... | collective-permute-start | bytes 393224 | tf_op jit(solution)/shard_map/ppermute | solution.py:14
  445.1 12.2 %collective-permute-done.7 = f32[2,128,128]{2,1,0:T(8,128)S(1)} collective-permute-done((f32[2,128,128]{2,1,0:T(8,128)S(1)}, f32[2,128,128]{2,1,0:T(8,128)S(1)}, u32[]{:S(2)}, u32[]{:S(2)}) %collective-permute-start.7) | collective-permute-done | bytes 131104 | tf_op jit(solution)/shard_map/ppermute | solution.py:14
  (172 shorter events, 25.4 us)
Async XLA Ops:
  7.2 161.5 %copy-start = (bf16[1,192,3072]{2,1,0:T(8,128)(2,1)S(1)}, bf16[1,192,3072]{2,1,0:T(8,128)(2,1)}, u32[]{:S(2)}) copy-start(bf16[1,192,3072]{2,1,0:T(8,128)(2,1)} %param.28) | copy-start | bytes 3538948
  7.2 15.4 %copy-start.31 = (bf16[128,96]{0,1:T(8,128)(2,1)S(1)}, bf16[128,96]{0,1:T(8,128)(2,1)}, u32[]{:S(2)}) copy-start(bf16[128,96]{0,1:T(8,128)(2,1)} %param.29) | copy-start | bytes 73732
  7.2 108.6 %all-gather.6.cloned.1.call-start = ((), (), s32[]{:S(2)}) async-start(), calls=%async_computation.8 | async-start | bytes 1671168 | tf_op jit(solution)/shard_map/all_gather | solution.py:68
  8.9 7.8 %copy-start.18 = (bf16[128,256]{0,1:T(8,128)(2,1)}, bf16[128,256]{0,1:T(8,128)(2,1)S(1)}, u32[]{:S(2)}) copy-start(bf16[128,256]{0,1:T(8,128)(2,1)S(1)} %copy.193) | copy-start | bytes 196612
  9.9 7.8 %collective-permute-start = (f32[2,128,128]{2,1,0:T(8,128)S(1)}, f32[2,128,128]{2,1,0:T(8,128)S(1)}, u32[]{:S(2)}, u32[]{:S(2)}) collective-permute-start(f32[2,128,128]{2,1,0:T(8,128)S(1)} %fusion.41), channel_id=1, source_target_pairs={{0,32},{32,0},{64,96},{96,64},{128,160},{160,128},{192,224},{224,1... | collective-permute-start | bytes 393224 | tf_op jit(solution)/shard_map/ppermute | solution.py:14
  15.7 16.6 %copy-start.32 = (bf16[128,256]{1,0:T(8,128)(2,1)S(1)}, bf16[128,256]{1,0:T(8,128)(2,1)}, u32[]{:S(2)}) copy-start(bf16[128,256]{1,0:T(8,128)(2,1)} %param.15) | copy-start | bytes 196612
  16.7 24.7 %copy-start.25 = (bf16[128,256]{1,0:T(8,128)(2,1)S(1)}, bf16[128,256]{1,0:T(8,128)(2,1)}, u32[]{:S(2)}) copy-start(bf16[128,256]{1,0:T(8,128)(2,1)} %param.16) | copy-start | bytes 196612
  17.6 49.5 %copy-start.20 = (bf16[128,256]{1,0:T(8,128)(2,1)S(1)}, bf16[128,256]{1,0:T(8,128)(2,1)}, u32[]{:S(2)}) copy-start(bf16[128,256]{1,0:T(8,128)(2,1)} %param.17) | copy-start | bytes 196612
  17.6 54.3 %copy-start.29 = (f32[2,128,128]{2,1,0:T(8,128)S(1)}, f32[2,128,128]{2,1,0:T(8,128)}, u32[]{:S(2)}) copy-start(f32[2,128,128]{2,1,0:T(8,128)} %param.18) | copy-start | bytes 393220
  17.7 14.8 %collective-permute-start.1 = (f32[2,128,128]{2,1,0:T(8,128)S(1)}, f32[2,128,128]{2,1,0:T(8,128)S(1)}, u32[]{:S(2)}, u32[]{:S(2)}) collective-permute-start(f32[2,128,128]{2,1,0:T(8,128)S(1)} %add.115), channel_id=1, source_target_pairs={{0,64},{32,96},{64,0},{96,32},{128,192},{160,224},{192,128},{224,1... | collective-permute-start | bytes 393224 | tf_op jit(solution)/shard_map/ppermute | solution.py:14
  22.9 50.0 %copy-start.34 = (f32[256]{0:T(256)S(1)}, f32[256]{0:T(256)}, u32[]{:S(2)}) copy-start(f32[256]{0:T(256)} %param.19) | copy-start | bytes 3076
  23.9 49.3 %all-to-all-start.3 = ((bf16[32,20,96]{2,1,0:T(8,128)(2,1)}), bf16[32,20,96]{2,1,0:T(8,128)(2,1)S(1)}, u32[]{:S(2)}, u32[]{:S(2)}) async-start(bf16[32,20,96]{2,1,0:T(8,128)(2,1)} %all_to_all.56), calls=%async_computation.3 | async-start | bytes 393216 | tf_op jit(solution)/shard_map/all_to_all | solution.py:133
  32.4 42.4 %copy-start.14 = (bf16[128,256]{0,1:T(8,128)(2,1)}, bf16[128,256]{0,1:T(8,128)(2,1)S(1)}, u32[]{:S(2)}) copy-start(bf16[128,256]{0,1:T(8,128)(2,1)S(1)} %copy.159) | copy-start | bytes 196612
  32.5 23.3 %collective-permute-start.2 = (f32[2,128,128]{2,1,0:T(8,128)S(1)}, f32[2,128,128]{2,1,0:T(8,128)S(1)}, u32[]{:S(2)}, u32[]{:S(2)}) collective-permute-start(f32[2,128,128]{2,1,0:T(8,128)S(1)} %add.117), channel_id=1, source_target_pairs={{0,128},{32,160},{64,192},{96,224},{128,0},{160,32},{192,64},{224,... | collective-permute-start | bytes 393224 | tf_op jit(solution)/shard_map/ppermute | solution.py:14
  41.6 33.2 %copy-start.27 = (bf16[2,128,128]{2,1,0:T(8,128)(2,1)}, bf16[2,128,128]{2,1,0:T(8,128)(2,1)S(1)}, u32[]{:S(2)}) copy-start(bf16[2,128,128]{2,1,0:T(8,128)(2,1)S(1)} %fusion.16) | copy-start | bytes 196612
  55.8 16.1 %collective-permute-start.3 = (f32[2,128,128]{2,1,0:T(8,128)S(1)}, f32[2,128,128]{2,1,0:T(8,128)S(1)}, u32[]{:S(2)}, u32[]{:S(2)}) collective-permute-start(f32[2,128,128]{2,1,0:T(8,128)S(1)} %add.119), channel_id=1, source_target_pairs={{0,256},{32,288},{64,320},{96,352},{128,384},{160,416},{192,448},{... | collective-permute-start | bytes 393224 | tf_op jit(solution)/shard_map/ppermute | solution.py:14
  74.8 41.0 %all-to-all-start = ((bf16[32,128,256]{2,1,0:T(8,128)(2,1)}), bf16[32,128,256]{2,1,0:T(8,128)(2,1)}, u32[]{:S(2)}, u32[]{:S(2)}) async-start(bf16[32,128,256]{2,1,0:T(8,128)(2,1)} %broadcast_in_dim.28), calls=%async_computation | async-start | bytes 4194304 | tf_op jit(solution)/shard_map/all_to_all | solution.py:26
  87.0 28.7 %copy-start.40 = (bf16[128,96]{0,1:T(8,128)(2,1)S(1)}, bf16[128,96]{0,1:T(8,128)(2,1)}, u32[]{:S(2)}) copy-start(bf16[128,96]{0,1:T(8,128)(2,1)} %param.21) | copy-start | bytes 73732
  87.0 77.6 %all-gather.10.cloned.1.call-start = ((), (), s32[]{:S(2)}) async-start(), calls=%async_computation.10 | async-start | bytes 2506752 | tf_op jit(solution)/shard_map/all_gather | solution.py:134
  88.0 148.8 %all-gather.8.cloned.1.call-start = ((), (), s32[]{:S(2)}) async-start(), calls=%async_computation.9 | async-start | bytes 2506752 | tf_op jit(solution)/shard_map/all_gather | solution.py:118
  118.6 258.8 %copy-start.23 = (bf16[128,96]{0,1:T(8,128)(2,1)}, bf16[128,96]{0,1:T(8,128)(2,1)S(1)}, u32[]{:S(2)}) copy-start(bf16[128,96]{0,1:T(8,128)(2,1)S(1)} %fusion.24) | copy-start | bytes 73732
  118.7 16.1 %copy-start.33 = (f32[3072]{0:T(1024)S(1)}, f32[3072]{0:T(1024)}, u32[]{:S(2)}) copy-start(f32[3072]{0:T(1024)} %param.22) | copy-start | bytes 36868
  118.9 17.6 %copy-start.9 = (bf16[8192,96]{0,1:T(8,128)(2,1)S(1)}, bf16[8192,96]{0,1:T(8,128)(2,1)}, u32[]{:S(2)}) copy-start(bf16[8192,96]{0,1:T(8,128)(2,1)} %all-gather.6.cloned.1.call-done) | copy-start | bytes 4718596
  137.9 103.0 %all-to-all-start.2 = ((bf16[32,256,96]{1,2,0:T(8,128)(2,1)}), bf16[32,256,96]{1,2,0:T(8,128)(2,1)S(1)}, u32[]{:S(2)}, u32[]{:S(2)}) async-start(bf16[32,256,96]{1,2,0:T(8,128)(2,1)} %bitcast.161), calls=%async_computation.2 | async-start | bytes 3145728 | tf_op jit(solution)/shard_map/all_to_all | solution.py:117
  240.8 3.4 copy-start.13
  299.3 24.7 %collective-permute-start.8 = (bf16[24,3072]{1,0:T(8,128)(2,1)}, bf16[24,3072]{1,0:T(8,128)(2,1)S(1)}, u32[]{:S(2)}, u32[]{:S(2)}) collective-permute-start(bf16[24,3072]{1,0:T(8,128)(2,1)} %get-tuple-element.44), channel_id=1, source_target_pairs={{0,32},{32,64},{64,96},{96,128},{128,160},{160,192},{192,224},{224... | collective-permute-start | bytes 442376
  302.3 21.7 %collective-permute-start.9 = (bf16[24,3072]{1,0:T(8,128)(2,1)}, bf16[24,3072]{1,0:T(8,128)(2,1)S(1)}, u32[]{:S(2)}, u32[]{:S(2)}) collective-permute-start(bf16[24,3072]{1,0:T(8,128)(2,1)} %get-tuple-element.44), channel_id=1, source_target_pairs={{0,64},{32,96},{64,128},{96,160},{128,192},{160,224},{192,256},{22... | collective-permute-start | bytes 442376
  306.5 11.0 %collective-permute-start.10 = (bf16[12,3072]{1,0:T(8,128)(2,1)S(1)}, bf16[12,3072]{1,0:T(8,128)(2,1)S(1)}, u32[]{:S(2)}, u32[]{:S(2)}) collective-permute-start(bf16[12,3072]{1,0:T(8,128)(2,1)S(1)} %slice.8), channel_id=1, source_target_pairs={{0,96},{32,128},{64,160},{96,192},{128,224},{160,256},{192,288},{2... | collective-permute-start | bytes 221192
  310.6 15.8 %collective-permute-start.11 = (bf16[24,3072]{1,0:T(8,128)(2,1)}, bf16[24,3072]{1,0:T(8,128)(2,1)S(1)}, u32[]{:S(2)}, u32[]{:S(2)}) collective-permute-start(bf16[24,3072]{1,0:T(8,128)(2,1)} %get-tuple-element.45), channel_id=1, source_target_pairs={{0,32},{32,64},{64,96},{96,128},{128,160},{160,192},{192,224},{224... | collective-permute-start | bytes 442376
  312.8 13.7 %collective-permute-start.12 = (bf16[24,3072]{1,0:T(8,128)(2,1)}, bf16[24,3072]{1,0:T(8,128)(2,1)S(1)}, u32[]{:S(2)}, u32[]{:S(2)}) collective-permute-start(bf16[24,3072]{1,0:T(8,128)(2,1)} %get-tuple-element.45), channel_id=1, source_target_pairs={{0,64},{32,96},{64,128},{96,160},{128,192},{160,224},{192,256},{22... | collective-permute-start | bytes 442376
  317.6 8.9 %collective-permute-start.13 = (bf16[12,3072]{1,0:T(8,128)(2,1)S(1)}, bf16[12,3072]{1,0:T(8,128)(2,1)S(1)}, u32[]{:S(2)}, u32[]{:S(2)}) collective-permute-start(bf16[12,3072]{1,0:T(8,128)(2,1)S(1)} %slice.9), channel_id=1, source_target_pairs={{0,96},{32,128},{64,160},{96,192},{128,224},{160,256},{192,288},{2... | collective-permute-start | bytes 221192
  329.9 66.9 %copy-start.2 = (bf16[32,256,96]{1,2,0:T(8,128)(2,1)S(1)}, bf16[32,256,96]{1,2,0:T(8,128)(2,1)}, u32[]{:S(2)}) copy-start(bf16[32,256,96]{1,2,0:T(8,128)(2,1)} %copy-done.1) | copy-start | bytes 4718596
  330.6 35.5 %all-to-all-start.4 = ((bf16[20,32,96]{2,0,1:T(8,128)(2,1)}), bf16[20,32,96]{2,0,1:T(8,128)(2,1)S(1)}, u32[]{:S(2)}, u32[]{:S(2)}) async-start(bf16[20,32,96]{2,0,1:T(8,128)(2,1)} %copy.130), calls=%async_computation.4 | async-start | bytes 393216 | tf_op jit(solution)/shard_map/all_to_all | solution.py:148
  378.5 18.3 %all-to-all-start.6 = ((bf16[32,128,96]{1,2,0:T(8,128)(2,1)}), bf16[32,128,96]{1,2,0:T(8,128)(2,1)S(1)}, u32[]{:S(2)}, u32[]{:S(2)}) async-start(bf16[32,128,96]{1,2,0:T(8,128)(2,1)} %broadcast_in_dim.30), calls=%async_computation.6 | async-start | bytes 1572864 | tf_op jit(solution)/shard_map/all_to_all | solution.py:26
  396.8 3.5 copy-start.19
  396.9 3.6 copy-start.11
  397.6 3.9 copy-start.17
  397.6 14.0 %copy-start.28 = (bf16[2,128,128]{2,1,0:T(8,128)(2,1)S(1)}, bf16[2,128,128]{2,1,0:T(8,128)(2,1)}, u32[]{:S(2)}) copy-start(bf16[2,128,128]{2,1,0:T(8,128)(2,1)} %copy-done.27) | copy-start | bytes 196612
  397.7 27.0 %copy-start.16 = (bf16[128,256]{0,1:T(8,128)(2,1)S(1)}, bf16[128,256]{0,1:T(8,128)(2,1)}, u32[]{:S(2)}) copy-start(bf16[128,256]{0,1:T(8,128)(2,1)} %copy-done.14) | copy-start | bytes 196612
  398.0 46.2 %copy-start.4 = (f32[128,32,20]{0,1,2:T(8,128)S(1)}, f32[128,32,20]{0,1,2:T(8,128)}, u32[]{:S(2)}) copy-start(f32[128,32,20]{0,1,2:T(8,128)} %copy-done.3) | copy-start | bytes 983044
  398.0 46.2 %copy-start.24 = (bf16[128,96]{0,1:T(8,128)(2,1)S(1)}, bf16[128,96]{0,1:T(8,128)(2,1)}, u32[]{:S(2)}) copy-start(bf16[128,96]{0,1:T(8,128)(2,1)} %copy-done.23) | copy-start | bytes 73732
  398.4 8.2 %collective-permute-start.4 = (f32[2,128,128]{2,1,0:T(8,128)S(1)}, f32[2,128,128]{2,1,0:T(8,128)S(1)}, u32[]{:S(2)}, u32[]{:S(2)}) collective-permute-start(f32[2,128,128]{2,1,0:T(8,128)S(1)} %convolution_bitcast_fusion.4), channel_id=1, source_target_pairs={{0,32},{32,0},{64,96},{96,64},{128,160},{160,128},{192,224},{224,1... | collective-permute-start | bytes 393224 | tf_op jit(solution)/shard_map/ppermute | solution.py:14
  401.6 56.4 %copy-start.26 = (bf16[128,256]{1,0:T(8,128)(2,1)S(1)}, bf16[128,256]{1,0:T(8,128)(2,1)}, u32[]{:S(2)}) copy-start(bf16[128,256]{1,0:T(8,128)(2,1)} %param.16) | copy-start | bytes 196612
  402.4 56.7 %copy-start.22 = (bf16[128,256]{1,0:T(8,128)(2,1)S(1)}, bf16[128,256]{1,0:T(8,128)(2,1)}, u32[]{:S(2)}) copy-start(bf16[128,256]{1,0:T(8,128)(2,1)} %param.17) | copy-start | bytes 196612
  402.4 41.7 %all-to-all-start.7 = ((bf16[20,32,96]{2,0,1:T(8,128)(2,1)}), bf16[20,32,96]{2,0,1:T(8,128)(2,1)S(1)}, u32[]{:S(2)}, u32[]{:S(2)}) async-start(bf16[20,32,96]{2,0,1:T(8,128)(2,1)} %copy.135), calls=%async_computation.7 | async-start | bytes 393216 | tf_op jit(solution)/shard_map/all_to_all | solution.py:171
  406.6 11.3 %collective-permute-start.5 = (f32[2,128,128]{2,1,0:T(8,128)S(1)}, f32[2,128,128]{2,1,0:T(8,128)S(1)}, u32[]{:S(2)}, u32[]{:S(2)}) collective-permute-start(f32[2,128,128]{2,1,0:T(8,128)S(1)} %add.136), channel_id=1, source_target_pairs={{0,64},{32,96},{64,0},{96,32},{128,192},{160,224},{192,128},{224,1... | collective-permute-start | bytes 393224 | tf_op jit(solution)/shard_map/ppermute | solution.py:14
  417.9 17.9 %collective-permute-start.6 = (f32[2,128,128]{2,1,0:T(8,128)S(1)}, f32[2,128,128]{2,1,0:T(8,128)S(1)}, u32[]{:S(2)}, u32[]{:S(2)}) collective-permute-start(f32[2,128,128]{2,1,0:T(8,128)S(1)} %add.138), channel_id=1, source_target_pairs={{0,128},{32,160},{64,192},{96,224},{128,0},{160,32},{192,64},{224,... | collective-permute-start | bytes 393224 | tf_op jit(solution)/shard_map/ppermute | solution.py:14
  435.9 21.5 %collective-permute-start.7 = (f32[2,128,128]{2,1,0:T(8,128)S(1)}, f32[2,128,128]{2,1,0:T(8,128)S(1)}, u32[]{:S(2)}, u32[]{:S(2)}) collective-permute-start(f32[2,128,128]{2,1,0:T(8,128)S(1)} %add.140), channel_id=1, source_target_pairs={{0,256},{32,288},{64,320},{96,352},{128,384},{160,416},{192,448},{... | collective-permute-start | bytes 393224 | tf_op jit(solution)/shard_map/ppermute | solution.py:14
  (16 other events, 24.0 us)
Sparse Core Ops, SparseCore 0:
  10.1 84.9 all-gather.5
  97.1 67.5 all-gather.9
  166.7 70.0 all-gather.7

commit v2 on v1

--- a/solution.py
+++ b/solution.py
@@ -18,6 +18,21 @@
         total = total + other
         step *= 2
     return carried, total
+
+
+def gather_doubling(value, axis):
+    count = lax.axis_size(axis)
+    place = lax.axis_index(axis)
+    held = value
+    step = 1
+    while step < count:
+        other = lax.ppermute(held, axis, [(i, i ^ step) for i in range(count)])
+        upper = (place & step) != 0
+        low = jnp.where(upper, other, held)
+        high = jnp.where(upper, held, other)
+        held = jnp.concatenate([low, high], 0)
+        step *= 2
+    return held
 
 
 def gather_blocks(value, axis):
@@ -131,7 +146,7 @@
     grad_out = out_grad.astype(f32)
     grad_send = jnp.dot(dest_weights.T, grad_out, precision=high).astype(jnp.bfloat16)
     grad_in = lax.all_to_all(grad_send, "ep", split_axis=0, concat_axis=1, tiled=True)
-    grad_act = contract_last(lax.all_gather(grad_in, "ctx", axis=0, tiled=True), w_down)
+    grad_act = contract_last(gather_doubling(grad_in, "ctx"), w_down)
     grad_gate_pre = (grad_act * pre_up * gate_sig * (1.0 + pre_gate * (1.0 - gate_sig))).astype(
         jnp.bfloat16
     )

time: 469 us -> 532 us (1.13)
  waiting for transfers between devices: 187 us -> 247 us
  starting transfers between devices: 133 us -> 149 us
  local copies, waits for them, and re-layouts: 33.3 us -> 25.7 us
  blocking collectives: 72.6 us -> 66.2 us
    ppermute x0 -> x4, waiting for transfers between devices: none -> 147 us  [gather_doubling(): other = lax.ppermute(held, axis, [(i, i ^ step) for i in range(count)])]
    all_gather x1, waiting for transfers between devices: 65 us -> 0.02 us  [local(): portion = lax.all_gather(expert_in, 'ctx', axis=0, tiled=True)]
    all_gather x1 -> x0, waiting for transfers between devices: 23 us -> none  [local(): lax.all_gather(grad_in, 'ctx', axis=0, tiled=True)]
    all_to_all x1, starting transfers between devices: 27.2 us -> 10.8 us  [local(): lax.all_to_all(grad_half, 'ep', split_axis=1, concat_axis=0, tiled=True)]
    all_to_all x1 -> x0, blocking collectives: 12.7 us -> none  [local(): lax.all_to_all(picked.reshape(ep_count, capacity, columns), 'ep', 0, 0, t...]
    all_to_all x0 -> x1, starting transfers between devices: none -> 12.3 us  [local(): lax.all_to_all(picked.reshape(ep_count, capacity, columns), 'ep', 0, 0, t...]
    ppermute x0 -> x4, starting transfers between devices: none -> 9.63 us  [gather_doubling(): other = lax.ppermute(held, axis, [(i, i ^ step) for i in range(count)])]
    all_to_all x2, waiting for transfers between devices: 41.9 us -> 32.9 us  [gather_blocks(): return lax.all_to_all(spread, axis, 0, 0, tiled=True)]
  transfers between devices with their start and end apart: 23 -> 27, of which waited for: 10 -> 12; matrix products, arithmetic and copies ran while one was open for 8% -> 5% of each run, Pallas kernels for 0% -> 0%
where the time goes in v2:
time: 532 us; the launch traced here: 530 us
  waiting for transfers between devices  247 us (46%)
  starting transfers between devices  149 us (28%)
  blocking collectives  66.2 us (12%)
  local copies, waits for them, and re-layouts  25.7 us (5%)
  matrix products  17.6 us (3%)
  between operations  15.9 us (3%)
  other arithmetic  7.89 us (1%)
    ppermute x4, waiting for transfers between devices, gather_doubling(): other = lax.ppermute(held, axis, [(i, i ^ step) for i in range(count)])  147 us
    ppermute x8, starting transfers between devices, butterfly_sums(): other = lax.ppermute(total, axis, [(i, i ^ step) for i in range(count)])  57.8 us
    unnamed x1, blocking collectives  55.3 us
    ppermute x8, waiting for transfers between devices, butterfly_sums(): other = lax.ppermute(total, axis, [(i, i ^ step) for i in range(count)])  51.2 us
    all_to_all x2, waiting for transfers between devices, gather_blocks(): return lax.all_to_all(spread, axis, 0, 0, tiled=True)  32.9 us
    unnamed x6, starting transfers between devices  22.3 us
    all_to_all x2, starting transfers between devices, gather_blocks(): return lax.all_to_all(spread, axis, 0, 0, tiled=True)  14.2 us
    all_to_all x1, starting transfers between devices, local(): lax.all_to_all(picked.reshape(ep_count, capacity, columns), 'ep', 0, 0, t...  12.3 us
  transfers between devices with their start and end apart: 27, of which 12 were waited for; matrix products, arithmetic and copies ran while one was open for 5% of the time, Pallas kernels for 0%

profile of v2, /device:TPU:1, one launch (start us, length us, event | category | flops | bytes accessed | tf_op | source)
XLA Modules:
  0.0 530.0 jit_solution(11071503534962572944)
XLA Ops:
  9.3 4.4 collective-permute-start
  17.1 4.9 collective-permute-start.1
  23.2 8.4 %all-to-all-start.3 = ((bf16[32,20,96]{2,1,0:T(8,128)(2,1)}), bf16[32,20,96]{2,1,0:T(8,128)(2,1)S(1)}, u32[]{:S(2)}, u32[]{:S(2)}) async-start(bf16[32,20,96]{2,1,0:T(8,128)(2,1)} %all_to_all.56), calls=%async_computation.3 | async-start | bytes 393216 | tf_op jit(solution)/shard_map/all_to_all | solution.py:148
  32.6 8.8 %collective-permute-start.2 = (f32[2,128,128]{2,1,0:T(8,128)S(1)}, f32[2,128,128]{2,1,0:T(8,128)S(1)}, u32[]{:S(2)}, u32[]{:S(2)}) collective-permute-start(f32[2,128,128]{2,1,0:T(8,128)S(1)} %add.117), channel_id=1, source_target_pairs={{0,128},{32,160},{64,192},{96,224},{128,0},{160,32},{192,64},{224,... | collective-permute-start | bytes 393224 | tf_op jit(solution)/shard_map/ppermute | solution.py:14
  41.6 11.6 %collective-permute-done.2 = f32[2,128,128]{2,1,0:T(8,128)S(1)} collective-permute-done((f32[2,128,128]{2,1,0:T(8,128)S(1)}, f32[2,128,128]{2,1,0:T(8,128)S(1)}, u32[]{:S(2)}, u32[]{:S(2)}) %collective-permute-start.2) | collective-permute-done | bytes 131104 | tf_op jit(solution)/shard_map/ppermute | solution.py:14
  53.3 11.9 %collective-permute-start.3 = (f32[2,128,128]{2,1,0:T(8,128)S(1)}, f32[2,128,128]{2,1,0:T(8,128)S(1)}, u32[]{:S(2)}, u32[]{:S(2)}) collective-permute-start(f32[2,128,128]{2,1,0:T(8,128)S(1)} %add.119), channel_id=1, source_target_pairs={{0,256},{32,288},{64,320},{96,352},{128,384},{160,416},{192,448},{... | collective-permute-start | bytes 393224 | tf_op jit(solution)/shard_map/ppermute | solution.py:14
  65.5 10.1 %collective-permute-done.3 = f32[2,128,128]{2,1,0:T(8,128)S(1)} collective-permute-done((f32[2,128,128]{2,1,0:T(8,128)S(1)}, f32[2,128,128]{2,1,0:T(8,128)S(1)}, u32[]{:S(2)}, u32[]{:S(2)}) %collective-permute-start.3) | collective-permute-done | bytes 131104 | tf_op jit(solution)/shard_map/ppermute | solution.py:14
  76.8 1.6 broadcast_in_dim.28
  78.4 10.2 %all-to-all-start = ((bf16[32,128,256]{2,1,0:T(8,128)(2,1)}), bf16[32,128,256]{2,1,0:T(8,128)(2,1)}, u32[]{:S(2)}, u32[]{:S(2)}) async-start(bf16[32,128,256]{2,1,0:T(8,128)(2,1)} %broadcast_in_dim.28), calls=%async_computation | async-start | bytes 4194304 | tf_op jit(solution)/shard_map/all_to_all | solution.py:41
  88.9 1.9 collective-permute-start.4
  91.0 5.8 %collective-permute-done.4 = bf16[20,3072]{1,0:T(8,128)(2,1)S(1)} collective-permute-done((bf16[20,3072]{1,0:T(8,128)(2,1)S(1)}, bf16[20,3072]{1,0:T(8,128)(2,1)S(1)}, u32[]{:S(2)}, u32[]{:S(2)}) %collective-permute-start.4) | collective-permute-done | bytes 122912 | tf_op jit(solution)/shard_map/ppermute | solution.py:29
  96.9 1.9 collective-permute-start.5
  98.8 18.6 %all-to-all-done = bf16[32,128,256]{2,1,0:T(8,128)(2,1)} async-done(((bf16[32,128,256]{2,1,0:T(8,128)(2,1)}), bf16[32,128,256]{2,1,0:T(8,128)(2,1)}, u32[]{:S(2)}, u32[]{:S(2)}) %all-to-all-start) | async-done | bytes 2097184 | tf_op jit(solution)/shard_map/all_to_all | solution.py:41
  117.3 2.8 fusion.27
  121.9 12.3 %all-to-all-start.1 = ((bf16[32,20,96]{2,1,0:T(8,128)(2,1)}), bf16[32,20,96]{2,1,0:T(8,128)(2,1)S(1)}, u32[]{:S(2)}, u32[]{:S(2)}) async-start(bf16[32,20,96]{2,1,0:T(8,128)(2,1)} %reshape.127), calls=%async_computation.1 | async-start | bytes 393216 | tf_op jit(solution)/shard_map/all_to_all | solution.py:122
  134.4 8.1 %all-to-all-done.1 = bf16[32,20,96]{2,1,0:T(8,128)(2,1)S(1)} async-done(((bf16[32,20,96]{2,1,0:T(8,128)(2,1)}), bf16[32,20,96]{2,1,0:T(8,128)(2,1)S(1)}, u32[]{:S(2)}, u32[]{:S(2)}) %all-to-all-start.1) | async-done | bytes 122912 | tf_op jit(solution)/shard_map/all_to_all | solution.py:122
  143.8 3.9 collective-permute-start.6
  147.7 78.5 %collective-permute-done.6 = bf16[80,3072]{1,0:T(8,128)(2,1)S(1)} collective-permute-done((bf16[80,3072]{1,0:T(8,128)(2,1)S(1)}, bf16[80,3072]{1,0:T(8,128)(2,1)S(1)}, u32[]{:S(2)}, u32[]{:S(2)}) %collective-permute-start.6) | collective-permute-done | bytes 491552 | tf_op jit(solution)/shard_map/ppermute | solution.py:29
  228.2 1.9 collective-permute-start.7
  230.1 1.3 copy.196
  231.5 9.4 %all-to-all-start.2 = ((bf16[32,256,96]{1,2,0:T(8,128)(2,1)}), bf16[32,256,96]{1,2,0:T(8,128)(2,1)S(1)}, u32[]{:S(2)}, u32[]{:S(2)}) async-start(bf16[32,256,96]{1,2,0:T(8,128)(2,1)} %bitcast.160), calls=%async_computation.2 | async-start | bytes 3145728 | tf_op jit(solution)/shard_map/all_to_all | solution.py:132
  240.9 62.6 %collective-permute-done.7 = bf16[160,3072]{1,0:T(8,128)(2,1)} collective-permute-done((bf16[160,3072]{1,0:T(8,128)(2,1)}, bf16[160,3072]{1,0:T(8,128)(2,1)}, u32[]{:S(2)}, u32[]{:S(2)}) %collective-permute-start.7) | collective-permute-done | bytes 983072 | tf_op jit(solution)/shard_map/ppermute | solution.py:29
  303.5 1.8 broadcast_select_fusion.1
  306.3 3.9 reshape.135
  310.2 3.4 fusion.10
  316.7 2.0 fusion.2
  318.7 55.3 %fusion.65 = (bf16[24,3072]{1,0:T(8,128)(2,1)S(1)}, bf16[24,3072]{1,0:T(8,128)(2,1)S(1)}) fusion(bf16[320,3072]{1,0:T(8,128)(2,1)S(1)} %convolution_convert_fusion, bf16[320,3072]{1,0:T(8,128)(2,1)} %fusion.2), kind=kCustom, calls=%all-reduce-scatter.2 | all-reduce-scatter fusion | flops 2359297 | bytes 4229120
  374.1 1.8 collective-permute-start.12
  375.9 6.2 %collective-permute-start.13 = (bf16[24,3072]{1,0:T(8,128)(2,1)S(1)}, bf16[24,3072]{1,0:T(8,128)(2,1)S(1)}, u32[]{:S(2)}, u32[]{:S(2)}) collective-permute-start(bf16[24,3072]{1,0:T(8,128)(2,1)S(1)} %get-tuple-element.44), channel_id=1, source_target_pairs={{0,64},{32,96},{64,128},{96,160},{128,192},{160,224},{192,256},{22... | collective-permute-start | bytes 442376
  382.1 5.0 collective-permute-start.14
  387.2 1.9 collective-permute-start.15
  389.1 2.8 collective-permute-start.16
  392.0 4.6 collective-permute-start.17
  396.5 1.3 dynamic-slice.6
  400.2 1.9 concatenate.17
  403.8 10.8 %all-to-all-start.4 = ((bf16[20,32,96]{2,0,1:T(8,128)(2,1)}), bf16[20,32,96]{2,0,1:T(8,128)(2,1)S(1)}, u32[]{:S(2)}, u32[]{:S(2)}) async-start(bf16[20,32,96]{2,0,1:T(8,128)(2,1)} %copy.130), calls=%async_computation.4 | async-start | bytes 393216 | tf_op jit(solution)/shard_map/all_to_all | solution.py:163
  415.4 7.6 %all-to-all-done.4 = bf16[20,32,96]{2,0,1:T(8,128)(2,1)S(1)} async-done(((bf16[20,32,96]{2,0,1:T(8,128)(2,1)}), bf16[20,32,96]{2,0,1:T(8,128)(2,1)S(1)}, u32[]{:S(2)}, u32[]{:S(2)}) %all-to-all-start.4) | async-done | bytes 122912 | tf_op jit(solution)/shard_map/all_to_all | solution.py:163
  423.4 10.9 %all_to_all.76 = f32[32,128,2]{1,2,0:T(2,128)S(1)} all-to-all(f32[32,128,2]{1,2,0:T(2,128)S(1)} %broadcast_in_dim.29), channel_id=1, replica_groups=mesh['ctx'=16,'ep'=32] {'ep'}, dimensions={0} | all-to-all | bytes 65536 | tf_op jit(solution)/shard_map/all_to_all | solution.py:41
  435.3 4.0 all-to-all-start.6
  439.3 14.3 %all-to-all-done.6 = bf16[32,128,96]{1,2,0:T(8,128)(2,1)S(1)} async-done(((bf16[32,128,96]{1,2,0:T(8,128)(2,1)}), bf16[32,128,96]{1,2,0:T(8,128)(2,1)S(1)}, u32[]{:S(2)}, u32[]{:S(2)}) %all-to-all-start.6) | async-done | bytes 786464 | tf_op jit(solution)/shard_map/all_to_all | solution.py:41
  455.2 6.5 %collective-permute-start.8 = (f32[2,128,128]{2,1,0:T(8,128)S(1)}, f32[2,128,128]{2,1,0:T(8,128)S(1)}, u32[]{:S(2)}, u32[]{:S(2)}) collective-permute-start(f32[2,128,128]{2,1,0:T(8,128)S(1)} %convolution_bitcast_fusion.4), channel_id=1, source_target_pairs={{0,32},{32,0},{64,96},{96,64},{128,160},{160,128},{192,224},{224,1... | collective-permute-start | bytes 393224 | tf_op jit(solution)/shard_map/ppermute | solution.py:14
  463.8 4.4 all-to-all-start.7
  468.3 7.1 %collective-permute-start.9 = (f32[2,128,128]{2,1,0:T(8,128)S(1)}, f32[2,128,128]{2,1,0:T(8,128)S(1)}, u32[]{:S(2)}, u32[]{:S(2)}) collective-permute-start(f32[2,128,128]{2,1,0:T(8,128)S(1)} %add.136), channel_id=1, source_target_pairs={{0,64},{32,96},{64,0},{96,32},{128,192},{160,224},{192,128},{224,1... | collective-permute-start | bytes 393224 | tf_op jit(solution)/shard_map/ppermute | solution.py:14
  475.5 6.1 %collective-permute-done.9 = f32[2,128,128]{2,1,0:T(8,128)S(1)} collective-permute-done((f32[2,128,128]{2,1,0:T(8,128)S(1)}, f32[2,128,128]{2,1,0:T(8,128)S(1)}, u32[]{:S(2)}, u32[]{:S(2)}) %collective-permute-start.9) | collective-permute-done | bytes 131104 | tf_op jit(solution)/shard_map/ppermute | solution.py:14
  481.7 7.5 %collective-permute-start.10 = (f32[2,128,128]{2,1,0:T(8,128)S(1)}, f32[2,128,128]{2,1,0:T(8,128)S(1)}, u32[]{:S(2)}, u32[]{:S(2)}) collective-permute-start(f32[2,128,128]{2,1,0:T(8,128)S(1)} %add.138), channel_id=1, source_target_pairs={{0,128},{32,160},{64,192},{96,224},{128,0},{160,32},{192,64},{224,... | collective-permute-start | bytes 393224 | tf_op jit(solution)/shard_map/ppermute | solution.py:14
  489.3 11.2 %collective-permute-done.10 = f32[2,128,128]{2,1,0:T(8,128)S(1)} collective-permute-done((f32[2,128,128]{2,1,0:T(8,128)S(1)}, f32[2,128,128]{2,1,0:T(8,128)S(1)}, u32[]{:S(2)}, u32[]{:S(2)}) %collective-permute-start.10) | collective-permute-done | bytes 131104 | tf_op jit(solution)/shard_map/ppermute | solution.py:14
  500.5 6.7 %collective-permute-start.11 = (f32[2,128,128]{2,1,0:T(8,128)S(1)}, f32[2,128,128]{2,1,0:T(8,128)S(1)}, u32[]{:S(2)}, u32[]{:S(2)}) collective-permute-start(f32[2,128,128]{2,1,0:T(8,128)S(1)} %add.140), channel_id=1, source_target_pairs={{0,256},{32,288},{64,320},{96,352},{128,384},{160,416},{192,448},{... | collective-permute-start | bytes 393224 | tf_op jit(solution)/shard_map/ppermute | solution.py:14
  508.2 12.2 %collective-permute-done.11 = f32[2,128,128]{2,1,0:T(8,128)S(1)} collective-permute-done((f32[2,128,128]{2,1,0:T(8,128)S(1)}, f32[2,128,128]{2,1,0:T(8,128)S(1)}, u32[]{:S(2)}, u32[]{:S(2)}) %collective-permute-start.11) | collective-permute-done | bytes 131104 | tf_op jit(solution)/shard_map/ppermute | solution.py:14
  (194 shorter events, 31.9 us)
Async XLA Ops:
  7.2 298.2 %copy-start = (bf16[1,192,3072]{2,1,0:T(8,128)(2,1)S(1)}, bf16[1,192,3072]{2,1,0:T(8,128)(2,1)}, u32[]{:S(2)}) copy-start(bf16[1,192,3072]{2,1,0:T(8,128)(2,1)} %param.28) | copy-start | bytes 3538948
  9.3 7.8 %collective-permute-start = (f32[2,128,128]{2,1,0:T(8,128)S(1)}, f32[2,128,128]{2,1,0:T(8,128)S(1)}, u32[]{:S(2)}, u32[]{:S(2)}) collective-permute-start(f32[2,128,128]{2,1,0:T(8,128)S(1)} %fusion.44), channel_id=1, source_target_pairs={{0,32},{32,0},{64,96},{96,64},{128,160},{160,128},{192,224},{224,1... | collective-permute-start | bytes 393224 | tf_op jit(solution)/shard_map/ppermute | solution.py:14
  16.0 74.8 %copy-start.4 = (f32[128,32,20]{0,1,2:T(8,128)}, f32[128,32,20]{0,1,2:T(8,128)S(1)}, u32[]{:S(2)}) copy-start(f32[128,32,20]{0,1,2:T(8,128)S(1)} %get-tuple-element.40) | copy-start | bytes 983044
  16.8 24.7 %copy-start.28 = (bf16[128,256]{1,0:T(8,128)(2,1)S(1)}, bf16[128,256]{1,0:T(8,128)(2,1)}, u32[]{:S(2)}) copy-start(bf16[128,256]{1,0:T(8,128)(2,1)} %param.16) | copy-start | bytes 196612
  17.0 48.3 %copy-start.22 = (bf16[128,256]{1,0:T(8,128)(2,1)S(1)}, bf16[128,256]{1,0:T(8,128)(2,1)}, u32[]{:S(2)}) copy-start(bf16[128,256]{1,0:T(8,128)(2,1)} %param.17) | copy-start | bytes 196612
  17.0 58.6 %copy-start.32 = (f32[2,128,128]{2,1,0:T(8,128)S(1)}, f32[2,128,128]{2,1,0:T(8,128)}, u32[]{:S(2)}) copy-start(f32[2,128,128]{2,1,0:T(8,128)} %param.18) | copy-start | bytes 393220
  17.1 15.5 %collective-permute-start.1 = (f32[2,128,128]{2,1,0:T(8,128)S(1)}, f32[2,128,128]{2,1,0:T(8,128)S(1)}, u32[]{:S(2)}, u32[]{:S(2)}) collective-permute-start(f32[2,128,128]{2,1,0:T(8,128)S(1)} %add.115), channel_id=1, source_target_pairs={{0,64},{32,96},{64,0},{96,32},{128,192},{160,224},{192,128},{224,1... | collective-permute-start | bytes 393224 | tf_op jit(solution)/shard_map/ppermute | solution.py:14
  22.3 54.3 %copy-start.39 = (f32[256]{0:T(256)S(1)}, f32[256]{0:T(256)}, u32[]{:S(2)}) copy-start(f32[256]{0:T(256)} %param.19) | copy-start | bytes 3076
  23.2 53.6 %all-to-all-start.3 = ((bf16[32,20,96]{2,1,0:T(8,128)(2,1)}), bf16[32,20,96]{2,1,0:T(8,128)(2,1)S(1)}, u32[]{:S(2)}, u32[]{:S(2)}) async-start(bf16[32,20,96]{2,1,0:T(8,128)(2,1)} %all_to_all.56), calls=%async_computation.3 | async-start | bytes 393216 | tf_op jit(solution)/shard_map/all_to_all | solution.py:148
  31.6 85.7 %all-gather.4.cloned.1.call-start = ((), (), s32[]{:S(2)}) async-start(), calls=%async_computation.8 | async-start | bytes 1671168 | tf_op jit(solution)/shard_map/all_gather | solution.py:83
  32.5 45.9 %copy-start.16 = (bf16[128,256]{0,1:T(8,128)(2,1)}, bf16[128,256]{0,1:T(8,128)(2,1)S(1)}, u32[]{:S(2)}) copy-start(bf16[128,256]{0,1:T(8,128)(2,1)S(1)} %copy.159) | copy-start | bytes 196612
  32.6 20.7 %collective-permute-start.2 = (f32[2,128,128]{2,1,0:T(8,128)S(1)}, f32[2,128,128]{2,1,0:T(8,128)S(1)}, u32[]{:S(2)}, u32[]{:S(2)}) collective-permute-start(f32[2,128,128]{2,1,0:T(8,128)S(1)} %add.117), channel_id=1, source_target_pairs={{0,128},{32,160},{64,192},{96,224},{128,0},{160,32},{192,64},{224,... | collective-permute-start | bytes 393224 | tf_op jit(solution)/shard_map/ppermute | solution.py:14
  41.6 36.8 %copy-start.30 = (bf16[2,128,128]{2,1,0:T(8,128)(2,1)}, bf16[2,128,128]{2,1,0:T(8,128)(2,1)S(1)}, u32[]{:S(2)}) copy-start(bf16[2,128,128]{2,1,0:T(8,128)(2,1)S(1)} %fusion.19) | copy-start | bytes 196612
  53.3 22.2 %collective-permute-start.3 = (f32[2,128,128]{2,1,0:T(8,128)S(1)}, f32[2,128,128]{2,1,0:T(8,128)S(1)}, u32[]{:S(2)}, u32[]{:S(2)}) collective-permute-start(f32[2,128,128]{2,1,0:T(8,128)S(1)} %add.119), channel_id=1, source_target_pairs={{0,256},{32,288},{64,320},{96,352},{128,384},{160,416},{192,448},{... | collective-permute-start | bytes 393224 | tf_op jit(solution)/shard_map/ppermute | solution.py:14
  78.4 38.9 %all-to-all-start = ((bf16[32,128,256]{2,1,0:T(8,128)(2,1)}), bf16[32,128,256]{2,1,0:T(8,128)(2,1)}, u32[]{:S(2)}, u32[]{:S(2)}) async-start(bf16[32,128,256]{2,1,0:T(8,128)(2,1)} %broadcast_in_dim.28), calls=%async_computation | async-start | bytes 4194304 | tf_op jit(solution)/shard_map/all_to_all | solution.py:41
  88.6 28.7 %copy-start.45 = (bf16[128,96]{0,1:T(8,128)(2,1)S(1)}, bf16[128,96]{0,1:T(8,128)(2,1)}, u32[]{:S(2)}) copy-start(bf16[128,96]{0,1:T(8,128)(2,1)} %param.21) | copy-start | bytes 73732
  88.9 7.9 %collective-permute-start.4 = (bf16[20,3072]{1,0:T(8,128)(2,1)S(1)}, bf16[20,3072]{1,0:T(8,128)(2,1)S(1)}, u32[]{:S(2)}, u32[]{:S(2)}) collective-permute-start(bf16[20,3072]{1,0:T(8,128)(2,1)S(1)} %all_to_all.59), channel_id=1, source_target_pairs={{0,32},{32,0},{64,96},{96,64},{128,160},{160,128},{192,224},{224,1... | collective-permute-start | bytes 368648 | tf_op jit(solution)/shard_map/ppermute | solution.py:29
  96.9 37.4 %collective-permute-start.5 = (bf16[40,3072]{1,0:T(8,128)(2,1)S(1)}, bf16[40,3072]{1,0:T(8,128)(2,1)S(1)}, u32[]{:S(2)}, u32[]{:S(2)}) collective-permute-start(bf16[40,3072]{1,0:T(8,128)(2,1)S(1)} %pad_maximum_fusion.2), channel_id=1, source_target_pairs={{0,64},{32,96},{64,0},{96,32},{128,192},{160,224},{192,128},{224,1... | collective-permute-start | bytes 737288 | tf_op jit(solution)/shard_map/ppermute | solution.py:29
  121.2 21.8 %copy-start.38 = (f32[3072]{0:T(1024)S(1)}, f32[3072]{0:T(1024)}, u32[]{:S(2)}) copy-start(f32[3072]{0:T(1024)} %param.22) | copy-start | bytes 36868
  121.9 20.5 %all-to-all-start.1 = ((bf16[32,20,96]{2,1,0:T(8,128)(2,1)}), bf16[32,20,96]{2,1,0:T(8,128)(2,1)S(1)}, u32[]{:S(2)}, u32[]{:S(2)}) async-start(bf16[32,20,96]{2,1,0:T(8,128)(2,1)} %reshape.127), calls=%async_computation.1 | async-start | bytes 393216 | tf_op jit(solution)/shard_map/all_to_all | solution.py:122
  134.2 172.1 %all-gather.6.cloned.1.call-start = ((), (), s32[]{:S(2)}) async-start(), calls=%async_computation.9 | async-start | bytes 2506752 | tf_op jit(solution)/shard_map/all_gather | solution.py:133
  143.8 86.4 %copy-start.11 = (bf16[8192,96]{0,1:T(8,128)(2,1)S(1)}, bf16[8192,96]{0,1:T(8,128)(2,1)}, u32[]{:S(2)}) copy-start(bf16[8192,96]{0,1:T(8,128)(2,1)} %all-gather.4.cloned.1.call-done) | copy-start | bytes 4718596
  143.8 82.4 %collective-permute-start.6 = (bf16[80,3072]{1,0:T(8,128)(2,1)S(1)}, bf16[80,3072]{1,0:T(8,128)(2,1)S(1)}, u32[]{:S(2)}, u32[]{:S(2)}) collective-permute-start(bf16[80,3072]{1,0:T(8,128)(2,1)S(1)} %pad_maximum_fusion.1), channel_id=1, source_target_pairs={{0,128},{32,160},{64,192},{96,224},{128,0},{160,32},{192,64},{224,... | collective-permute-start | bytes 1474568 | tf_op jit(solution)/shard_map/ppermute | solution.py:29
  228.2 75.3 %collective-permute-start.7 = (bf16[160,3072]{1,0:T(8,128)(2,1)}, bf16[160,3072]{1,0:T(8,128)(2,1)}, u32[]{:S(2)}, u32[]{:S(2)}) collective-permute-start(bf16[160,3072]{1,0:T(8,128)(2,1)} %pad_maximum_fusion), channel_id=1, source_target_pairs={{0,256},{32,288},{64,320},{96,352},{128,384},{160,416},{192,448},{... | collective-permute-start | bytes 2949128 | tf_op jit(solution)/shard_map/ppermute | solution.py:29
  231.5 78.7 %all-to-all-start.2 = ((bf16[32,256,96]{1,2,0:T(8,128)(2,1)}), bf16[32,256,96]{1,2,0:T(8,128)(2,1)S(1)}, u32[]{:S(2)}, u32[]{:S(2)}) async-start(bf16[32,256,96]{1,2,0:T(8,128)(2,1)} %bitcast.160), calls=%async_computation.2 | async-start | bytes 3145728 | tf_op jit(solution)/shard_map/all_to_all | solution.py:132
  374.1 24.4 %collective-permute-start.12 = (bf16[24,3072]{1,0:T(8,128)(2,1)S(1)}, bf16[24,3072]{1,0:T(8,128)(2,1)S(1)}, u32[]{:S(2)}, u32[]{:S(2)}) collective-permute-start(bf16[24,3072]{1,0:T(8,128)(2,1)S(1)} %get-tuple-element.44), channel_id=1, source_target_pairs={{0,32},{32,64},{64,96},{96,128},{128,160},{160,192},{192,224},{224... | collective-permute-start | bytes 442376
  375.9 22.6 %collective-permute-start.13 = (bf16[24,3072]{1,0:T(8,128)(2,1)S(1)}, bf16[24,3072]{1,0:T(8,128)(2,1)S(1)}, u32[]{:S(2)}, u32[]{:S(2)}) collective-permute-start(bf16[24,3072]{1,0:T(8,128)(2,1)S(1)} %get-tuple-element.44), channel_id=1, source_target_pairs={{0,64},{32,96},{64,128},{96,160},{128,192},{160,224},{192,256},{22... | collective-permute-start | bytes 442376
  382.1 9.8 %collective-permute-start.14 = (bf16[12,3072]{1,0:T(8,128)(2,1)S(1)}, bf16[12,3072]{1,0:T(8,128)(2,1)S(1)}, u32[]{:S(2)}, u32[]{:S(2)}) collective-permute-start(bf16[12,3072]{1,0:T(8,128)(2,1)S(1)} %slice.8), channel_id=1, source_target_pairs={{0,96},{32,128},{64,160},{96,192},{128,224},{160,256},{192,288},{2... | collective-permute-start | bytes 221192
  387.2 12.4 %collective-permute-start.15 = (bf16[24,3072]{1,0:T(8,128)(2,1)S(1)}, bf16[24,3072]{1,0:T(8,128)(2,1)S(1)}, u32[]{:S(2)}, u32[]{:S(2)}) collective-permute-start(bf16[24,3072]{1,0:T(8,128)(2,1)S(1)} %get-tuple-element.45), channel_id=1, source_target_pairs={{0,32},{32,64},{64,96},{96,128},{128,160},{160,192},{192,224},{224... | collective-permute-start | bytes 442376
  389.1 11.1 %collective-permute-start.16 = (bf16[24,3072]{1,0:T(8,128)(2,1)S(1)}, bf16[24,3072]{1,0:T(8,128)(2,1)S(1)}, u32[]{:S(2)}, u32[]{:S(2)}) collective-permute-start(bf16[24,3072]{1,0:T(8,128)(2,1)S(1)} %get-tuple-element.45), channel_id=1, source_target_pairs={{0,64},{32,96},{64,128},{96,160},{128,192},{160,224},{192,256},{22... | collective-permute-start | bytes 442376
  391.9 31.0 %copy-start.5 = (f32[128,32,20]{0,1,2:T(8,128)S(1)}, f32[128,32,20]{0,1,2:T(8,128)}, u32[]{:S(2)}) copy-start(f32[128,32,20]{0,1,2:T(8,128)} %copy-done.4) | copy-start | bytes 983044
  392.0 31.0 %copy-start.26 = (bf16[128,96]{0,1:T(8,128)(2,1)S(1)}, bf16[128,96]{0,1:T(8,128)(2,1)}, u32[]{:S(2)}) copy-start(bf16[128,96]{0,1:T(8,128)(2,1)} %copy-done.25) | copy-start | bytes 73732
  392.0 7.6 %collective-permute-start.17 = (bf16[12,3072]{1,0:T(8,128)(2,1)S(1)}, bf16[12,3072]{1,0:T(8,128)(2,1)S(1)}, u32[]{:S(2)}, u32[]{:S(2)}) collective-permute-start(bf16[12,3072]{1,0:T(8,128)(2,1)S(1)} %slice.9), channel_id=1, source_target_pairs={{0,96},{32,128},{64,160},{96,192},{128,224},{160,256},{192,288},{2... | collective-permute-start | bytes 221192
  399.5 34.8 %copy-start.36 = (bf16[128,96]{0,1:T(8,128)(2,1)S(1)}, bf16[128,96]{0,1:T(8,128)(2,1)}, u32[]{:S(2)}) copy-start(bf16[128,96]{0,1:T(8,128)(2,1)} %param.29) | copy-start | bytes 73732
  403.0 50.6 %copy-start.2 = (bf16[32,256,96]{1,2,0:T(8,128)(2,1)S(1)}, bf16[32,256,96]{1,2,0:T(8,128)(2,1)}, u32[]{:S(2)}) copy-start(bf16[32,256,96]{1,2,0:T(8,128)(2,1)} %copy-done.1) | copy-start | bytes 4718596
  403.8 19.2 %all-to-all-start.4 = ((bf16[20,32,96]{2,0,1:T(8,128)(2,1)}), bf16[20,32,96]{2,0,1:T(8,128)(2,1)S(1)}, u32[]{:S(2)}, u32[]{:S(2)}) async-start(bf16[20,32,96]{2,0,1:T(8,128)(2,1)} %copy.130), calls=%async_computation.4 | async-start | bytes 393216 | tf_op jit(solution)/shard_map/all_to_all | solution.py:163
  435.3 18.3 %all-to-all-start.6 = ((bf16[32,128,96]{1,2,0:T(8,128)(2,1)}), bf16[32,128,96]{1,2,0:T(8,128)(2,1)S(1)}, u32[]{:S(2)}, u32[]{:S(2)}) async-start(bf16[32,128,96]{1,2,0:T(8,128)(2,1)} %broadcast_in_dim.30), calls=%async_computation.6 | async-start | bytes 1572864 | tf_op jit(solution)/shard_map/all_to_all | solution.py:41
  454.5 20.9 %copy-start.31 = (bf16[2,128,128]{2,1,0:T(8,128)(2,1)S(1)}, bf16[2,128,128]{2,1,0:T(8,128)(2,1)}, u32[]{:S(2)}) copy-start(bf16[2,128,128]{2,1,0:T(8,128)(2,1)} %copy-done.30) | copy-start | bytes 196612
  454.6 34.6 %copy-start.18 = (bf16[128,256]{0,1:T(8,128)(2,1)S(1)}, bf16[128,256]{0,1:T(8,128)(2,1)}, u32[]{:S(2)}) copy-start(bf16[128,256]{0,1:T(8,128)(2,1)} %copy-done.16) | copy-start | bytes 196612
  454.8 52.4 %copy-start.7 = (f32[128,32,20]{0,1,2:T(8,128)S(1)}, f32[128,32,20]{0,1,2:T(8,128)}, u32[]{:S(2)}) copy-start(f32[128,32,20]{0,1,2:T(8,128)} %copy-done.6) | copy-start | bytes 983044
  454.8 52.4 %copy-start.27 = (bf16[128,96]{0,1:T(8,128)(2,1)S(1)}, bf16[128,96]{0,1:T(8,128)(2,1)}, u32[]{:S(2)}) copy-start(bf16[128,96]{0,1:T(8,128)(2,1)} %copy-done.25) | copy-start | bytes 73732
  455.2 13.0 %collective-permute-start.8 = (f32[2,128,128]{2,1,0:T(8,128)S(1)}, f32[2,128,128]{2,1,0:T(8,128)S(1)}, u32[]{:S(2)}, u32[]{:S(2)}) collective-permute-start(f32[2,128,128]{2,1,0:T(8,128)S(1)} %convolution_bitcast_fusion.4), channel_id=1, source_target_pairs={{0,32},{32,0},{64,96},{96,64},{128,160},{160,128},{192,224},{224,1... | collective-permute-start | bytes 393224 | tf_op jit(solution)/shard_map/ppermute | solution.py:14
  463.0 58.1 %copy-start.29 = (bf16[128,256]{1,0:T(8,128)(2,1)S(1)}, bf16[128,256]{1,0:T(8,128)(2,1)}, u32[]{:S(2)}) copy-start(bf16[128,256]{1,0:T(8,128)(2,1)} %param.16) | copy-start | bytes 196612
  463.8 58.4 %copy-start.24 = (bf16[128,256]{1,0:T(8,128)(2,1)S(1)}, bf16[128,256]{1,0:T(8,128)(2,1)}, u32[]{:S(2)}) copy-start(bf16[128,256]{1,0:T(8,128)(2,1)} %param.17) | copy-start | bytes 196612
  463.8 43.5 %all-to-all-start.7 = ((bf16[20,32,96]{2,0,1:T(8,128)(2,1)}), bf16[20,32,96]{2,0,1:T(8,128)(2,1)S(1)}, u32[]{:S(2)}, u32[]{:S(2)}) async-start(bf16[20,32,96]{2,0,1:T(8,128)(2,1)} %copy.135), calls=%async_computation.7 | async-start | bytes 393216 | tf_op jit(solution)/shard_map/all_to_all | solution.py:186
  468.3 13.3 %collective-permute-start.9 = (f32[2,128,128]{2,1,0:T(8,128)S(1)}, f32[2,128,128]{2,1,0:T(8,128)S(1)}, u32[]{:S(2)}, u32[]{:S(2)}) collective-permute-start(f32[2,128,128]{2,1,0:T(8,128)S(1)} %add.136), channel_id=1, source_target_pairs={{0,64},{32,96},{64,0},{96,32},{128,192},{160,224},{192,128},{224,1... | collective-permute-start | bytes 393224 | tf_op jit(solution)/shard_map/ppermute | solution.py:14
  481.7 18.9 %collective-permute-start.10 = (f32[2,128,128]{2,1,0:T(8,128)S(1)}, f32[2,128,128]{2,1,0:T(8,128)S(1)}, u32[]{:S(2)}, u32[]{:S(2)}) collective-permute-start(f32[2,128,128]{2,1,0:T(8,128)S(1)} %add.138), channel_id=1, source_target_pairs={{0,128},{32,160},{64,192},{96,224},{128,0},{160,32},{192,64},{224,... | collective-permute-start | bytes 393224 | tf_op jit(solution)/shard_map/ppermute | solution.py:14
  500.5 19.9 %collective-permute-start.11 = (f32[2,128,128]{2,1,0:T(8,128)S(1)}, f32[2,128,128]{2,1,0:T(8,128)S(1)}, u32[]{:S(2)}, u32[]{:S(2)}) collective-permute-start(f32[2,128,128]{2,1,0:T(8,128)S(1)} %add.140), channel_id=1, source_target_pairs={{0,256},{32,288},{64,320},{96,352},{128,384},{160,416},{192,448},{... | collective-permute-start | bytes 393224 | tf_op jit(solution)/shard_map/ppermute | solution.py:14
  (25 other events, 89.5 us)
Sparse Core Ops, SparseCore 0:
  34.5 80.3 all-gather.3
  143.8 133.9 all-gather.5

commit v3 on v1

--- a/solution.py
+++ b/solution.py
@@ -65,6 +65,21 @@
     model_width = model_gain.shape[0]
     columns = stream_in.shape[1]
     capacity = 5 * tokens_here // (2 * expert_count)
+    dest_expert = jnp.arange(ep_count) % expert_count
+    slot_iota = jnp.arange(capacity)
+    hits = (expert_ids[:, :, None, None] == dest_expert[None, None, :, None]) & (
+        expert_slots[:, :, None, None] == slot_iota[None, None, None, :]
+    )
+    hits_f = hits.astype(f32)
+    dest_picks = jnp.sum(hits_f, 1).reshape(tokens_here, ep_count * capacity)
+    dest_weights = jnp.sum(hits_f * route_gates[:, :, None, None], 1).reshape(
+        tokens_here, ep_count * capacity
+    )
+    grad_out = out_grad.astype(f32)
+    grad_send = jnp.dot(dest_weights.T, grad_out, precision=high).astype(jnp.bfloat16)
+    ctx_count = lax.axis_size("ctx")
+    grad_all = lax.all_gather(grad_send, "ctx", axis=0)
+    out_weight, grad_all = lax.optimization_barrier((out_weight, grad_all))
     w_cols = lax.all_gather(out_weight, "ctx", axis=0, tiled=True)
     query3 = query_act.reshape(tokens_here, head_count, head_size)
     key3 = key_act.reshape(tokens_here, head_count, head_size)
@@ -91,16 +106,6 @@
     stream = (stream_in.astype(f32) + attn_proj).astype(jnp.bfloat16)
     stream_f = stream.astype(f32)
     gain_cols = lax.dynamic_slice_in_dim(model_gain, my_ep * columns, columns, 0)
-    dest_expert = jnp.arange(ep_count) % expert_count
-    slot_iota = jnp.arange(capacity)
-    hits = (expert_ids[:, :, None, None] == dest_expert[None, None, :, None]) & (
-        expert_slots[:, :, None, None] == slot_iota[None, None, None, :]
-    )
-    hits_f = hits.astype(f32)
-    dest_picks = jnp.sum(hits_f, 1).reshape(tokens_here, ep_count * capacity)
-    dest_weights = jnp.sum(hits_f * route_gates[:, :, None, None], 1).reshape(
-        tokens_here, ep_count * capacity
-    )
     picked = jnp.dot(
         dest_picks.T.astype(jnp.bfloat16), stream, preferred_element_type=f32
     ).astype(jnp.bfloat16)
@@ -128,10 +133,10 @@
         scatter_dimension=0,
         tiled=True,
     )
-    grad_out = out_grad.astype(f32)
-    grad_send = jnp.dot(dest_weights.T, grad_out, precision=high).astype(jnp.bfloat16)
-    grad_in = lax.all_to_all(grad_send, "ep", split_axis=0, concat_axis=1, tiled=True)
-    grad_act = contract_last(lax.all_gather(grad_in, "ctx", axis=0, tiled=True), w_down)
+    grad_all = grad_all.reshape(ctx_count, ep_count, capacity, columns).transpose(1, 0, 2, 3)
+    grad_in = lax.all_to_all(grad_all, "ep", 0, 0, tiled=True)
+    grad_in = grad_in.transpose(1, 2, 0, 3).reshape(ctx_count * capacity, model_width)
+    grad_act = contract_last(grad_in, w_down)
     grad_gate_pre = (grad_act * pre_up * gate_sig * (1.0 + pre_gate * (1.0 - gate_sig))).astype(
         jnp.bfloat16
     )

time: 469 us -> 500 us (1.066)
  blocking collectives: 72.6 us -> 90.6 us
  local copies, waits for them, and re-layouts: 33.3 us -> 50.1 us
  waiting for transfers between devices: 187 us -> 181 us
    all_gather x1, waiting for transfers between devices: 65 us -> 0.01 us  [local(): portion = lax.all_gather(expert_in, 'ctx', axis=0, tiled=True)]
    all_to_all x1, waiting for transfers between devices: 0.01 us -> 32.6 us  [local(): grad_in = lax.all_to_all(grad_all, 'ep', 0, 0, tiled=True)]
    all_to_all x1, starting transfers between devices: 27.2 us -> 9.42 us  [local(): lax.all_to_all(grad_half, 'ep', split_axis=1, concat_axis=0, tiled=True)]
    all_gather x1, waiting for transfers between devices: 0.01 us -> 15.9 us  [local(): w_cols = lax.all_gather(out_weight, 'ctx', axis=0, tiled=True)]
    ppermute x8, starting transfers between devices: 51.3 us -> 65.1 us  [butterfly_sums(): other = lax.ppermute(total, axis, [(i, i ^ step) for i in range(count)])]
    all_to_all x1, blocking collectives: 12.7 us -> 24.6 us  [local(): lax.all_to_all(picked.reshape(ep_count, capacity, columns), 'ep', 0, 0, t...]
    all_gather x1, waiting for transfers between devices: 23 us -> 31.4 us  [local(): grad_all = lax.all_gather(grad_send, 'ctx', axis=0)]
    unnamed x1, blocking collectives: 49 us -> 55.1 us
  transfers between devices with their start and end apart: 23 -> 23, of which waited for: 10 -> 13; matrix products, arithmetic and copies ran while one was open for 8% -> 9% of each run, Pallas kernels for 0% -> 0%
where the time goes in v3:
time: 500 us; the launch traced here: 497 us
  waiting for transfers between devices  181 us (36%)
  starting transfers between devices  129 us (26%)
  blocking collectives  90.6 us (18%)
  local copies, waits for them, and re-layouts  50.1 us (10%)
  matrix products  21.9 us (4%)
  between operations  15.4 us (3%)
  other arithmetic  9.52 us (2%)
    ppermute x8, starting transfers between devices, butterfly_sums(): other = lax.ppermute(total, axis, [(i, i ^ step) for i in range(count)])  65.1 us
    unnamed x1, blocking collectives  55.1 us
    ppermute x8, waiting for transfers between devices, butterfly_sums(): other = lax.ppermute(total, axis, [(i, i ^ step) for i in range(count)])  48.4 us
    all_to_all x2, waiting for transfers between devices, gather_blocks(): return lax.all_to_all(spread, axis, 0, 0, tiled=True)  40.6 us
    all_to_all x1, waiting for transfers between devices, local(): grad_in = lax.all_to_all(grad_all, 'ep', 0, 0, tiled=True)  32.6 us
    all_gather x1, waiting for transfers between devices, local(): grad_all = lax.all_gather(grad_send, 'ctx', axis=0)  31.4 us
    all_to_all x1, blocking collectives, local(): lax.all_to_all(picked.reshape(ep_count, capacity, columns), 'ep', 0, 0, t...  24.6 us
    unnamed x6, starting transfers between devices  20.4 us
  transfers between devices with their start and end apart: 23, of which 13 were waited for; matrix products, arithmetic and copies ran while one was open for 9% of the time, Pallas kernels for 0%

profile of v3, /device:TPU:1, one launch (start us, length us, event | category | flops | bytes accessed | tf_op | source)
XLA Modules:
  0.0 497.5 jit_solution(15426238611408014242)
XLA Ops:
  12.1 4.4 collective-permute-start
  16.4 2.3 collective-permute-done
  18.8 5.6 %collective-permute-start.1 = (f32[2,128,128]{2,1,0:T(8,128)S(1)}, f32[2,128,128]{2,1,0:T(8,128)S(1)}, u32[]{:S(2)}, u32[]{:S(2)}) collective-permute-start(f32[2,128,128]{2,1,0:T(8,128)S(1)} %add.115), channel_id=1, source_target_pairs={{0,64},{32,96},{64,0},{96,32},{128,192},{160,224},{192,128},{224,1... | collective-permute-start | bytes 393224 | tf_op jit(solution)/shard_map/ppermute | solution.py:14
  24.6 3.6 collective-permute-done.1
  28.2 10.8 %collective-permute-start.2 = (f32[2,128,128]{2,1,0:T(8,128)S(1)}, f32[2,128,128]{2,1,0:T(8,128)S(1)}, u32[]{:S(2)}, u32[]{:S(2)}) collective-permute-start(f32[2,128,128]{2,1,0:T(8,128)S(1)} %add.117), channel_id=1, source_target_pairs={{0,128},{32,160},{64,192},{96,224},{128,0},{160,32},{192,64},{224,... | collective-permute-start | bytes 393224 | tf_op jit(solution)/shard_map/ppermute | solution.py:14
  39.3 13.4 %collective-permute-done.2 = f32[2,128,128]{2,1,0:T(8,128)S(1)} collective-permute-done((f32[2,128,128]{2,1,0:T(8,128)S(1)}, f32[2,128,128]{2,1,0:T(8,128)S(1)}, u32[]{:S(2)}, u32[]{:S(2)}) %collective-permute-start.2) | collective-permute-done | bytes 131104 | tf_op jit(solution)/shard_map/ppermute | solution.py:14
  53.4 13.0 %collective-permute-start.3 = (f32[2,128,128]{2,1,0:T(8,128)}, f32[2,128,128]{2,1,0:T(8,128)}, u32[]{:S(2)}, u32[]{:S(2)}) collective-permute-start(f32[2,128,128]{2,1,0:T(8,128)} %add.119), channel_id=1, source_target_pairs={{0,256},{32,288},{64,320},{96,352},{128,384},{160,416},{192,448},{... | collective-permute-start | bytes 393224 | tf_op jit(solution)/shard_map/ppermute | solution.py:14
  67.2 31.4 %all-gather.8.cloned.1.call-done = bf16[10240,96]{0,1:T(8,128)(2,1)} async-done(((bf16[640,96]{0,1:T(8,128)(2,1)}), bf16[10240,96]{0,1:T(8,128)(2,1)}) %all-gather.8.cloned.1.call-update) | async-done | bytes 1966096 | tf_op jit(solution)/shard_map/all_gather | solution.py:81
  98.6 1.9 copy.163
  107.4 14.3 %all-to-all-start = ((bf16[32,128,256]{2,1,0:T(8,128)(2,1)}), bf16[32,128,256]{2,1,0:T(8,128)(2,1)}, u32[]{:S(2)}, u32[]{:S(2)}) async-start(bf16[32,128,256]{2,1,0:T(8,128)(2,1)} %broadcast_in_dim.28), calls=%async_computation | async-start | bytes 4194304 | tf_op jit(solution)/shard_map/all_to_all | solution.py:26
  124.2 26.3 %all-to-all-done = bf16[32,128,256]{2,1,0:T(8,128)(2,1)} async-done(((bf16[32,128,256]{2,1,0:T(8,128)(2,1)}), bf16[32,128,256]{2,1,0:T(8,128)(2,1)}, u32[]{:S(2)}, u32[]{:S(2)}) %all-to-all-start) | async-done | bytes 2097184 | tf_op jit(solution)/shard_map/all_to_all | solution.py:26
  150.5 15.9 %all-gather.6.cloned.1.call-done = bf16[8192,96]{0,1:T(8,128)(2,1)} async-done(((bf16[512,96]{0,1:T(8,128)(2,1)}), bf16[8192,96]{0,1:T(8,128)(2,1)}) %all-gather.6.cloned.1.call-update) | async-done | bytes 1572880 | tf_op jit(solution)/shard_map/all_gather | solution.py:83
  166.3 2.9 fusion.24
  173.4 24.6 %all_to_all.62 = bf16[32,20,96]{2,1,0:T(8,128)(2,1)S(1)} all-to-all(bf16[32,20,96]{2,1,0:T(8,128)(2,1)} %reshape.131), channel_id=1, replica_groups=mesh['ctx'=16,'ep'=32] {'ep'}, dimensions={0} | all-to-all | bytes 245760 | tf_op jit(solution)/shard_map/all_to_all | solution.py:112
  199.6 1.9 reshape.138
  204.4 3.7 copy.128
  208.1 4.7 all-to-all-start.3
  214.2 32.6 %all-to-all-done.3 = bf16[32,16,20,96]{3,1,2,0:T(8,128)(2,1)} async-done(((bf16[32,16,20,96]{3,1,2,0:T(8,128)(2,1)}), bf16[32,16,20,96]{3,1,2,0:T(8,128)(2,1)}, u32[]{:S(2)}, u32[]{:S(2)}) %all-to-all-start.3) | async-done | bytes 1966112 | tf_op jit(solution)/shard_map/all_to_all | solution.py:137
  246.9 6.2 %all-to-all-start.2 = ((bf16[32,256,96]{1,2,0:T(8,128)(2,1)}), bf16[32,256,96]{1,2,0:T(8,128)(2,1)S(1)}, u32[]{:S(2)}, u32[]{:S(2)}) async-start(bf16[32,256,96]{1,2,0:T(8,128)(2,1)} %bitcast.172), calls=%async_computation.2 | async-start | bytes 3145728 | tf_op jit(solution)/shard_map/all_to_all | solution.py:122
  253.0 5.0 copy.129
  258.0 6.0 %reshape.133 = bf16[320,3072]{1,0:T(8,128)(2,1)} reshape(bf16[16,20,32,96]{3,2,1,0:T(8,128)(2,1)} %copy.129) | data formatting | bytes 3932160 | tf_op jit(solution)/shard_map/reshape | solution.py:138
  264.0 3.2 fusion.3
  267.2 4.0 reshape.141
  271.1 4.2 all-to-all-done.2
  275.4 3.4 fusion.11
  281.9 2.0 fusion.2
  283.9 55.1 %fusion.61 = (bf16[24,3072]{1,0:T(8,128)(2,1)}, bf16[24,3072]{1,0:T(8,128)(2,1)}) fusion(bf16[320,3072]{1,0:T(8,128)(2,1)S(1)} %convolution_convert_fusion, bf16[320,3072]{1,0:T(8,128)(2,1)} %fusion.2), kind=kCustom, calls=%all-reduce-scatter.2 | all-reduce-scatter fusion | flops 2359297 | bytes 4229120
  340.0 2.9 collective-permute-start.8
  342.9 2.0 collective-permute-start.9
  344.9 4.3 collective-permute-start.10
  349.3 2.2 collective-permute-start.11
  351.5 5.0 %collective-permute-start.12 = (bf16[24,3072]{1,0:T(8,128)(2,1)}, bf16[24,3072]{1,0:T(8,128)(2,1)S(1)}, u32[]{:S(2)}, u32[]{:S(2)}) collective-permute-start(bf16[24,3072]{1,0:T(8,128)(2,1)} %get-tuple-element.49), channel_id=1, source_target_pairs={{0,64},{32,96},{64,128},{96,160},{128,192},{160,224},{192,256},{22... | collective-permute-start | bytes 442376
  357.5 3.9 collective-permute-start.13
  363.3 2.5 concatenate
  365.8 2.5 concatenate.1
  369.9 9.4 %all-to-all-start.4 = ((bf16[20,32,96]{2,0,1:T(8,128)(2,1)}), bf16[20,32,96]{2,0,1:T(8,128)(2,1)S(1)}, u32[]{:S(2)}, u32[]{:S(2)}) async-start(bf16[20,32,96]{2,0,1:T(8,128)(2,1)} %copy.130), calls=%async_computation.4 | async-start | bytes 393216 | tf_op jit(solution)/shard_map/all_to_all | solution.py:153
  379.5 8.2 %all-to-all-done.4 = bf16[20,32,96]{2,0,1:T(8,128)(2,1)S(1)} async-done(((bf16[20,32,96]{2,0,1:T(8,128)(2,1)}), bf16[20,32,96]{2,0,1:T(8,128)(2,1)S(1)}, u32[]{:S(2)}, u32[]{:S(2)}) %all-to-all-start.4) | async-done | bytes 122912 | tf_op jit(solution)/shard_map/all_to_all | solution.py:153
  388.0 10.9 %all_to_all.63 = f32[32,128,2]{1,2,0:T(2,128)S(1)} all-to-all(f32[32,128,2]{1,2,0:T(2,128)S(1)} %broadcast_in_dim.29), channel_id=1, replica_groups=mesh['ctx'=16,'ep'=32] {'ep'}, dimensions={0} | all-to-all | bytes 65536 | tf_op jit(solution)/shard_map/all_to_all | solution.py:26
  400.0 4.0 all-to-all-start.6
  404.0 14.3 %all-to-all-done.6 = bf16[32,128,96]{1,2,0:T(8,128)(2,1)S(1)} async-done(((bf16[32,128,96]{1,2,0:T(8,128)(2,1)}), bf16[32,128,96]{1,2,0:T(8,128)(2,1)S(1)}, u32[]{:S(2)}, u32[]{:S(2)}) %all-to-all-start.6) | async-done | bytes 786464 | tf_op jit(solution)/shard_map/all_to_all | solution.py:26
  419.9 5.5 %collective-permute-start.4 = (f32[2,128,128]{2,1,0:T(8,128)S(1)}, f32[2,128,128]{2,1,0:T(8,128)S(1)}, u32[]{:S(2)}, u32[]{:S(2)}) collective-permute-start(f32[2,128,128]{2,1,0:T(8,128)S(1)} %convolution_bitcast_fusion.4), channel_id=1, source_target_pairs={{0,32},{32,0},{64,96},{96,64},{128,160},{160,128},{192,224},{224,1... | collective-permute-start | bytes 393224 | tf_op jit(solution)/shard_map/ppermute | solution.py:14
  427.5 4.4 all-to-all-start.7
  431.9 6.9 %collective-permute-start.5 = (f32[2,128,128]{2,1,0:T(8,128)S(1)}, f32[2,128,128]{2,1,0:T(8,128)S(1)}, u32[]{:S(2)}, u32[]{:S(2)}) collective-permute-start(f32[2,128,128]{2,1,0:T(8,128)S(1)} %add.136), channel_id=1, source_target_pairs={{0,64},{32,96},{64,0},{96,32},{128,192},{160,224},{192,128},{224,1... | collective-permute-start | bytes 393224 | tf_op jit(solution)/shard_map/ppermute | solution.py:14
  439.1 6.4 %collective-permute-done.5 = f32[2,128,128]{2,1,0:T(8,128)S(1)} collective-permute-done((f32[2,128,128]{2,1,0:T(8,128)S(1)}, f32[2,128,128]{2,1,0:T(8,128)S(1)}, u32[]{:S(2)}, u32[]{:S(2)}) %collective-permute-start.5) | collective-permute-done | bytes 131104 | tf_op jit(solution)/shard_map/ppermute | solution.py:14
  445.4 8.2 %collective-permute-start.6 = (f32[2,128,128]{2,1,0:T(8,128)S(1)}, f32[2,128,128]{2,1,0:T(8,128)S(1)}, u32[]{:S(2)}, u32[]{:S(2)}) collective-permute-start(f32[2,128,128]{2,1,0:T(8,128)S(1)} %add.138), channel_id=1, source_target_pairs={{0,128},{32,160},{64,192},{96,224},{128,0},{160,32},{192,64},{224,... | collective-permute-start | bytes 393224 | tf_op jit(solution)/shard_map/ppermute | solution.py:14
  453.8 11.0 %collective-permute-done.6 = f32[2,128,128]{2,1,0:T(8,128)S(1)} collective-permute-done((f32[2,128,128]{2,1,0:T(8,128)S(1)}, f32[2,128,128]{2,1,0:T(8,128)S(1)}, u32[]{:S(2)}, u32[]{:S(2)}) %collective-permute-start.6) | collective-permute-done | bytes 131104 | tf_op jit(solution)/shard_map/ppermute | solution.py:14
  464.8 10.6 %collective-permute-start.7 = (f32[2,128,128]{2,1,0:T(8,128)S(1)}, f32[2,128,128]{2,1,0:T(8,128)S(1)}, u32[]{:S(2)}, u32[]{:S(2)}) collective-permute-start(f32[2,128,128]{2,1,0:T(8,128)S(1)} %add.140), channel_id=1, source_target_pairs={{0,256},{32,288},{64,320},{96,352},{128,384},{160,416},{192,448},{... | collective-permute-start | bytes 393224 | tf_op jit(solution)/shard_map/ppermute | solution.py:14
  476.4 11.8 %collective-permute-done.7 = f32[2,128,128]{2,1,0:T(8,128)S(1)} collective-permute-done((f32[2,128,128]{2,1,0:T(8,128)S(1)}, f32[2,128,128]{2,1,0:T(8,128)S(1)}, u32[]{:S(2)}, u32[]{:S(2)}) %collective-permute-start.7) | collective-permute-done | bytes 131104 | tf_op jit(solution)/shard_map/ppermute | solution.py:14
  (179 shorter events, 42.9 us)
Async XLA Ops:
  7.2 256.8 %copy-start = (bf16[1,192,3072]{2,1,0:T(8,128)(2,1)S(1)}, bf16[1,192,3072]{2,1,0:T(8,128)(2,1)}, u32[]{:S(2)}) copy-start(bf16[1,192,3072]{2,1,0:T(8,128)(2,1)} %param.28) | copy-start | bytes 3538948
  7.2 4.6 copy-start.30
  7.2 4.7 copy-start.22
  7.2 17.2 %copy-start.37 = (bf16[128,256]{1,0:T(8,128)(2,1)S(1)}, bf16[128,256]{1,0:T(8,128)(2,1)}, u32[]{:S(2)}) copy-start(bf16[128,256]{1,0:T(8,128)(2,1)} %param.15) | copy-start | bytes 196612
  7.2 91.4 %all-gather.8.cloned.1.call-start = ((), (), s32[]{:S(2)}) async-start(), calls=%async_computation.9 | async-start | bytes 2088960 | tf_op jit(solution)/shard_map/all_gather | solution.py:81
  11.7 154.6 %all-gather.6.cloned.1.call-start = ((), (), s32[]{:S(2)}) async-start(), calls=%async_computation.8 | async-start | bytes 1671168 | tf_op jit(solution)/shard_map/all_gather | solution.py:83
  11.9 86.7 %copy-start.20 = (bf16[128,256]{0,1:T(8,128)(2,1)}, bf16[128,256]{0,1:T(8,128)(2,1)S(1)}, u32[]{:S(2)}) copy-start(bf16[128,256]{0,1:T(8,128)(2,1)S(1)} %copy.194) | copy-start | bytes 196612
  12.1 6.7 %collective-permute-start = (f32[2,128,128]{2,1,0:T(8,128)S(1)}, f32[2,128,128]{2,1,0:T(8,128)S(1)}, u32[]{:S(2)}, u32[]{:S(2)}) collective-permute-start(f32[2,128,128]{2,1,0:T(8,128)S(1)} %fusion.41), channel_id=1, source_target_pairs={{0,32},{32,0},{64,96},{96,64},{128,160},{160,128},{192,224},{224,1... | collective-permute-start | bytes 393224 | tf_op jit(solution)/shard_map/ppermute | solution.py:14
  18.8 79.8 %copy-start.25 = (f32[2,128,128]{2,1,0:T(8,128)}, f32[2,128,128]{2,1,0:T(8,128)S(1)}, u32[]{:S(2)}) copy-start(f32[2,128,128]{2,1,0:T(8,128)S(1)} %collective-permute-done) | copy-start | bytes 393220
  18.8 9.4 %collective-permute-start.1 = (f32[2,128,128]{2,1,0:T(8,128)S(1)}, f32[2,128,128]{2,1,0:T(8,128)S(1)}, u32[]{:S(2)}, u32[]{:S(2)}) collective-permute-start(f32[2,128,128]{2,1,0:T(8,128)S(1)} %add.115), channel_id=1, source_target_pairs={{0,64},{32,96},{64,0},{96,32},{128,192},{160,224},{192,128},{224,1... | collective-permute-start | bytes 393224 | tf_op jit(solution)/shard_map/ppermute | solution.py:14
  24.6 76.9 %copy-start.15 = (bf16[128,256]{0,1:T(8,128)(2,1)}, bf16[128,256]{0,1:T(8,128)(2,1)S(1)}, u32[]{:S(2)}) copy-start(bf16[128,256]{0,1:T(8,128)(2,1)S(1)} %copy.159) | copy-start | bytes 196612
  28.2 70.4 %copy-start.26 = (f32[2,128,128]{2,1,0:T(8,128)}, f32[2,128,128]{2,1,0:T(8,128)S(1)}, u32[]{:S(2)}) copy-start(f32[2,128,128]{2,1,0:T(8,128)S(1)} %collective-permute-done.1) | copy-start | bytes 393220
  28.2 24.4 %collective-permute-start.2 = (f32[2,128,128]{2,1,0:T(8,128)S(1)}, f32[2,128,128]{2,1,0:T(8,128)S(1)}, u32[]{:S(2)}, u32[]{:S(2)}) collective-permute-start(f32[2,128,128]{2,1,0:T(8,128)S(1)} %add.117), channel_id=1, source_target_pairs={{0,128},{32,160},{64,192},{96,224},{128,0},{160,32},{192,64},{224,... | collective-permute-start | bytes 393224 | tf_op jit(solution)/shard_map/ppermute | solution.py:14
  39.3 59.3 %copy-start.32 = (bf16[2,128,128]{2,1,0:T(8,128)(2,1)}, bf16[2,128,128]{2,1,0:T(8,128)(2,1)S(1)}, u32[]{:S(2)}) copy-start(bf16[2,128,128]{2,1,0:T(8,128)(2,1)S(1)} %fusion.16) | copy-start | bytes 196612
  52.7 46.0 %copy-start.27 = (f32[2,128,128]{2,1,0:T(8,128)}, f32[2,128,128]{2,1,0:T(8,128)S(1)}, u32[]{:S(2)}) copy-start(f32[2,128,128]{2,1,0:T(8,128)S(1)} %collective-permute-done.2) | copy-start | bytes 393220
  53.4 47.2 %collective-permute-start.3 = (f32[2,128,128]{2,1,0:T(8,128)}, f32[2,128,128]{2,1,0:T(8,128)}, u32[]{:S(2)}, u32[]{:S(2)}) collective-permute-start(f32[2,128,128]{2,1,0:T(8,128)} %add.119), channel_id=1, source_target_pairs={{0,256},{32,288},{64,320},{96,352},{128,384},{160,416},{192,448},{... | collective-permute-start | bytes 393224 | tf_op jit(solution)/shard_map/ppermute | solution.py:14
  107.4 58.9 %copy-start.44 = (bf16[128,96]{0,1:T(8,128)(2,1)S(1)}, bf16[128,96]{0,1:T(8,128)(2,1)}, u32[]{:S(2)}) copy-start(bf16[128,96]{0,1:T(8,128)(2,1)} %param.21) | copy-start | bytes 73732
  107.4 43.1 %all-to-all-start = ((bf16[32,128,256]{2,1,0:T(8,128)(2,1)}), bf16[32,128,256]{2,1,0:T(8,128)(2,1)}, u32[]{:S(2)}, u32[]{:S(2)}) async-start(bf16[32,128,256]{2,1,0:T(8,128)(2,1)} %broadcast_in_dim.28), calls=%async_computation | async-start | bytes 4194304 | tf_op jit(solution)/shard_map/all_to_all | solution.py:26
  121.7 145.5 %all-gather.10.cloned.1.call-start = ((), (), s32[]{:S(2)}) async-start(), calls=%async_computation.10 | async-start | bytes 2506752 | tf_op jit(solution)/shard_map/all_gather | solution.py:123
  169.2 229.7 %copy-start.28 = (bf16[128,96]{0,1:T(8,128)(2,1)}, bf16[128,96]{0,1:T(8,128)(2,1)S(1)}, u32[]{:S(2)}) copy-start(bf16[128,96]{0,1:T(8,128)(2,1)S(1)} %fusion.24) | copy-start | bytes 73732
  169.2 33.4 %copy-start.38 = (f32[3072]{0:T(1024)S(1)}, f32[3072]{0:T(1024)}, u32[]{:S(2)}) copy-start(f32[3072]{0:T(1024)} %param.22) | copy-start | bytes 36868
  208.1 4.7 copy-start.10
  208.1 38.7 %all-to-all-start.3 = ((bf16[32,16,20,96]{3,1,2,0:T(8,128)(2,1)}), bf16[32,16,20,96]{3,1,2,0:T(8,128)(2,1)}, u32[]{:S(2)}, u32[]{:S(2)}) async-start(bf16[32,16,20,96]{3,1,2,0:T(8,128)(2,1)} %bitcast.170), calls=%async_computation.3 | async-start | bytes 5242880 | tf_op jit(solution)/shard_map/all_to_all | solution.py:137
  246.9 28.5 %all-to-all-start.2 = ((bf16[32,256,96]{1,2,0:T(8,128)(2,1)}), bf16[32,256,96]{1,2,0:T(8,128)(2,1)S(1)}, u32[]{:S(2)}, u32[]{:S(2)}) async-start(bf16[32,256,96]{1,2,0:T(8,128)(2,1)} %bitcast.172), calls=%async_computation.2 | async-start | bytes 3145728 | tf_op jit(solution)/shard_map/all_to_all | solution.py:122
  340.0 23.3 %collective-permute-start.8 = (bf16[24,3072]{1,0:T(8,128)(2,1)}, bf16[24,3072]{1,0:T(8,128)(2,1)S(1)}, u32[]{:S(2)}, u32[]{:S(2)}) collective-permute-start(bf16[24,3072]{1,0:T(8,128)(2,1)} %get-tuple-element.48), channel_id=1, source_target_pairs={{0,32},{32,64},{64,96},{96,128},{128,160},{160,192},{192,224},{224... | collective-permute-start | bytes 442376
  342.9 20.4 %collective-permute-start.9 = (bf16[24,3072]{1,0:T(8,128)(2,1)}, bf16[24,3072]{1,0:T(8,128)(2,1)S(1)}, u32[]{:S(2)}, u32[]{:S(2)}) collective-permute-start(bf16[24,3072]{1,0:T(8,128)(2,1)} %get-tuple-element.48), channel_id=1, source_target_pairs={{0,64},{32,96},{64,128},{96,160},{128,192},{160,224},{192,256},{22... | collective-permute-start | bytes 442376
  344.9 12.6 %collective-permute-start.10 = (bf16[12,3072]{1,0:T(8,128)(2,1)S(1)}, bf16[12,3072]{1,0:T(8,128)(2,1)S(1)}, u32[]{:S(2)}, u32[]{:S(2)}) collective-permute-start(bf16[12,3072]{1,0:T(8,128)(2,1)S(1)} %slice.8), channel_id=1, source_target_pairs={{0,96},{32,128},{64,160},{96,192},{128,224},{160,256},{192,288},{2... | collective-permute-start | bytes 221192
  349.3 16.5 %collective-permute-start.11 = (bf16[24,3072]{1,0:T(8,128)(2,1)}, bf16[24,3072]{1,0:T(8,128)(2,1)S(1)}, u32[]{:S(2)}, u32[]{:S(2)}) collective-permute-start(bf16[24,3072]{1,0:T(8,128)(2,1)} %get-tuple-element.49), channel_id=1, source_target_pairs={{0,32},{32,64},{64,96},{96,128},{128,160},{160,192},{192,224},{224... | collective-permute-start | bytes 442376
  351.5 14.3 %collective-permute-start.12 = (bf16[24,3072]{1,0:T(8,128)(2,1)}, bf16[24,3072]{1,0:T(8,128)(2,1)S(1)}, u32[]{:S(2)}, u32[]{:S(2)}) collective-permute-start(bf16[24,3072]{1,0:T(8,128)(2,1)} %get-tuple-element.49), channel_id=1, source_target_pairs={{0,64},{32,96},{64,128},{96,160},{128,192},{160,224},{192,256},{22... | collective-permute-start | bytes 442376
  357.5 8.3 %collective-permute-start.13 = (bf16[12,3072]{1,0:T(8,128)(2,1)S(1)}, bf16[12,3072]{1,0:T(8,128)(2,1)S(1)}, u32[]{:S(2)}, u32[]{:S(2)}) collective-permute-start(bf16[12,3072]{1,0:T(8,128)(2,1)S(1)} %slice.9), channel_id=1, source_target_pairs={{0,96},{32,128},{64,160},{96,192},{128,224},{160,256},{192,288},{2... | collective-permute-start | bytes 221192
  365.8 33.2 %copy-start.36 = (bf16[128,96]{0,1:T(8,128)(2,1)S(1)}, bf16[128,96]{0,1:T(8,128)(2,1)}, u32[]{:S(2)}) copy-start(bf16[128,96]{0,1:T(8,128)(2,1)} %param.29) | copy-start | bytes 73732
  369.2 49.1 %copy-start.2 = (bf16[32,256,96]{1,2,0:T(8,128)(2,1)S(1)}, bf16[32,256,96]{1,2,0:T(8,128)(2,1)}, u32[]{:S(2)}) copy-start(bf16[32,256,96]{1,2,0:T(8,128)(2,1)} %copy-done.1) | copy-start | bytes 4718596
  369.9 17.7 %all-to-all-start.4 = ((bf16[20,32,96]{2,0,1:T(8,128)(2,1)}), bf16[20,32,96]{2,0,1:T(8,128)(2,1)S(1)}, u32[]{:S(2)}, u32[]{:S(2)}) async-start(bf16[20,32,96]{2,0,1:T(8,128)(2,1)} %copy.130), calls=%async_computation.4 | async-start | bytes 393216 | tf_op jit(solution)/shard_map/all_to_all | solution.py:153
  400.0 18.3 %all-to-all-start.6 = ((bf16[32,128,96]{1,2,0:T(8,128)(2,1)}), bf16[32,128,96]{1,2,0:T(8,128)(2,1)S(1)}, u32[]{:S(2)}, u32[]{:S(2)}) async-start(bf16[32,128,96]{1,2,0:T(8,128)(2,1)} %broadcast_in_dim.30), calls=%async_computation.6 | async-start | bytes 1572864 | tf_op jit(solution)/shard_map/all_to_all | solution.py:26
  418.4 7.0 %copy-start.21 = (bf16[128,256]{0,1:T(8,128)(2,1)S(1)}, bf16[128,256]{0,1:T(8,128)(2,1)}, u32[]{:S(2)}) copy-start(bf16[128,256]{0,1:T(8,128)(2,1)} %copy-done.20) | copy-start | bytes 196612
  418.4 7.2 %copy-start.12 = (f32[2,128,128]{2,1,0:T(8,128)S(1)}, f32[2,128,128]{2,1,0:T(8,128)}, u32[]{:S(2)}) copy-start(f32[2,128,128]{2,1,0:T(8,128)} %copy-done.11) | copy-start | bytes 393220
  419.1 7.4 %copy-start.19 = (bf16[20,3072]{1,0:T(8,128)(2,1)S(1)}, bf16[20,3072]{1,0:T(8,128)(2,1)}, u32[]{:S(2)}) copy-start(bf16[20,3072]{1,0:T(8,128)(2,1)} %get-tuple-element.16) | copy-start | bytes 368644
  419.1 19.8 %copy-start.33 = (bf16[2,128,128]{2,1,0:T(8,128)(2,1)S(1)}, bf16[2,128,128]{2,1,0:T(8,128)(2,1)}, u32[]{:S(2)}) copy-start(bf16[2,128,128]{2,1,0:T(8,128)(2,1)} %copy-done.32) | copy-start | bytes 196612
  419.2 34.5 %copy-start.17 = (bf16[128,256]{0,1:T(8,128)(2,1)S(1)}, bf16[128,256]{0,1:T(8,128)(2,1)}, u32[]{:S(2)}) copy-start(bf16[128,256]{0,1:T(8,128)(2,1)} %copy-done.15) | copy-start | bytes 196612
  419.5 55.9 %copy-start.4 = (f32[128,32,20]{0,1,2:T(8,128)S(1)}, f32[128,32,20]{0,1,2:T(8,128)}, u32[]{:S(2)}) copy-start(f32[128,32,20]{0,1,2:T(8,128)} %copy-done.3) | copy-start | bytes 983044
  419.5 55.9 %copy-start.29 = (bf16[128,96]{0,1:T(8,128)(2,1)S(1)}, bf16[128,96]{0,1:T(8,128)(2,1)}, u32[]{:S(2)}) copy-start(bf16[128,96]{0,1:T(8,128)(2,1)} %copy-done.28) | copy-start | bytes 73732
  419.9 12.0 %collective-permute-start.4 = (f32[2,128,128]{2,1,0:T(8,128)S(1)}, f32[2,128,128]{2,1,0:T(8,128)S(1)}, u32[]{:S(2)}, u32[]{:S(2)}) collective-permute-start(f32[2,128,128]{2,1,0:T(8,128)S(1)} %convolution_bitcast_fusion.4), channel_id=1, source_target_pairs={{0,32},{32,0},{64,96},{96,64},{128,160},{160,128},{192,224},{224,1... | collective-permute-start | bytes 393224 | tf_op jit(solution)/shard_map/ppermute | solution.py:14
  426.7 62.2 %copy-start.31 = (bf16[128,256]{1,0:T(8,128)(2,1)S(1)}, bf16[128,256]{1,0:T(8,128)(2,1)}, u32[]{:S(2)}) copy-start(bf16[128,256]{1,0:T(8,128)(2,1)} %param.16) | copy-start | bytes 196612
  427.5 62.5 %copy-start.24 = (bf16[128,256]{1,0:T(8,128)(2,1)S(1)}, bf16[128,256]{1,0:T(8,128)(2,1)}, u32[]{:S(2)}) copy-start(bf16[128,256]{1,0:T(8,128)(2,1)} %param.17) | copy-start | bytes 196612
  427.5 47.9 %all-to-all-start.7 = ((bf16[20,32,96]{2,0,1:T(8,128)(2,1)}), bf16[20,32,96]{2,0,1:T(8,128)(2,1)S(1)}, u32[]{:S(2)}, u32[]{:S(2)}) async-start(bf16[20,32,96]{2,0,1:T(8,128)(2,1)} %copy.135), calls=%async_computation.7 | async-start | bytes 393216 | tf_op jit(solution)/shard_map/all_to_all | solution.py:176
  431.9 13.5 %collective-permute-start.5 = (f32[2,128,128]{2,1,0:T(8,128)S(1)}, f32[2,128,128]{2,1,0:T(8,128)S(1)}, u32[]{:S(2)}, u32[]{:S(2)}) collective-permute-start(f32[2,128,128]{2,1,0:T(8,128)S(1)} %add.136), channel_id=1, source_target_pairs={{0,64},{32,96},{64,0},{96,32},{128,192},{160,224},{192,128},{224,1... | collective-permute-start | bytes 393224 | tf_op jit(solution)/shard_map/ppermute | solution.py:14
  445.4 19.4 %collective-permute-start.6 = (f32[2,128,128]{2,1,0:T(8,128)S(1)}, f32[2,128,128]{2,1,0:T(8,128)S(1)}, u32[]{:S(2)}, u32[]{:S(2)}) collective-permute-start(f32[2,128,128]{2,1,0:T(8,128)S(1)} %add.138), channel_id=1, source_target_pairs={{0,128},{32,160},{64,192},{96,224},{128,0},{160,32},{192,64},{224,... | collective-permute-start | bytes 393224 | tf_op jit(solution)/shard_map/ppermute | solution.py:14
  464.8 23.4 %collective-permute-start.7 = (f32[2,128,128]{2,1,0:T(8,128)S(1)}, f32[2,128,128]{2,1,0:T(8,128)S(1)}, u32[]{:S(2)}, u32[]{:S(2)}) collective-permute-start(f32[2,128,128]{2,1,0:T(8,128)S(1)} %add.140), channel_id=1, source_target_pairs={{0,256},{32,288},{64,320},{96,352},{128,384},{160,416},{192,448},{... | collective-permute-start | bytes 393224 | tf_op jit(solution)/shard_map/ppermute | solution.py:14
  (20 other events, 36.0 us)
Sparse Core Ops, SparseCore 0:
  11.8 86.7 all-gather.7
  100.7 65.6 all-gather.5
  204.5 58.1 all-gather.9

commit v4 on v1

--- a/solution.py
+++ b/solution.py
@@ -24,6 +24,15 @@
     count = lax.axis_size(axis)
     spread = jnp.broadcast_to(value[None], (count,) + value.shape)
     return lax.all_to_all(spread, axis, 0, 0, tiled=True)
+
+
+def scatter_sum(value, axis):
+    count = lax.axis_size(axis)
+    rows, width = value.shape
+    block = rows // count
+    dense = value.reshape(count, block * width // 128, 128)
+    part = lax.psum_scatter(dense, axis, scatter_dimension=0, tiled=True)
+    return part.reshape(block, width)
 
 
 def head_normalize(attended, gain):
@@ -116,17 +125,16 @@
     hidden_block = w_gate.shape[0]
     w_rows = lax.all_to_all(w_blocks, "ep", 0, 0, tiled=True)
     portion = lax.all_gather(expert_in, "ctx", axis=0, tiled=True)
-    portion, w_rows = lax.optimization_barrier((portion, w_rows))
+    square_sums = jnp.sum(gather_blocks(jnp.sum(stream_f * stream_f, -1, keepdims=True), "ep"), 0)
+    portion, w_rows, square_sums = lax.optimization_barrier((portion, w_rows, square_sums))
+    row_scale = lax.rsqrt(square_sums / model_width + 1e-05)
     projected = jnp.concatenate([contract_last(portion, w_gate), contract_last(portion, w_up)], 1)
     pre_gate = projected[:, :hidden_block]
     pre_up = projected[:, hidden_block:]
     gate_sig = jax.nn.sigmoid(pre_gate)
     activated = (pre_gate * gate_sig * pre_up).astype(jnp.bfloat16)
-    half_out = lax.psum_scatter(
-        jnp.dot(activated, w_down, preferred_element_type=f32).astype(jnp.bfloat16),
-        "ctx",
-        scatter_dimension=0,
-        tiled=True,
+    half_out = scatter_sum(
+        jnp.dot(activated, w_down, preferred_element_type=f32).astype(jnp.bfloat16), "ctx"
     )
     grad_out = out_grad.astype(f32)
     grad_send = jnp.dot(dest_weights.T, grad_out, precision=high).astype(jnp.bfloat16)
@@ -136,24 +144,27 @@
         jnp.bfloat16
     )
     grad_up_pre = (grad_act * pre_gate * gate_sig).astype(jnp.bfloat16)
-    grad_half = lax.psum_scatter(
+    grad_half = scatter_sum(
         (
             jnp.dot(grad_gate_pre, w_gate, preferred_element_type=f32)
             + jnp.dot(grad_up_pre, w_up, preferred_element_type=f32)
         ).astype(jnp.bfloat16),
         "ctx",
-        scatter_dimension=0,
-        tiled=True,
-    )
-    grad_back = lax.all_to_all(grad_half, "ep", split_axis=1, concat_axis=0, tiled=True)
-    grad_model_in = jnp.dot(dest_picks, grad_back.astype(f32), precision=high)
+    )
+    slot_inner = jnp.sum(slot_rows * model_gain * grad_half.astype(f32), -1, keepdims=True)
+    inner_hi = slot_inner.astype(jnp.bfloat16)
+    inner_lo = (slot_inner - inner_hi.astype(f32)).astype(jnp.bfloat16)
+    inner_pair = jnp.broadcast_to(
+        jnp.concatenate([inner_hi, inner_lo], -1)[:, None, :], (capacity, ep_count, 2)
+    )
+    payload = jnp.concatenate([grad_half.reshape(capacity, ep_count, columns), inner_pair], -1)
+    grad_back = lax.all_to_all(payload, "ep", split_axis=1, concat_axis=0, tiled=True)
+    grad_back = grad_back.reshape(ep_count * capacity, columns + 2).astype(f32)
+    grad_model_in = jnp.dot(dest_picks, grad_back[:, :columns], precision=high)
     scaled_grad = grad_model_in * gain_cols
-    row_parts = jnp.stack(
-        [jnp.sum(stream_f * stream_f, -1), jnp.sum(stream_f * scaled_grad, -1)], -1
-    )
-    row_sums = jnp.sum(gather_blocks(row_parts, "ep"), 0)
-    row_scale = lax.rsqrt(row_sums[:, :1] / model_width + 1e-05)
-    inner_sum = row_sums[:, 1:]
+    inner_sum = jnp.dot(
+        dest_picks, grad_back[:, columns:columns + 1] + grad_back[:, columns + 1:], precision=high
+    )
     grad_stream = (
         grad_out
         + row_scale * scaled_grad

time: 469 us -> 485 us (1.034)
  waiting for transfers between devices: 187 us -> 276 us
  blocking collectives: 72.6 us -> 12.8 us
  starting transfers between devices: 133 us -> 117 us
    reduce_scatter x0 -> x2, waiting for transfers between devices: none -> 102 us  [scatter_sum(): part = lax.psum_scatter(dense, axis, scatter_dimension=0, tiled=True)]
    unnamed x1 -> x0, blocking collectives: 49 us -> none
    unnamed x6 -> x0, starting transfers between devices: 21.8 us -> none
    all_to_all x1, starting transfers between devices: 4.16 us -> 17.8 us  [local(): lax.all_to_all(half_out, 'ep', split_axis=1, concat_axis=0, tiled=True)]
    all_to_all x1 -> x0, blocking collectives: 10.9 us -> none  [gather_blocks(): return lax.all_to_all(spread, axis, 0, 0, tiled=True)]
    all_gather x1, waiting for transfers between devices: 23 us -> 12.6 us  [local(): lax.all_gather(grad_in, 'ctx', axis=0, tiled=True)]
    all_to_all x1, starting transfers between devices: 27.2 us -> 18.2 us  [local(): lax.all_to_all(payload, 'ep', split_axis=1, concat_axis=0, tiled=True)]
    all_to_all x2 -> x3, waiting for transfers between devices: 41.9 us -> 32.9 us  [gather_blocks(): return lax.all_to_all(spread, axis, 0, 0, tiled=True)]
  transfers between devices with their start and end apart: 23 -> 20, of which waited for: 10 -> 13; matrix products, arithmetic and copies ran while one was open for 8% -> 9% of each run, Pallas kernels for 0% -> 0%
where the time goes in v4:
time: 485 us; the launch traced here: 483 us
  waiting for transfers between devices  276 us (57%)
  starting transfers between devices  117 us (24%)
  local copies, waits for them, and re-layouts  32.3 us (7%)
  matrix products  23.3 us (5%)
  between operations  14.8 us (3%)
  blocking collectives  12.8 us (3%)
  other arithmetic  6.78 us (1%)
    reduce_scatter x2, waiting for transfers between devices, scatter_sum(): part = lax.psum_scatter(dense, axis, scatter_dimension=0, tiled=True)  102 us
    all_gather x1, waiting for transfers between devices, local(): portion = lax.all_gather(expert_in, 'ctx', axis=0, tiled=True)  65.4 us
    ppermute x8, waiting for transfers between devices, butterfly_sums(): other = lax.ppermute(total, axis, [(i, i ^ step) for i in range(count)])  54.4 us
    ppermute x8, starting transfers between devices, butterfly_sums(): other = lax.ppermute(total, axis, [(i, i ^ step) for i in range(count)])  48.8 us
    all_to_all x3, waiting for transfers between devices, gather_blocks(): return lax.all_to_all(spread, axis, 0, 0, tiled=True)  32.9 us
    all_to_all x3, starting transfers between devices, gather_blocks(): return lax.all_to_all(spread, axis, 0, 0, tiled=True)  18.8 us
    all_to_all x1, starting transfers between devices, local(): lax.all_to_all(payload, 'ep', split_axis=1, concat_axis=0, tiled=True)  18.2 us
    all_to_all x1, starting transfers between devices, local(): lax.all_to_all(half_out, 'ep', split_axis=1, concat_axis=0, tiled=True)  17.8 us
  transfers between devices with their start and end apart: 20, of which 13 were waited for; matrix products, arithmetic and copies ran while one was open for 9% of the time, Pallas kernels for 0%

profile of v4, /device:TPU:1, one launch (start us, length us, event | category | flops | bytes accessed | tf_op | source)
XLA Modules:
  0.0 483.2 jit_solution(12952110606629207792)
XLA Ops:
  8.9 1.0 fusion.47
  9.9 4.4 collective-permute-start
  17.7 5.0 %collective-permute-start.1 = (f32[2,128,128]{2,1,0:T(8,128)S(1)}, f32[2,128,128]{2,1,0:T(8,128)S(1)}, u32[]{:S(2)}, u32[]{:S(2)}) collective-permute-start(f32[2,128,128]{2,1,0:T(8,128)S(1)} %add.118), channel_id=1, source_target_pairs={{0,64},{32,96},{64,0},{96,32},{128,192},{160,224},{192,128},{224,1... | collective-permute-start | bytes 393224 | tf_op jit(solution)/shard_map/ppermute | solution.py:14
  24.0 8.5 %all-to-all-start.4 = ((bf16[32,20,96]{2,1,0:T(8,128)(2,1)}), bf16[32,20,96]{2,1,0:T(8,128)(2,1)S(1)}, u32[]{:S(2)}, u32[]{:S(2)}) async-start(bf16[32,20,96]{2,1,0:T(8,128)(2,1)} %all_to_all.56), calls=%async_computation.5 | async-start | bytes 393216 | tf_op jit(solution)/shard_map/all_to_all | solution.py:141
  32.8 8.8 %collective-permute-start.2 = (f32[2,128,128]{2,1,0:T(8,128)S(1)}, f32[2,128,128]{2,1,0:T(8,128)S(1)}, u32[]{:S(2)}, u32[]{:S(2)}) collective-permute-start(f32[2,128,128]{2,1,0:T(8,128)S(1)} %add.120), channel_id=1, source_target_pairs={{0,128},{32,160},{64,192},{96,224},{128,0},{160,32},{192,64},{224,... | collective-permute-start | bytes 393224 | tf_op jit(solution)/shard_map/ppermute | solution.py:14
  41.8 14.2 %collective-permute-done.2 = f32[2,128,128]{2,1,0:T(8,128)S(1)} collective-permute-done((f32[2,128,128]{2,1,0:T(8,128)S(1)}, f32[2,128,128]{2,1,0:T(8,128)S(1)}, u32[]{:S(2)}, u32[]{:S(2)}) %collective-permute-start.2) | collective-permute-done | bytes 131104 | tf_op jit(solution)/shard_map/ppermute | solution.py:14
  56.1 11.0 %collective-permute-start.3 = (f32[2,128,128]{2,1,0:T(8,128)S(1)}, f32[2,128,128]{2,1,0:T(8,128)S(1)}, u32[]{:S(2)}, u32[]{:S(2)}) collective-permute-start(f32[2,128,128]{2,1,0:T(8,128)S(1)} %add.122), channel_id=1, source_target_pairs={{0,256},{32,288},{64,320},{96,352},{128,384},{160,416},{192,448},{... | collective-permute-start | bytes 393224 | tf_op jit(solution)/shard_map/ppermute | solution.py:14
  67.3 4.3 collective-permute-done.3
  72.9 1.6 broadcast_in_dim.30
  74.5 10.5 %all-to-all-start = ((bf16[32,128,256]{2,1,0:T(8,128)(2,1)}), bf16[32,128,256]{2,1,0:T(8,128)(2,1)}, u32[]{:S(2)}, u32[]{:S(2)}) async-start(bf16[32,128,256]{2,1,0:T(8,128)(2,1)} %broadcast_in_dim.30), calls=%async_computation | async-start | bytes 4194304 | tf_op jit(solution)/shard_map/all_to_all | solution.py:26
  86.3 27.4 %all-to-all-done = bf16[32,128,256]{2,1,0:T(8,128)(2,1)} async-done(((bf16[32,128,256]{2,1,0:T(8,128)(2,1)}), bf16[32,128,256]{2,1,0:T(8,128)(2,1)}, u32[]{:S(2)}, u32[]{:S(2)}) %all-to-all-start) | async-done | bytes 2097184 | tf_op jit(solution)/shard_map/all_to_all | solution.py:26
  113.8 3.4 fusion.51
  118.2 12.8 %all_to_all.75 = bf16[32,20,96]{2,1,0:T(8,128)(2,1)S(1)} all-to-all(bf16[32,20,96]{2,1,0:T(8,128)(2,1)S(1)} %reshape.178), channel_id=1, replica_groups=mesh['ctx'=16,'ep'=32] {'ep'}, dimensions={0} | all-to-all | bytes 245760 | tf_op jit(solution)/shard_map/all_to_all | solution.py:116
  131.8 1.9 reshape.189
  133.9 1.7 fusion.37
  136.3 3.8 all-to-all-start.3
  140.1 1.4 copy.265
  141.5 5.4 %all-to-all-done.3 = f32[32,128,1]{1,2,0:T(1,128)S(1)} async-done(((f32[32,128,1]{1,2,0:T(1,128)}), f32[32,128,1]{1,2,0:T(1,128)S(1)}, u32[]{:S(2)}, u32[]{:S(2)}) %all-to-all-start.3) | async-done | bytes 16416 | tf_op jit(solution)/shard_map/all_to_all | solution.py:26
  147.0 4.3 all-to-all-start.2
  151.9 12.6 %all-gather.10.cloned.1.call-done = bf16[16,20,3072]{2,1,0:T(8,128)(2,1)} async-done(((bf16[1,20,3072]{2,1,0:T(8,128)(2,1)}), bf16[16,20,3072]{2,1,0:T(8,128)(2,1)}) %all-gather.10.cloned.1.call-update) | async-done | bytes 1966096 | tf_op jit(solution)/shard_map/all_gather | solution.py:142
  164.4 4.0 reshape.193
  168.4 2.8 fusion.1
  171.2 65.4 %all-gather.8.cloned.1.call-done = bf16[16,20,3072]{2,1,0:T(8,128)(2,1)} async-done(((bf16[1,20,3072]{2,1,0:T(8,128)(2,1)}), bf16[16,20,3072]{2,1,0:T(8,128)(2,1)}) %all-gather.8.cloned.1.call-update) | async-done | bytes 1966096 | tf_op jit(solution)/shard_map/all_gather | solution.py:127
  236.6 4.0 reshape.191
  240.6 3.4 fusion.5
  246.4 1.7 fusion
  248.1 1.9 reshape.182
  250.2 2.2 convolution_convert_fusion
  252.4 1.9 reshape.179
  255.1 64.4 %reduce-scatter.5.cloned.1.call-done = bf16[1,480,128]{2,1,0:T(8,128)(2,1)} async-done(((bf16[16,480,128]{2,1,0:T(8,128)(2,1)}), bf16[1,480,128]{2,1,0:T(8,128)(2,1)}) %reduce-scatter.5.cloned.1.call-update) | async-done | bytes 122896 | tf_op jit(solution)/shard_map/reduce_scatter | solution.py:34
  319.5 1.1 reshape_reshape.3
  321.9 18.2 %all-to-all-start.5 = ((bf16[20,32,98]{2,0,1:T(8,128)(2,1)}), bf16[20,32,98]{2,0,1:T(8,128)(2,1)S(1)}, u32[]{:S(2)}, u32[]{:S(2)}) async-start(bf16[20,32,98]{2,0,1:T(8,128)(2,1)} %copy.203), calls=%async_computation.7 | async-start | bytes 393216 | tf_op jit(solution)/shard_map/all_to_all | solution.py:161
  340.1 8.2 %all-to-all-done.5 = bf16[20,32,98]{2,0,1:T(8,128)(2,1)S(1)} async-done(((bf16[20,32,98]{2,0,1:T(8,128)(2,1)}), bf16[20,32,98]{2,0,1:T(8,128)(2,1)S(1)}, u32[]{:S(2)}, u32[]{:S(2)}) %all-to-all-start.5) | async-done | bytes 125472 | tf_op jit(solution)/shard_map/all_to_all | solution.py:161
  349.1 1.2 fusion.25
  350.3 1.0 broadcast_in_dim.33
  351.3 4.4 all-to-all-start.6
  355.8 37.8 %reduce-scatter.3.cloned.1.call-done = bf16[1,480,128]{2,1,0:T(8,128)(2,1)} async-done(((bf16[16,480,128]{2,1,0:T(8,128)(2,1)}), bf16[1,480,128]{2,1,0:T(8,128)(2,1)}) %reduce-scatter.3.cloned.1.call-update) | async-done | bytes 122896 | tf_op jit(solution)/shard_map/reduce_scatter | solution.py:34
  393.6 1.0 reshape.180
  394.6 1.9 fusion.66
  398.1 17.8 %all-to-all-start.7 = ((bf16[20,32,96]{2,0,1:T(8,128)(2,1)}), bf16[20,32,96]{2,0,1:T(8,128)(2,1)S(1)}, u32[]{:S(2)}, u32[]{:S(2)}) async-start(bf16[20,32,96]{2,0,1:T(8,128)(2,1)} %copy.207), calls=%async_computation.9 | async-start | bytes 393216 | tf_op jit(solution)/shard_map/all_to_all | solution.py:182
  416.1 2.7 collective-permute-start.4
  419.8 3.0 collective-permute-done.4
  422.9 4.0 collective-permute-start.5
  427.0 6.3 %collective-permute-done.5 = f32[2,128,128]{2,1,0:T(8,128)S(1)} collective-permute-done((f32[2,128,128]{2,1,0:T(8,128)S(1)}, f32[2,128,128]{2,1,0:T(8,128)S(1)}, u32[]{:S(2)}, u32[]{:S(2)}) %collective-permute-start.5) | collective-permute-done | bytes 131104 | tf_op jit(solution)/shard_map/ppermute | solution.py:14
  433.3 5.6 %collective-permute-start.6 = (f32[2,128,128]{2,1,0:T(8,128)S(1)}, f32[2,128,128]{2,1,0:T(8,128)S(1)}, u32[]{:S(2)}, u32[]{:S(2)}) collective-permute-start(f32[2,128,128]{2,1,0:T(8,128)S(1)} %add.142), channel_id=1, source_target_pairs={{0,128},{32,160},{64,192},{96,224},{128,0},{160,32},{192,64},{224,... | collective-permute-start | bytes 393224 | tf_op jit(solution)/shard_map/ppermute | solution.py:14
  439.1 12.8 %collective-permute-done.6 = f32[2,128,128]{2,1,0:T(8,128)S(1)} collective-permute-done((f32[2,128,128]{2,1,0:T(8,128)S(1)}, f32[2,128,128]{2,1,0:T(8,128)S(1)}, u32[]{:S(2)}, u32[]{:S(2)}) %collective-permute-start.6) | collective-permute-done | bytes 131104 | tf_op jit(solution)/shard_map/ppermute | solution.py:14
  452.0 7.3 %collective-permute-start.7 = (f32[2,128,128]{2,1,0:T(8,128)S(1)}, f32[2,128,128]{2,1,0:T(8,128)S(1)}, u32[]{:S(2)}, u32[]{:S(2)}) collective-permute-start(f32[2,128,128]{2,1,0:T(8,128)S(1)} %add.144), channel_id=1, source_target_pairs={{0,256},{32,288},{64,320},{96,352},{128,384},{160,416},{192,448},{... | collective-permute-start | bytes 393224 | tf_op jit(solution)/shard_map/ppermute | solution.py:14
  460.2 13.7 %collective-permute-done.7 = f32[2,128,128]{2,1,0:T(8,128)S(1)} collective-permute-done((f32[2,128,128]{2,1,0:T(8,128)S(1)}, f32[2,128,128]{2,1,0:T(8,128)S(1)}, u32[]{:S(2)}, u32[]{:S(2)}) %collective-permute-start.7) | collective-permute-done | bytes 131104 | tf_op jit(solution)/shard_map/ppermute | solution.py:14
  (177 shorter events, 24.7 us)
Async XLA Ops:
  7.2 236.9 %copy-start = (bf16[1,192,3072]{2,1,0:T(8,128)(2,1)S(1)}, bf16[1,192,3072]{2,1,0:T(8,128)(2,1)}, u32[]{:S(2)}) copy-start(bf16[1,192,3072]{2,1,0:T(8,128)(2,1)} %param.26) | copy-start | bytes 3538948
  7.2 15.6 %copy-start.29 = (bf16[128,96]{0,1:T(8,128)(2,1)S(1)}, bf16[128,96]{0,1:T(8,128)(2,1)}, u32[]{:S(2)}) copy-start(bf16[128,96]{0,1:T(8,128)(2,1)} %param.29) | copy-start | bytes 73732
  7.2 106.6 %all-gather.6.cloned.1.call-start = ((), (), s32[]{:S(2)}) async-start(), calls=%async_computation.10 | async-start | bytes 1671168 | tf_op jit(solution)/shard_map/all_gather | solution.py:77
  9.9 7.8 %collective-permute-start = (f32[2,128,128]{2,1,0:T(8,128)S(1)}, f32[2,128,128]{2,1,0:T(8,128)S(1)}, u32[]{:S(2)}, u32[]{:S(2)}) collective-permute-start(f32[2,128,128]{2,1,0:T(8,128)S(1)} %fusion.47), channel_id=1, source_target_pairs={{0,32},{32,0},{64,96},{96,64},{128,160},{160,128},{192,224},{224,1... | collective-permute-start | bytes 393224 | tf_op jit(solution)/shard_map/ppermute | solution.py:14
  17.4 15.2 %copy-start.30 = (bf16[128,256]{1,0:T(8,128)(2,1)S(1)}, bf16[128,256]{1,0:T(8,128)(2,1)}, u32[]{:S(2)}) copy-start(bf16[128,256]{1,0:T(8,128)(2,1)} %param.15) | copy-start | bytes 196612
  17.6 24.0 %copy-start.21 = (bf16[128,256]{1,0:T(8,128)(2,1)S(1)}, bf16[128,256]{1,0:T(8,128)(2,1)}, u32[]{:S(2)}) copy-start(bf16[128,256]{1,0:T(8,128)(2,1)} %param.16) | copy-start | bytes 196612
  17.6 49.5 %copy-start.19 = (bf16[128,256]{1,0:T(8,128)(2,1)S(1)}, bf16[128,256]{1,0:T(8,128)(2,1)}, u32[]{:S(2)}) copy-start(bf16[128,256]{1,0:T(8,128)(2,1)} %param.17) | copy-start | bytes 196612
  17.7 53.9 %copy-start.27 = (f32[2,128,128]{2,1,0:T(8,128)S(1)}, f32[2,128,128]{2,1,0:T(8,128)}, u32[]{:S(2)}) copy-start(f32[2,128,128]{2,1,0:T(8,128)} %param.18) | copy-start | bytes 393220
  17.7 15.0 %collective-permute-start.1 = (f32[2,128,128]{2,1,0:T(8,128)S(1)}, f32[2,128,128]{2,1,0:T(8,128)S(1)}, u32[]{:S(2)}, u32[]{:S(2)}) collective-permute-start(f32[2,128,128]{2,1,0:T(8,128)S(1)} %add.118), channel_id=1, source_target_pairs={{0,64},{32,96},{64,0},{96,32},{128,192},{160,224},{192,128},{224,1... | collective-permute-start | bytes 393224 | tf_op jit(solution)/shard_map/ppermute | solution.py:14
  24.0 48.6 %copy-start.34 = (f32[256]{0:T(256)S(1)}, f32[256]{0:T(256)}, u32[]{:S(2)}) copy-start(f32[256]{0:T(256)} %param.19) | copy-start | bytes 3076
  24.0 48.9 %all-to-all-start.4 = ((bf16[32,20,96]{2,1,0:T(8,128)(2,1)}), bf16[32,20,96]{2,1,0:T(8,128)(2,1)S(1)}, u32[]{:S(2)}, u32[]{:S(2)}) async-start(bf16[32,20,96]{2,1,0:T(8,128)(2,1)} %all_to_all.56), calls=%async_computation.5 | async-start | bytes 393216 | tf_op jit(solution)/shard_map/all_to_all | solution.py:141
  32.7 41.8 %copy-start.32 = (pred[128,128]{1,0:T(8,128)(4,1)}, pred[128,128]{1,0:T(8,128)(4,1)S(1)}, u32[]{:S(2)}) copy-start(pred[128,128]{1,0:T(8,128)(4,1)S(1)} %iota_compare_fusion) | copy-start | bytes 49156
  32.8 23.3 %collective-permute-start.2 = (f32[2,128,128]{2,1,0:T(8,128)S(1)}, f32[2,128,128]{2,1,0:T(8,128)S(1)}, u32[]{:S(2)}, u32[]{:S(2)}) collective-permute-start(f32[2,128,128]{2,1,0:T(8,128)S(1)} %add.120), channel_id=1, source_target_pairs={{0,128},{32,160},{64,192},{96,224},{128,0},{160,32},{192,64},{224,... | collective-permute-start | bytes 393224 | tf_op jit(solution)/shard_map/ppermute | solution.py:14
  41.8 32.7 %copy-start.23 = (bf16[2,128,128]{2,1,0:T(8,128)(2,1)}, bf16[2,128,128]{2,1,0:T(8,128)(2,1)S(1)}, u32[]{:S(2)}) copy-start(bf16[2,128,128]{2,1,0:T(8,128)(2,1)S(1)} %fusion.14) | copy-start | bytes 196612
  56.1 15.5 %collective-permute-start.3 = (f32[2,128,128]{2,1,0:T(8,128)S(1)}, f32[2,128,128]{2,1,0:T(8,128)S(1)}, u32[]{:S(2)}, u32[]{:S(2)}) collective-permute-start(f32[2,128,128]{2,1,0:T(8,128)S(1)} %add.122), channel_id=1, source_target_pairs={{0,256},{32,288},{64,320},{96,352},{128,384},{160,416},{192,448},{... | collective-permute-start | bytes 393224 | tf_op jit(solution)/shard_map/ppermute | solution.py:14
  74.5 39.3 %all-to-all-start = ((bf16[32,128,256]{2,1,0:T(8,128)(2,1)}), bf16[32,128,256]{2,1,0:T(8,128)(2,1)}, u32[]{:S(2)}, u32[]{:S(2)}) async-start(bf16[32,128,256]{2,1,0:T(8,128)(2,1)} %broadcast_in_dim.30), calls=%async_computation | async-start | bytes 4194304 | tf_op jit(solution)/shard_map/all_to_all | solution.py:26
  85.0 28.7 %copy-start.42 = (bf16[128,96]{0,1:T(8,128)(2,1)S(1)}, bf16[128,96]{0,1:T(8,128)(2,1)}, u32[]{:S(2)}) copy-start(bf16[128,96]{0,1:T(8,128)(2,1)} %param.21) | copy-start | bytes 73732
  85.1 79.4 %all-gather.10.cloned.1.call-start = ((), (), s32[]{:S(2)}) async-start(), calls=%async_computation.14 | async-start | bytes 2506752 | tf_op jit(solution)/shard_map/all_gather | solution.py:142
  86.1 150.6 %all-gather.8.cloned.1.call-start = ((), (), s32[]{:S(2)}) async-start(), calls=%async_computation.13 | async-start | bytes 2506752 | tf_op jit(solution)/shard_map/all_gather | solution.py:127
  118.0 15.9 %copy-start.31 = (f32[3072]{0:T(1024)S(1)}, f32[3072]{0:T(1024)}, u32[]{:S(2)}) copy-start(f32[3072]{0:T(1024)} %param.22) | copy-start | bytes 36868
  118.2 21.9 %copy-start.13 = (bf16[8192,96]{0,1:T(8,128)(2,1)S(1)}, bf16[8192,96]{0,1:T(8,128)(2,1)}, u32[]{:S(2)}) copy-start(bf16[8192,96]{0,1:T(8,128)(2,1)} %all-gather.6.cloned.1.call-done) | copy-start | bytes 4718596
  131.0 10.6 %copy-start.4 = (bf16[32,20,96]{2,1,0:T(8,128)(2,1)}, bf16[32,20,96]{2,1,0:T(8,128)(2,1)S(1)}, u32[]{:S(2)}) copy-start(bf16[32,20,96]{2,1,0:T(8,128)(2,1)S(1)} %all_to_all.75) | copy-start | bytes 368644
  136.3 10.7 %all-to-all-start.3 = ((f32[32,128,1]{1,2,0:T(1,128)}), f32[32,128,1]{1,2,0:T(1,128)S(1)}, u32[]{:S(2)}, u32[]{:S(2)}) async-start(f32[32,128,1]{1,2,0:T(1,128)} %broadcast_in_dim.31), calls=%async_computation.3 | async-start | bytes 32768 | tf_op jit(solution)/shard_map/all_to_all | solution.py:26
  147.0 93.6 %all-to-all-start.2 = ((bf16[32,256,96]{1,2,0:T(8,128)(2,1)}), bf16[32,256,96]{1,2,0:T(8,128)(2,1)S(1)}, u32[]{:S(2)}, u32[]{:S(2)}) async-start(bf16[32,256,96]{1,2,0:T(8,128)(2,1)} %bitcast.170), calls=%async_computation.2 | async-start | bytes 3145728 | tf_op jit(solution)/shard_map/all_to_all | solution.py:126
  151.3 168.3 %reduce-scatter.5.cloned.1.call-start = ((), (), s32[]{:S(2)}) async-start(), calls=%async_computation.12 | async-start | bytes 2088960 | tf_op jit(solution)/shard_map/reduce_scatter | solution.py:34
  171.2 73.8 %copy-start.12 = (f32[320,192]{0,1:T(8,128)}, f32[320,192]{0,1:T(8,128)S(1)}, u32[]{:S(2)}) copy-start(f32[320,192]{0,1:T(8,128)S(1)} %fusion.1) | copy-start | bytes 737284
  250.0 143.6 %reduce-scatter.3.cloned.1.call-start = ((), (), s32[]{:S(2)}) async-start(), calls=%async_computation.11 | async-start | bytes 2088960 | tf_op jit(solution)/shard_map/reduce_scatter | solution.py:34
  254.3 66.3 %copy-start.5 = (bf16[32,20,96]{2,1,0:T(8,128)(2,1)S(1)}, bf16[32,20,96]{2,1,0:T(8,128)(2,1)}, u32[]{:S(2)}) copy-start(bf16[32,20,96]{2,1,0:T(8,128)(2,1)} %copy-done.4) | copy-start | bytes 368644
  254.3 85.7 %copy-start.39 = (f32[128]{0:T(128)S(1)}, f32[128]{0:T(128)}, u32[]{:S(2)}) copy-start(f32[128]{0:T(128)} %reduce_sum.89) | copy-start | bytes 1540
  321.0 28.1 %copy-start.26 = (bf16[128,96]{0,1:T(8,128)(2,1)S(1)}, bf16[128,96]{0,1:T(8,128)(2,1)}, u32[]{:S(2)}) copy-start(bf16[128,96]{0,1:T(8,128)(2,1)} %copy-done.25) | copy-start | bytes 73732
  321.0 28.1 %copy-start.41 = (f32[96]{0:T(128)S(1)}, f32[96]{0:T(128)}, u32[]{:S(2)}) copy-start(f32[96]{0:T(128)} %dynamic_slice.3) | copy-start | bytes 1156
  321.9 26.4 %all-to-all-start.5 = ((bf16[20,32,98]{2,0,1:T(8,128)(2,1)}), bf16[20,32,98]{2,0,1:T(8,128)(2,1)S(1)}, u32[]{:S(2)}, u32[]{:S(2)}) async-start(bf16[20,32,98]{2,0,1:T(8,128)(2,1)} %copy.203), calls=%async_computation.7 | async-start | bytes 393216 | tf_op jit(solution)/shard_map/all_to_all | solution.py:161
  349.1 45.5 %copy-start.2 = (bf16[32,256,96]{1,2,0:T(8,128)(2,1)S(1)}, bf16[32,256,96]{1,2,0:T(8,128)(2,1)}, u32[]{:S(2)}) copy-start(bf16[32,256,96]{1,2,0:T(8,128)(2,1)} %copy-done.1) | copy-start | bytes 4718596
  350.3 44.3 %copy-start.28 = (bf16[128,96]{0,1:T(8,128)(2,1)}, bf16[128,96]{0,1:T(8,128)(2,1)S(1)}, u32[]{:S(2)}) copy-start(bf16[128,96]{0,1:T(8,128)(2,1)S(1)} %fusion.25) | copy-start | bytes 73732
  351.3 43.3 %all-to-all-start.6 = ((bf16[32,128,96]{1,2,0:T(8,128)(2,1)}), bf16[32,128,96]{1,2,0:T(8,128)(2,1)}, u32[]{:S(2)}, u32[]{:S(2)}) async-start(bf16[32,128,96]{1,2,0:T(8,128)(2,1)} %broadcast_in_dim.33), calls=%async_computation.8 | async-start | bytes 1572864 | tf_op jit(solution)/shard_map/all_to_all | solution.py:26
  355.7 40.8 %copy-start.10 = (f32[128,2,128]{0,2,1:T(8,128)S(1)}, f32[128,2,128]{0,2,1:T(8,128)}, u32[]{:S(2)}) copy-start(f32[128,2,128]{0,2,1:T(8,128)} %copy-done.9) | copy-start | bytes 393220
  355.7 40.9 %copy-start.38 = (f32[128,2]{0,1:T(2,128)S(1)}, f32[128,2]{0,1:T(2,128)}, u32[]{:S(2)}) copy-start(f32[128,2]{0,1:T(2,128)} %copy-done.37) | copy-start | bytes 3076
  355.8 40.9 %copy-start.36 = (f32[128,2]{0,1:T(2,128)S(1)}, f32[128,2]{0,1:T(2,128)}, u32[]{:S(2)}) copy-start(f32[128,2]{0,1:T(2,128)} %copy-done.35) | copy-start | bytes 3076
  396.5 19.5 %copy-start.18 = (bf16[128,256]{0,1:T(8,128)(2,1)S(1)}, bf16[128,256]{0,1:T(8,128)(2,1)}, u32[]{:S(2)}) copy-start(bf16[128,256]{0,1:T(8,128)(2,1)} %copy-done.17) | copy-start | bytes 196612
  396.5 22.4 %copy-start.15 = (f32[2,128,128]{2,1,0:T(8,128)S(1)}, f32[2,128,128]{2,1,0:T(8,128)}, u32[]{:S(2)}) copy-start(f32[2,128,128]{2,1,0:T(8,128)} %copy-done.14) | copy-start | bytes 393220
  397.0 42.0 %copy-start.24 = (bf16[2,128,128]{2,1,0:T(8,128)(2,1)S(1)}, bf16[2,128,128]{2,1,0:T(8,128)(2,1)}, u32[]{:S(2)}) copy-start(bf16[2,128,128]{2,1,0:T(8,128)(2,1)} %copy-done.23) | copy-start | bytes 196612
  397.4 61.9 %copy-start.7 = (f32[128,32,20]{0,1,2:T(8,128)S(1)}, f32[128,32,20]{0,1,2:T(8,128)}, u32[]{:S(2)}) copy-start(f32[128,32,20]{0,1,2:T(8,128)} %copy-done.6) | copy-start | bytes 983044
  398.1 61.1 %all-to-all-start.7 = ((bf16[20,32,96]{2,0,1:T(8,128)(2,1)}), bf16[20,32,96]{2,0,1:T(8,128)(2,1)S(1)}, u32[]{:S(2)}, u32[]{:S(2)}) async-start(bf16[20,32,96]{2,0,1:T(8,128)(2,1)} %copy.207), calls=%async_computation.9 | async-start | bytes 393216 | tf_op jit(solution)/shard_map/all_to_all | solution.py:182
  416.1 6.7 %collective-permute-start.4 = (f32[2,128,128]{2,1,0:T(8,128)S(1)}, f32[2,128,128]{2,1,0:T(8,128)S(1)}, u32[]{:S(2)}, u32[]{:S(2)}) collective-permute-start(f32[2,128,128]{2,1,0:T(8,128)S(1)} %convolution_bitcast_fusion.4), channel_id=1, source_target_pairs={{0,32},{32,0},{64,96},{96,64},{128,160},{160,128},{192,224},{224,1... | collective-permute-start | bytes 393224 | tf_op jit(solution)/shard_map/ppermute | solution.py:14
  422.9 10.4 %collective-permute-start.5 = (f32[2,128,128]{2,1,0:T(8,128)S(1)}, f32[2,128,128]{2,1,0:T(8,128)S(1)}, u32[]{:S(2)}, u32[]{:S(2)}) collective-permute-start(f32[2,128,128]{2,1,0:T(8,128)S(1)} %add.140), channel_id=1, source_target_pairs={{0,64},{32,96},{64,0},{96,32},{128,192},{160,224},{192,128},{224,1... | collective-permute-start | bytes 393224 | tf_op jit(solution)/shard_map/ppermute | solution.py:14
  427.0 48.7 %copy-start.22 = (bf16[128,256]{1,0:T(8,128)(2,1)S(1)}, bf16[128,256]{1,0:T(8,128)(2,1)}, u32[]{:S(2)}) copy-start(bf16[128,256]{1,0:T(8,128)(2,1)} %param.16) | copy-start | bytes 196612
  433.3 18.6 %collective-permute-start.6 = (f32[2,128,128]{2,1,0:T(8,128)S(1)}, f32[2,128,128]{2,1,0:T(8,128)S(1)}, u32[]{:S(2)}, u32[]{:S(2)}) collective-permute-start(f32[2,128,128]{2,1,0:T(8,128)S(1)} %add.142), channel_id=1, source_target_pairs={{0,128},{32,160},{64,192},{96,224},{128,0},{160,32},{192,64},{224,... | collective-permute-start | bytes 393224 | tf_op jit(solution)/shard_map/ppermute | solution.py:14
  452.0 22.0 %collective-permute-start.7 = (f32[2,128,128]{2,1,0:T(8,128)S(1)}, f32[2,128,128]{2,1,0:T(8,128)S(1)}, u32[]{:S(2)}, u32[]{:S(2)}) collective-permute-start(f32[2,128,128]{2,1,0:T(8,128)S(1)} %add.144), channel_id=1, source_target_pairs={{0,256},{32,288},{64,320},{96,352},{128,384},{160,416},{192,448},{... | collective-permute-start | bytes 393224 | tf_op jit(solution)/shard_map/ppermute | solution.py:14
  (15 other events, 35.3 us)
Sparse Core Ops, SparseCore 0:
  10.1 84.0 all-gather.5
  96.2 68.1 all-gather.9
  166.5 70.0 all-gather.7
  250.1 69.3 reduce-scatter.4
  322.2 71.3 reduce-scatter.2

commit v5 on v4

--- a/solution.py
+++ b/solution.py
@@ -4,7 +4,7 @@
 from jax.sharding import PartitionSpec as P
 
 
-def butterfly_sums(value, axis, backward):
+def butterfly_sums(value, axis, backward, ride=None):
     count = lax.axis_size(axis)
     place = lax.axis_index(axis)
     total = value
@@ -12,11 +12,15 @@
     step = 1
     while step < count:
         other = lax.ppermute(total, axis, [(i, i ^ step) for i in range(count)])
+        if ride is not None and step == 1:
+            other, ride = lax.optimization_barrier((other, ride))
         upper = (place & step) != 0
         take = jnp.logical_not(upper) if backward else upper
         carried = carried + jnp.where(take, other, jnp.zeros_like(other))
         total = total + other
         step *= 2
+    if ride is not None:
+        return carried, total, ride
     return carried, total
 
 
@@ -178,11 +182,10 @@
         jnp.bfloat16
     )
     state_part = jnp.einsum("thd,the->hde", query3, grad_attended, preferred_element_type=f32)
-    half_out, state_part = lax.optimization_barrier((half_out, state_part))
+    later_sum, state_total, half_out = butterfly_sums(state_part, "ctx", True, half_out)
     returned = lax.all_to_all(half_out, "ep", split_axis=1, concat_axis=0, tiled=True)
     expert_mix = jnp.dot(dest_weights, returned.astype(f32), precision=high)
     layer_out = (stream_f + expert_mix).astype(jnp.bfloat16)
-    later_sum, state_total = butterfly_sums(state_part, "ctx", True)
     grad_scores = jnp.einsum("the,she->hts", grad_attended, value3, preferred_element_type=f32)
     grad_masked = jnp.where(causal[None], grad_scores, 0.0).astype(jnp.bfloat16)
     grad_att_f = grad_attended.astype(f32)

time: 485 us -> 480 us (0.990)
    ppermute x8, waiting for transfers between devices: 54.4 us -> 48.2 us  [butterfly_sums(): other = lax.ppermute(total, axis, [(i, i ^ step) for i in range(count)])]
    unnamed x91 -> x93, local copies, waits for them, and re-layouts: 9.82 us -> 9.94 us
  transfers between devices with their start and end apart: 20 -> 20, of which waited for: 13 -> 12; matrix products, arithmetic and copies ran while one was open for 9% -> 9% of each run, Pallas kernels for 0% -> 0%
where the time goes in v5:
time: 480 us; the launch traced here: 479 us
  waiting for transfers between devices  272 us (57%)
  starting transfers between devices  117 us (24%)
  local copies, waits for them, and re-layouts  32.4 us (7%)
  matrix products  23.1 us (5%)
  between operations  14.8 us (3%)
  blocking collectives  12.8 us (3%)
  other arithmetic  6.78 us (1%)
    reduce_scatter x2, waiting for transfers between devices, scatter_sum(): part = lax.psum_scatter(dense, axis, scatter_dimension=0, tiled=True)  102 us
    all_gather x1, waiting for transfers between devices, local(): portion = lax.all_gather(expert_in, 'ctx', axis=0, tiled=True)  65.6 us
    ppermute x8, starting transfers between devices, butterfly_sums(): other = lax.ppermute(total, axis, [(i, i ^ step) for i in range(count)])  49.7 us
    ppermute x8, waiting for transfers between devices, butterfly_sums(): other = lax.ppermute(total, axis, [(i, i ^ step) for i in range(count)])  48.2 us
    all_to_all x3, waiting for transfers between devices, gather_blocks(): return lax.all_to_all(spread, axis, 0, 0, tiled=True)  32.9 us
    all_to_all x1, starting transfers between devices, local(): lax.all_to_all(half_out, 'ep', split_axis=1, concat_axis=0, tiled=True)  18.8 us
    all_to_all x1, starting transfers between devices, local(): lax.all_to_all(payload, 'ep', split_axis=1, concat_axis=0, tiled=True)  18.1 us
    all_to_all x3, starting transfers between devices, gather_blocks(): return lax.all_to_all(spread, axis, 0, 0, tiled=True)  17.4 us
  transfers between devices with their start and end apart: 20, of which 12 were waited for; matrix products, arithmetic and copies ran while one was open for 9% of the time, Pallas kernels for 0%

profile of v5, /device:TPU:1, one launch (start us, length us, event | category | flops | bytes accessed | tf_op | source)
XLA Modules:
  0.0 478.8 jit_solution(11159334952579096498)
XLA Ops:
  8.9 1.0 fusion.47
  9.9 4.4 collective-permute-start
  17.7 5.0 %collective-permute-start.1 = (f32[2,128,128]{2,1,0:T(8,128)S(1)}, f32[2,128,128]{2,1,0:T(8,128)S(1)}, u32[]{:S(2)}, u32[]{:S(2)}) collective-permute-start(f32[2,128,128]{2,1,0:T(8,128)S(1)} %add.118), channel_id=1, source_target_pairs={{0,64},{32,96},{64,0},{96,32},{128,192},{160,224},{192,128},{224,1... | collective-permute-start | bytes 393224 | tf_op jit(solution)/shard_map/ppermute | solution.py:14
  24.0 8.5 %all-to-all-start.4 = ((bf16[32,20,96]{2,1,0:T(8,128)(2,1)}), bf16[32,20,96]{2,1,0:T(8,128)(2,1)S(1)}, u32[]{:S(2)}, u32[]{:S(2)}) async-start(bf16[32,20,96]{2,1,0:T(8,128)(2,1)} %all_to_all.56), calls=%async_computation.4 | async-start | bytes 393216 | tf_op jit(solution)/shard_map/all_to_all | solution.py:145
  32.8 8.8 %collective-permute-start.2 = (f32[2,128,128]{2,1,0:T(8,128)S(1)}, f32[2,128,128]{2,1,0:T(8,128)S(1)}, u32[]{:S(2)}, u32[]{:S(2)}) collective-permute-start(f32[2,128,128]{2,1,0:T(8,128)S(1)} %add.120), channel_id=1, source_target_pairs={{0,128},{32,160},{64,192},{96,224},{128,0},{160,32},{192,64},{224,... | collective-permute-start | bytes 393224 | tf_op jit(solution)/shard_map/ppermute | solution.py:14
  41.8 14.2 %collective-permute-done.2 = f32[2,128,128]{2,1,0:T(8,128)S(1)} collective-permute-done((f32[2,128,128]{2,1,0:T(8,128)S(1)}, f32[2,128,128]{2,1,0:T(8,128)S(1)}, u32[]{:S(2)}, u32[]{:S(2)}) %collective-permute-start.2) | collective-permute-done | bytes 131104 | tf_op jit(solution)/shard_map/ppermute | solution.py:14
  56.1 11.0 %collective-permute-start.3 = (f32[2,128,128]{2,1,0:T(8,128)S(1)}, f32[2,128,128]{2,1,0:T(8,128)S(1)}, u32[]{:S(2)}, u32[]{:S(2)}) collective-permute-start(f32[2,128,128]{2,1,0:T(8,128)S(1)} %add.122), channel_id=1, source_target_pairs={{0,256},{32,288},{64,320},{96,352},{128,384},{160,416},{192,448},{... | collective-permute-start | bytes 393224 | tf_op jit(solution)/shard_map/ppermute | solution.py:14
  67.3 4.3 collective-permute-done.3
  72.9 1.6 broadcast_in_dim.30
  74.5 9.2 %all-to-all-start = ((bf16[32,128,256]{2,1,0:T(8,128)(2,1)}), bf16[32,128,256]{2,1,0:T(8,128)(2,1)}, u32[]{:S(2)}, u32[]{:S(2)}) async-start(bf16[32,128,256]{2,1,0:T(8,128)(2,1)} %broadcast_in_dim.30), calls=%async_computation | async-start | bytes 4194304 | tf_op jit(solution)/shard_map/all_to_all | solution.py:30
  85.0 27.4 %all-to-all-done = bf16[32,128,256]{2,1,0:T(8,128)(2,1)} async-done(((bf16[32,128,256]{2,1,0:T(8,128)(2,1)}), bf16[32,128,256]{2,1,0:T(8,128)(2,1)}, u32[]{:S(2)}, u32[]{:S(2)}) %all-to-all-start) | async-done | bytes 2097184 | tf_op jit(solution)/shard_map/all_to_all | solution.py:30
  112.4 3.4 fusion.51
  116.8 12.8 %all_to_all.75 = bf16[32,20,96]{2,1,0:T(8,128)(2,1)S(1)} all-to-all(bf16[32,20,96]{2,1,0:T(8,128)(2,1)S(1)} %reshape.178), channel_id=1, replica_groups=mesh['ctx'=16,'ep'=32] {'ep'}, dimensions={0} | all-to-all | bytes 245760 | tf_op jit(solution)/shard_map/all_to_all | solution.py:120
  130.5 1.9 reshape.189
  132.5 1.7 fusion.37
  134.9 3.8 all-to-all-start.3
  138.7 1.4 copy.265
  140.2 5.4 %all-to-all-done.3 = f32[32,128,1]{1,2,0:T(1,128)S(1)} async-done(((f32[32,128,1]{1,2,0:T(1,128)}), f32[32,128,1]{1,2,0:T(1,128)S(1)}, u32[]{:S(2)}, u32[]{:S(2)}) %all-to-all-start.3) | async-done | bytes 16416 | tf_op jit(solution)/shard_map/all_to_all | solution.py:30
  145.6 4.3 all-to-all-start.2
  150.5 13.8 %all-gather.10.cloned.1.call-done = bf16[16,20,3072]{2,1,0:T(8,128)(2,1)} async-done(((bf16[1,20,3072]{2,1,0:T(8,128)(2,1)}), bf16[16,20,3072]{2,1,0:T(8,128)(2,1)}) %all-gather.10.cloned.1.call-update) | async-done | bytes 1966096 | tf_op jit(solution)/shard_map/all_gather | solution.py:146
  164.3 4.0 reshape.193
  168.3 2.8 fusion.9
  171.1 65.6 %all-gather.8.cloned.1.call-done = bf16[16,20,3072]{2,1,0:T(8,128)(2,1)} async-done(((bf16[1,20,3072]{2,1,0:T(8,128)(2,1)}), bf16[16,20,3072]{2,1,0:T(8,128)(2,1)}) %all-gather.8.cloned.1.call-update) | async-done | bytes 1966096 | tf_op jit(solution)/shard_map/all_gather | solution.py:131
  236.6 4.0 reshape.191
  240.6 3.1 fusion.3
  246.2 1.7 fusion
  247.9 1.9 reshape.180
  250.0 2.2 convolution_convert_fusion
  252.2 1.9 reshape.184
  254.9 64.5 %reduce-scatter.3.cloned.1.call-done = bf16[1,480,128]{2,1,0:T(8,128)(2,1)} async-done(((bf16[16,480,128]{2,1,0:T(8,128)(2,1)}), bf16[1,480,128]{2,1,0:T(8,128)(2,1)}) %reduce-scatter.3.cloned.1.call-update) | async-done | bytes 122896 | tf_op jit(solution)/shard_map/reduce_scatter | solution.py:38
  319.3 1.1 reshape_reshape.3
  321.7 18.1 %all-to-all-start.5 = ((bf16[20,32,98]{2,0,1:T(8,128)(2,1)}), bf16[20,32,98]{2,0,1:T(8,128)(2,1)S(1)}, u32[]{:S(2)}, u32[]{:S(2)}) async-start(bf16[20,32,98]{2,0,1:T(8,128)(2,1)} %copy.203), calls=%async_computation.6 | async-start | bytes 393216 | tf_op jit(solution)/shard_map/all_to_all | solution.py:165
  339.8 8.2 %all-to-all-done.5 = bf16[20,32,98]{2,0,1:T(8,128)(2,1)S(1)} async-done(((bf16[20,32,98]{2,0,1:T(8,128)(2,1)}), bf16[20,32,98]{2,0,1:T(8,128)(2,1)S(1)}, u32[]{:S(2)}, u32[]{:S(2)}) %all-to-all-start.5) | async-done | bytes 125472 | tf_op jit(solution)/shard_map/all_to_all | solution.py:165
  348.8 1.2 fusion.25
  350.0 1.0 broadcast_in_dim.33
  351.0 4.4 all-to-all-start.6
  355.5 37.9 %reduce-scatter.5.cloned.1.call-done = bf16[1,480,128]{2,1,0:T(8,128)(2,1)} async-done(((bf16[16,480,128]{2,1,0:T(8,128)(2,1)}), bf16[1,480,128]{2,1,0:T(8,128)(2,1)}) %reduce-scatter.5.cloned.1.call-update) | async-done | bytes 122896 | tf_op jit(solution)/shard_map/reduce_scatter | solution.py:38
  393.4 1.0 reshape.185
  394.5 1.9 fusion.66
  397.1 2.8 collective-permute-start.4
  401.1 2.0 collective-permute-done.4
  403.1 3.4 collective-permute-start.5
  407.7 18.8 %all-to-all-start.7 = ((bf16[20,32,96]{2,0,1:T(8,128)(2,1)}), bf16[20,32,96]{2,0,1:T(8,128)(2,1)S(1)}, u32[]{:S(2)}, u32[]{:S(2)}) async-start(bf16[20,32,96]{2,0,1:T(8,128)(2,1)} %copy.207), calls=%async_computation.9 | async-start | bytes 393216 | tf_op jit(solution)/shard_map/all_to_all | solution.py:186
  426.5 6.2 %collective-permute-start.6 = (f32[2,128,128]{2,1,0:T(8,128)S(1)}, f32[2,128,128]{2,1,0:T(8,128)S(1)}, u32[]{:S(2)}, u32[]{:S(2)}) collective-permute-start(f32[2,128,128]{2,1,0:T(8,128)S(1)} %add.142), channel_id=1, source_target_pairs={{0,128},{32,160},{64,192},{96,224},{128,0},{160,32},{192,64},{224,... | collective-permute-start | bytes 393224 | tf_op jit(solution)/shard_map/ppermute | solution.py:14
  432.9 12.7 %collective-permute-done.6 = f32[2,128,128]{2,1,0:T(8,128)S(1)} collective-permute-done((f32[2,128,128]{2,1,0:T(8,128)S(1)}, f32[2,128,128]{2,1,0:T(8,128)S(1)}, u32[]{:S(2)}, u32[]{:S(2)}) %collective-permute-start.6) | collective-permute-done | bytes 131104 | tf_op jit(solution)/shard_map/ppermute | solution.py:14
  445.7 8.0 %collective-permute-start.7 = (f32[2,128,128]{2,1,0:T(8,128)S(1)}, f32[2,128,128]{2,1,0:T(8,128)S(1)}, u32[]{:S(2)}, u32[]{:S(2)}) collective-permute-start(f32[2,128,128]{2,1,0:T(8,128)S(1)} %add.144), channel_id=1, source_target_pairs={{0,256},{32,288},{64,320},{96,352},{128,384},{160,416},{192,448},{... | collective-permute-start | bytes 393224 | tf_op jit(solution)/shard_map/ppermute | solution.py:14
  453.7 1.0 fusion.26
  454.6 14.9 %collective-permute-done.7 = f32[2,128,128]{2,1,0:T(8,128)S(1)} collective-permute-done((f32[2,128,128]{2,1,0:T(8,128)S(1)}, f32[2,128,128]{2,1,0:T(8,128)S(1)}, u32[]{:S(2)}, u32[]{:S(2)}) %collective-permute-start.7) | collective-permute-done | bytes 131104 | tf_op jit(solution)/shard_map/ppermute | solution.py:14
  (179 shorter events, 23.8 us)
Async XLA Ops:
  7.2 233.4 %copy-start = (bf16[1,192,3072]{2,1,0:T(8,128)(2,1)S(1)}, bf16[1,192,3072]{2,1,0:T(8,128)(2,1)}, u32[]{:S(2)}) copy-start(bf16[1,192,3072]{2,1,0:T(8,128)(2,1)} %param.26) | copy-start | bytes 3538948
  7.2 15.6 %copy-start.30 = (bf16[128,96]{0,1:T(8,128)(2,1)S(1)}, bf16[128,96]{0,1:T(8,128)(2,1)}, u32[]{:S(2)}) copy-start(bf16[128,96]{0,1:T(8,128)(2,1)} %param.29) | copy-start | bytes 73732
  7.2 105.2 %all-gather.6.cloned.1.call-start = ((), (), s32[]{:S(2)}) async-start(), calls=%async_computation.10 | async-start | bytes 1671168 | tf_op jit(solution)/shard_map/all_gather | solution.py:81
  8.9 7.8 %copy-start.17 = (bf16[128,256]{0,1:T(8,128)(2,1)}, bf16[128,256]{0,1:T(8,128)(2,1)S(1)}, u32[]{:S(2)}) copy-start(bf16[128,256]{0,1:T(8,128)(2,1)S(1)} %copy.262) | copy-start | bytes 196612
  9.9 7.8 %collective-permute-start = (f32[2,128,128]{2,1,0:T(8,128)S(1)}, f32[2,128,128]{2,1,0:T(8,128)S(1)}, u32[]{:S(2)}, u32[]{:S(2)}) collective-permute-start(f32[2,128,128]{2,1,0:T(8,128)S(1)} %fusion.47), channel_id=1, source_target_pairs={{0,32},{32,0},{64,96},{96,64},{128,160},{160,128},{192,224},{224,1... | collective-permute-start | bytes 393224 | tf_op jit(solution)/shard_map/ppermute | solution.py:14
  17.4 15.2 %copy-start.31 = (bf16[128,256]{1,0:T(8,128)(2,1)S(1)}, bf16[128,256]{1,0:T(8,128)(2,1)}, u32[]{:S(2)}) copy-start(bf16[128,256]{1,0:T(8,128)(2,1)} %param.15) | copy-start | bytes 196612
  17.6 24.0 %copy-start.22 = (bf16[128,256]{1,0:T(8,128)(2,1)S(1)}, bf16[128,256]{1,0:T(8,128)(2,1)}, u32[]{:S(2)}) copy-start(bf16[128,256]{1,0:T(8,128)(2,1)} %param.16) | copy-start | bytes 196612
  17.6 49.5 %copy-start.19 = (bf16[128,256]{1,0:T(8,128)(2,1)S(1)}, bf16[128,256]{1,0:T(8,128)(2,1)}, u32[]{:S(2)}) copy-start(bf16[128,256]{1,0:T(8,128)(2,1)} %param.17) | copy-start | bytes 196612
  17.7 53.9 %copy-start.28 = (f32[2,128,128]{2,1,0:T(8,128)S(1)}, f32[2,128,128]{2,1,0:T(8,128)}, u32[]{:S(2)}) copy-start(f32[2,128,128]{2,1,0:T(8,128)} %param.18) | copy-start | bytes 393220
  17.7 15.0 %collective-permute-start.1 = (f32[2,128,128]{2,1,0:T(8,128)S(1)}, f32[2,128,128]{2,1,0:T(8,128)S(1)}, u32[]{:S(2)}, u32[]{:S(2)}) collective-permute-start(f32[2,128,128]{2,1,0:T(8,128)S(1)} %add.118), channel_id=1, source_target_pairs={{0,64},{32,96},{64,0},{96,32},{128,192},{160,224},{192,128},{224,1... | collective-permute-start | bytes 393224 | tf_op jit(solution)/shard_map/ppermute | solution.py:14
  24.0 48.6 %copy-start.35 = (f32[256]{0:T(256)S(1)}, f32[256]{0:T(256)}, u32[]{:S(2)}) copy-start(f32[256]{0:T(256)} %param.19) | copy-start | bytes 3076
  24.0 48.9 %all-to-all-start.4 = ((bf16[32,20,96]{2,1,0:T(8,128)(2,1)}), bf16[32,20,96]{2,1,0:T(8,128)(2,1)S(1)}, u32[]{:S(2)}, u32[]{:S(2)}) async-start(bf16[32,20,96]{2,1,0:T(8,128)(2,1)} %all_to_all.56), calls=%async_computation.4 | async-start | bytes 393216 | tf_op jit(solution)/shard_map/all_to_all | solution.py:145
  32.7 41.8 %copy-start.33 = (pred[128,128]{1,0:T(8,128)(4,1)}, pred[128,128]{1,0:T(8,128)(4,1)S(1)}, u32[]{:S(2)}) copy-start(pred[128,128]{1,0:T(8,128)(4,1)S(1)} %iota_compare_fusion) | copy-start | bytes 49156
  32.8 23.3 %collective-permute-start.2 = (f32[2,128,128]{2,1,0:T(8,128)S(1)}, f32[2,128,128]{2,1,0:T(8,128)S(1)}, u32[]{:S(2)}, u32[]{:S(2)}) collective-permute-start(f32[2,128,128]{2,1,0:T(8,128)S(1)} %add.120), channel_id=1, source_target_pairs={{0,128},{32,160},{64,192},{96,224},{128,0},{160,32},{192,64},{224,... | collective-permute-start | bytes 393224 | tf_op jit(solution)/shard_map/ppermute | solution.py:14
  41.8 32.7 %copy-start.24 = (bf16[2,128,128]{2,1,0:T(8,128)(2,1)}, bf16[2,128,128]{2,1,0:T(8,128)(2,1)S(1)}, u32[]{:S(2)}) copy-start(bf16[2,128,128]{2,1,0:T(8,128)(2,1)S(1)} %fusion.14) | copy-start | bytes 196612
  56.1 15.5 %collective-permute-start.3 = (f32[2,128,128]{2,1,0:T(8,128)S(1)}, f32[2,128,128]{2,1,0:T(8,128)S(1)}, u32[]{:S(2)}, u32[]{:S(2)}) collective-permute-start(f32[2,128,128]{2,1,0:T(8,128)S(1)} %add.122), channel_id=1, source_target_pairs={{0,256},{32,288},{64,320},{96,352},{128,384},{160,416},{192,448},{... | collective-permute-start | bytes 393224 | tf_op jit(solution)/shard_map/ppermute | solution.py:14
  74.5 37.9 %all-to-all-start = ((bf16[32,128,256]{2,1,0:T(8,128)(2,1)}), bf16[32,128,256]{2,1,0:T(8,128)(2,1)}, u32[]{:S(2)}, u32[]{:S(2)}) async-start(bf16[32,128,256]{2,1,0:T(8,128)(2,1)} %broadcast_in_dim.30), calls=%async_computation | async-start | bytes 4194304 | tf_op jit(solution)/shard_map/all_to_all | solution.py:30
  83.7 28.7 %copy-start.43 = (bf16[128,96]{0,1:T(8,128)(2,1)S(1)}, bf16[128,96]{0,1:T(8,128)(2,1)}, u32[]{:S(2)}) copy-start(bf16[128,96]{0,1:T(8,128)(2,1)} %param.21) | copy-start | bytes 73732
  83.7 80.6 %all-gather.10.cloned.1.call-start = ((), (), s32[]{:S(2)}) async-start(), calls=%async_computation.14 | async-start | bytes 2506752 | tf_op jit(solution)/shard_map/all_gather | solution.py:146
  84.7 152.0 %all-gather.8.cloned.1.call-start = ((), (), s32[]{:S(2)}) async-start(), calls=%async_computation.13 | async-start | bytes 2506752 | tf_op jit(solution)/shard_map/all_gather | solution.py:131
  116.6 16.0 %copy-start.32 = (f32[3072]{0:T(1024)S(1)}, f32[3072]{0:T(1024)}, u32[]{:S(2)}) copy-start(f32[3072]{0:T(1024)} %param.22) | copy-start | bytes 36868
  116.8 21.9 %copy-start.13 = (bf16[8192,96]{0,1:T(8,128)(2,1)S(1)}, bf16[8192,96]{0,1:T(8,128)(2,1)}, u32[]{:S(2)}) copy-start(bf16[8192,96]{0,1:T(8,128)(2,1)} %all-gather.6.cloned.1.call-done) | copy-start | bytes 4718596
  129.6 10.6 %copy-start.4 = (bf16[32,20,96]{2,1,0:T(8,128)(2,1)}, bf16[32,20,96]{2,1,0:T(8,128)(2,1)S(1)}, u32[]{:S(2)}) copy-start(bf16[32,20,96]{2,1,0:T(8,128)(2,1)S(1)} %all_to_all.75) | copy-start | bytes 368644
  134.9 10.7 %all-to-all-start.3 = ((f32[32,128,1]{1,2,0:T(1,128)}), f32[32,128,1]{1,2,0:T(1,128)S(1)}, u32[]{:S(2)}, u32[]{:S(2)}) async-start(f32[32,128,1]{1,2,0:T(1,128)} %broadcast_in_dim.31), calls=%async_computation.3 | async-start | bytes 32768 | tf_op jit(solution)/shard_map/all_to_all | solution.py:30
  145.6 95.0 %all-to-all-start.2 = ((bf16[32,256,96]{1,2,0:T(8,128)(2,1)}), bf16[32,256,96]{1,2,0:T(8,128)(2,1)S(1)}, u32[]{:S(2)}, u32[]{:S(2)}) async-start(bf16[32,256,96]{1,2,0:T(8,128)(2,1)} %bitcast.170), calls=%async_computation.2 | async-start | bytes 3145728 | tf_op jit(solution)/shard_map/all_to_all | solution.py:130
  149.9 169.4 %reduce-scatter.3.cloned.1.call-start = ((), (), s32[]{:S(2)}) async-start(), calls=%async_computation.11 | async-start | bytes 2088960 | tf_op jit(solution)/shard_map/reduce_scatter | solution.py:38
  171.1 73.6 %copy-start.12 = (f32[320,192]{0,1:T(8,128)}, f32[320,192]{0,1:T(8,128)S(1)}, u32[]{:S(2)}) copy-start(f32[320,192]{0,1:T(8,128)S(1)} %fusion.9) | copy-start | bytes 737284
  249.8 143.6 %reduce-scatter.5.cloned.1.call-start = ((), (), s32[]{:S(2)}) async-start(), calls=%async_computation.12 | async-start | bytes 2088960 | tf_op jit(solution)/shard_map/reduce_scatter | solution.py:38
  254.1 66.3 %copy-start.5 = (bf16[32,20,96]{2,1,0:T(8,128)(2,1)S(1)}, bf16[32,20,96]{2,1,0:T(8,128)(2,1)}, u32[]{:S(2)}) copy-start(bf16[32,20,96]{2,1,0:T(8,128)(2,1)} %copy-done.4) | copy-start | bytes 368644
  254.1 85.7 %copy-start.40 = (f32[128]{0:T(128)S(1)}, f32[128]{0:T(128)}, u32[]{:S(2)}) copy-start(f32[128]{0:T(128)} %reduce_sum.89) | copy-start | bytes 1540
  320.8 28.0 %copy-start.27 = (bf16[128,96]{0,1:T(8,128)(2,1)S(1)}, bf16[128,96]{0,1:T(8,128)(2,1)}, u32[]{:S(2)}) copy-start(bf16[128,96]{0,1:T(8,128)(2,1)} %copy-done.26) | copy-start | bytes 73732
  320.8 28.0 %copy-start.42 = (f32[96]{0:T(128)S(1)}, f32[96]{0:T(128)}, u32[]{:S(2)}) copy-start(f32[96]{0:T(128)} %dynamic_slice.3) | copy-start | bytes 1156
  321.7 26.3 %all-to-all-start.5 = ((bf16[20,32,98]{2,0,1:T(8,128)(2,1)}), bf16[20,32,98]{2,0,1:T(8,128)(2,1)S(1)}, u32[]{:S(2)}, u32[]{:S(2)}) async-start(bf16[20,32,98]{2,0,1:T(8,128)(2,1)} %copy.203), calls=%async_computation.6 | async-start | bytes 393216 | tf_op jit(solution)/shard_map/all_to_all | solution.py:165
  348.8 45.7 %copy-start.2 = (bf16[32,256,96]{1,2,0:T(8,128)(2,1)S(1)}, bf16[32,256,96]{1,2,0:T(8,128)(2,1)}, u32[]{:S(2)}) copy-start(bf16[32,256,96]{1,2,0:T(8,128)(2,1)} %copy-done.1) | copy-start | bytes 4718596
  350.0 46.4 %copy-start.29 = (bf16[128,96]{0,1:T(8,128)(2,1)}, bf16[128,96]{0,1:T(8,128)(2,1)S(1)}, u32[]{:S(2)}) copy-start(bf16[128,96]{0,1:T(8,128)(2,1)S(1)} %fusion.25) | copy-start | bytes 73732
  351.0 43.4 %all-to-all-start.6 = ((bf16[32,128,96]{1,2,0:T(8,128)(2,1)}), bf16[32,128,96]{1,2,0:T(8,128)(2,1)}, u32[]{:S(2)}, u32[]{:S(2)}) async-start(bf16[32,128,96]{1,2,0:T(8,128)(2,1)} %broadcast_in_dim.33), calls=%async_computation.7 | async-start | bytes 1572864 | tf_op jit(solution)/shard_map/all_to_all | solution.py:30
  355.4 41.0 %copy-start.10 = (f32[128,2,128]{0,2,1:T(8,128)S(1)}, f32[128,2,128]{0,2,1:T(8,128)}, u32[]{:S(2)}) copy-start(f32[128,2,128]{0,2,1:T(8,128)} %copy-done.9) | copy-start | bytes 393220
  355.4 41.1 %copy-start.39 = (f32[128,2]{0,1:T(2,128)S(1)}, f32[128,2]{0,1:T(2,128)}, u32[]{:S(2)}) copy-start(f32[128,2]{0,1:T(2,128)} %copy-done.38) | copy-start | bytes 3076
  355.5 41.1 %copy-start.37 = (f32[128,2]{0,1:T(2,128)S(1)}, f32[128,2]{0,1:T(2,128)}, u32[]{:S(2)}) copy-start(f32[128,2]{0,1:T(2,128)} %copy-done.36) | copy-start | bytes 3076
  396.4 10.2 %copy-start.25 = (bf16[2,128,128]{2,1,0:T(8,128)(2,1)S(1)}, bf16[2,128,128]{2,1,0:T(8,128)(2,1)}, u32[]{:S(2)}) copy-start(bf16[2,128,128]{2,1,0:T(8,128)(2,1)} %copy-done.24) | copy-start | bytes 196612
  397.1 6.0 %collective-permute-start.4 = (f32[2,128,128]{2,1,0:T(8,128)S(1)}, f32[2,128,128]{2,1,0:T(8,128)S(1)}, u32[]{:S(2)}, u32[]{:S(2)}) collective-permute-start(f32[2,128,128]{2,1,0:T(8,128)S(1)} %convolution_bitcast_fusion.4), channel_id=1, source_target_pairs={{0,32},{32,0},{64,96},{96,64},{128,160},{160,128},{192,224},{224,1... | collective-permute-start | bytes 393224 | tf_op jit(solution)/shard_map/ppermute | solution.py:14
  400.1 53.6 %copy-start.7 = (f32[128,32,20]{0,1,2:T(8,128)S(1)}, f32[128,32,20]{0,1,2:T(8,128)}, u32[]{:S(2)}) copy-start(f32[128,32,20]{0,1,2:T(8,128)} %copy-done.6) | copy-start | bytes 983044
  403.1 23.4 %collective-permute-start.5 = (f32[2,128,128]{2,1,0:T(8,128)S(1)}, f32[2,128,128]{2,1,0:T(8,128)S(1)}, u32[]{:S(2)}, u32[]{:S(2)}) collective-permute-start(f32[2,128,128]{2,1,0:T(8,128)S(1)} %add.140), channel_id=1, source_target_pairs={{0,64},{32,96},{64,0},{96,32},{128,192},{160,224},{192,128},{224,1... | collective-permute-start | bytes 393224 | tf_op jit(solution)/shard_map/ppermute | solution.py:14
  406.9 63.3 %copy-start.23 = (bf16[128,256]{1,0:T(8,128)(2,1)S(1)}, bf16[128,256]{1,0:T(8,128)(2,1)}, u32[]{:S(2)}) copy-start(bf16[128,256]{1,0:T(8,128)(2,1)} %param.16) | copy-start | bytes 196612
  407.7 46.0 %all-to-all-start.7 = ((bf16[20,32,96]{2,0,1:T(8,128)(2,1)}), bf16[20,32,96]{2,0,1:T(8,128)(2,1)S(1)}, u32[]{:S(2)}, u32[]{:S(2)}) async-start(bf16[20,32,96]{2,0,1:T(8,128)(2,1)} %copy.207), calls=%async_computation.9 | async-start | bytes 393216 | tf_op jit(solution)/shard_map/all_to_all | solution.py:186
  426.5 44.8 %copy-start.21 = (bf16[128,256]{1,0:T(8,128)(2,1)S(1)}, bf16[128,256]{1,0:T(8,128)(2,1)}, u32[]{:S(2)}) copy-start(bf16[128,256]{1,0:T(8,128)(2,1)} %param.17) | copy-start | bytes 196612
  426.5 19.1 %collective-permute-start.6 = (f32[2,128,128]{2,1,0:T(8,128)S(1)}, f32[2,128,128]{2,1,0:T(8,128)S(1)}, u32[]{:S(2)}, u32[]{:S(2)}) collective-permute-start(f32[2,128,128]{2,1,0:T(8,128)S(1)} %add.142), channel_id=1, source_target_pairs={{0,128},{32,160},{64,192},{96,224},{128,0},{160,32},{192,64},{224,... | collective-permute-start | bytes 393224 | tf_op jit(solution)/shard_map/ppermute | solution.py:14
  445.7 23.9 %collective-permute-start.7 = (f32[2,128,128]{2,1,0:T(8,128)S(1)}, f32[2,128,128]{2,1,0:T(8,128)S(1)}, u32[]{:S(2)}, u32[]{:S(2)}) collective-permute-start(f32[2,128,128]{2,1,0:T(8,128)S(1)} %add.144), channel_id=1, source_target_pairs={{0,256},{32,288},{64,320},{96,352},{128,384},{160,416},{192,448},{... | collective-permute-start | bytes 393224 | tf_op jit(solution)/shard_map/ppermute | solution.py:14
  (16 other events, 41.3 us)
Sparse Core Ops, SparseCore 0:
  10.1 84.2 all-gather.5
  96.4 67.8 all-gather.9
  166.4 70.2 all-gather.7
  249.9 69.3 reduce-scatter.2
  322.0 71.3 reduce-scatter.4

commit v6 on v4

--- a/solution.py
+++ b/solution.py
@@ -28,11 +28,12 @@
 
 def scatter_sum(value, axis):
     count = lax.axis_size(axis)
-    rows, width = value.shape
+    parts, rows, width = value.shape
     block = rows // count
-    dense = value.reshape(count, block * width // 128, 128)
+    dense = value.reshape(parts, count, block, width).transpose(1, 0, 2, 3)
+    dense = dense.reshape(count, parts * block * width // 128, 128)
     part = lax.psum_scatter(dense, axis, scatter_dimension=0, tiled=True)
-    return part.reshape(block, width)
+    return part.reshape(parts, block, width)
 
 
 def head_normalize(attended, gain):
@@ -133,9 +134,7 @@
     pre_up = projected[:, hidden_block:]
     gate_sig = jax.nn.sigmoid(pre_gate)
     activated = (pre_gate * gate_sig * pre_up).astype(jnp.bfloat16)
-    half_out = scatter_sum(
-        jnp.dot(activated, w_down, preferred_element_type=f32).astype(jnp.bfloat16), "ctx"
-    )
+    out_terms = jnp.dot(activated, w_down, preferred_element_type=f32).astype(jnp.bfloat16)
     grad_out = out_grad.astype(f32)
     grad_send = jnp.dot(dest_weights.T, grad_out, precision=high).astype(jnp.bfloat16)
     grad_in = lax.all_to_all(grad_send, "ep", split_axis=0, concat_axis=1, tiled=True)
@@ -144,13 +143,13 @@
         jnp.bfloat16
     )
     grad_up_pre = (grad_act * pre_gate * gate_sig).astype(jnp.bfloat16)
-    grad_half = scatter_sum(
-        (
-            jnp.dot(grad_gate_pre, w_gate, preferred_element_type=f32)
-            + jnp.dot(grad_up_pre, w_up, preferred_element_type=f32)
-        ).astype(jnp.bfloat16),
-        "ctx",
-    )
+    grad_terms = (
+        jnp.dot(grad_gate_pre, w_gate, preferred_element_type=f32)
+        + jnp.dot(grad_up_pre, w_up, preferred_element_type=f32)
+    ).astype(jnp.bfloat16)
+    both_halves = scatter_sum(jnp.stack([out_terms, grad_terms]), "ctx")
+    half_out = both_halves[0]
+    grad_half = both_halves[1]
     slot_inner = jnp.sum(slot_rows * model_gain * grad_half.astype(f32), -1, keepdims=True)
     inner_hi = slot_inner.astype(jnp.bfloat16)
     inner_lo = (slot_inner - inner_hi.astype(f32)).astype(jnp.bfloat16)

time: 485 us -> 468 us (0.965)
  waiting for transfers between devices: 276 us -> 256 us
  local copies, waits for them, and re-layouts: 32.3 us -> 44.1 us
  starting transfers between devices: 117 us -> 109 us
    reduce_scatter x2 -> x1, waiting for transfers between devices: 102 us -> 75.8 us  [scatter_sum(): part = lax.psum_scatter(dense, axis, scatter_dimension=0, tiled=True)]
    all_to_all x1, starting transfers between devices: 17.8 us -> 4.45 us  [local(): lax.all_to_all(half_out, 'ep', split_axis=1, concat_axis=0, tiled=True)]
    all_to_all x3, waiting for transfers between devices: 32.9 us -> 45.5 us  [gather_blocks(): return lax.all_to_all(spread, axis, 0, 0, tiled=True)]
    another operation x1 -> x3, local copies, waits for them, and re-layouts: 0.01 us -> 6.22 us  [the longest x2 6.21 us: local(): both_halves = scatter_sum(jnp.stack([out_terms, grad_terms]), 'ctx')]
    ppermute x8, waiting for transfers between devices: 54.4 us -> 49 us  [butterfly_sums(): other = lax.ppermute(total, axis, [(i, i ^ step) for i in range(count)])]
    unnamed x91 -> x107, local copies, waits for them, and re-layouts: 9.82 us -> 9.9 us
  transfers between devices with their start and end apart: 20 -> 19, of which waited for: 13 -> 12; matrix products, arithmetic and copies ran while one was open for 9% -> 7% of each run, Pallas kernels for 0% -> 0%
where the time goes in v6:
time: 468 us; the launch traced here: 467 us
  waiting for transfers between devices  256 us (55%)
  starting transfers between devices  109 us (23%)
  local copies, waits for them, and re-layouts  44.1 us (9%)
  matrix products  21.7 us (5%)
  between operations  14.8 us (3%)
  blocking collectives  12.8 us (3%)
  other arithmetic  8.47 us (2%)
    reduce_scatter x1, waiting for transfers between devices, scatter_sum(): part = lax.psum_scatter(dense, axis, scatter_dimension=0, tiled=True)  75.8 us
    all_gather x1, waiting for transfers between devices, local(): portion = lax.all_gather(expert_in, 'ctx', axis=0, tiled=True)  65 us
    ppermute x8, starting transfers between devices, butterfly_sums(): other = lax.ppermute(total, axis, [(i, i ^ step) for i in range(count)])  51.3 us
    ppermute x8, waiting for transfers between devices, butterfly_sums(): other = lax.ppermute(total, axis, [(i, i ^ step) for i in range(count)])  49 us
    all_to_all x3, waiting for transfers between devices, gather_blocks(): return lax.all_to_all(spread, axis, 0, 0, tiled=True)  45.5 us
    all_to_all x3, starting transfers between devices, gather_blocks(): return lax.all_to_all(spread, axis, 0, 0, tiled=True)  21.6 us
    all_to_all x1, starting transfers between devices, local(): lax.all_to_all(payload, 'ep', split_axis=1, concat_axis=0, tiled=True)  18.4 us
    all_to_all x1, blocking collectives, local(): lax.all_to_all(picked.reshape(ep_count, capacity, columns), 'ep', 0, 0, t...  12.8 us
  transfers between devices with their start and end apart: 19, of which 12 were waited for; matrix products, arithmetic and copies ran while one was open for 7% of the time, Pallas kernels for 0%

profile of v6, /device:TPU:1, one launch (start us, length us, event | category | flops | bytes accessed | tf_op | source)
XLA Modules:
  0.0 466.7 jit_solution(3157847016492347011)
XLA Ops:
  8.9 1.0 fusion.47
  9.9 4.4 collective-permute-start
  17.7 4.9 %collective-permute-start.1 = (f32[2,128,128]{2,1,0:T(8,128)S(1)}, f32[2,128,128]{2,1,0:T(8,128)S(1)}, u32[]{:S(2)}, u32[]{:S(2)}) collective-permute-start(f32[2,128,128]{2,1,0:T(8,128)S(1)} %add.116), channel_id=1, source_target_pairs={{0,64},{32,96},{64,0},{96,32},{128,192},{160,224},{192,128},{224,1... | collective-permute-start | bytes 393224 | tf_op jit(solution)/shard_map/ppermute | solution.py:14
  23.9 8.4 %all-to-all-start.4 = ((bf16[32,20,96]{2,1,0:T(8,128)(2,1)}), bf16[32,20,96]{2,1,0:T(8,128)(2,1)S(1)}, u32[]{:S(2)}, u32[]{:S(2)}) async-start(bf16[32,20,96]{2,1,0:T(8,128)(2,1)} %all_to_all.56), calls=%async_computation.4 | async-start | bytes 393216 | tf_op jit(solution)/shard_map/all_to_all | solution.py:140
  32.5 8.8 %collective-permute-start.2 = (f32[2,128,128]{2,1,0:T(8,128)S(1)}, f32[2,128,128]{2,1,0:T(8,128)S(1)}, u32[]{:S(2)}, u32[]{:S(2)}) collective-permute-start(f32[2,128,128]{2,1,0:T(8,128)S(1)} %add.118), channel_id=1, source_target_pairs={{0,128},{32,160},{64,192},{96,224},{128,0},{160,32},{192,64},{224,... | collective-permute-start | bytes 393224 | tf_op jit(solution)/shard_map/ppermute | solution.py:14
  41.6 14.2 %collective-permute-done.2 = f32[2,128,128]{2,1,0:T(8,128)S(1)} collective-permute-done((f32[2,128,128]{2,1,0:T(8,128)S(1)}, f32[2,128,128]{2,1,0:T(8,128)S(1)}, u32[]{:S(2)}, u32[]{:S(2)}) %collective-permute-start.2) | collective-permute-done | bytes 131104 | tf_op jit(solution)/shard_map/ppermute | solution.py:14
  55.8 11.5 %collective-permute-start.3 = (f32[2,128,128]{2,1,0:T(8,128)S(1)}, f32[2,128,128]{2,1,0:T(8,128)S(1)}, u32[]{:S(2)}, u32[]{:S(2)}) collective-permute-start(f32[2,128,128]{2,1,0:T(8,128)S(1)} %add.120), channel_id=1, source_target_pairs={{0,256},{32,288},{64,320},{96,352},{128,384},{160,416},{192,448},{... | collective-permute-start | bytes 393224 | tf_op jit(solution)/shard_map/ppermute | solution.py:14
  67.5 4.1 collective-permute-done.3
  72.9 1.6 broadcast_in_dim.30
  74.5 14.0 %all-to-all-start = ((bf16[32,128,256]{2,1,0:T(8,128)(2,1)}), bf16[32,128,256]{2,1,0:T(8,128)(2,1)}, u32[]{:S(2)}, u32[]{:S(2)}) async-start(bf16[32,128,256]{2,1,0:T(8,128)(2,1)} %broadcast_in_dim.30), calls=%async_computation | async-start | bytes 4194304 | tf_op jit(solution)/shard_map/all_to_all | solution.py:26
  89.8 27.4 %all-to-all-done = bf16[32,128,256]{2,1,0:T(8,128)(2,1)} async-done(((bf16[32,128,256]{2,1,0:T(8,128)(2,1)}), bf16[32,128,256]{2,1,0:T(8,128)(2,1)}, u32[]{:S(2)}, u32[]{:S(2)}) %all-to-all-start) | async-done | bytes 2097184 | tf_op jit(solution)/shard_map/all_to_all | solution.py:26
  117.2 2.8 fusion.51
  121.1 12.8 %all_to_all.75 = bf16[32,20,96]{2,1,0:T(8,128)(2,1)S(1)} all-to-all(bf16[32,20,96]{2,1,0:T(8,128)(2,1)S(1)} %reshape.182), channel_id=1, replica_groups=mesh['ctx'=16,'ep'=32] {'ep'}, dimensions={0} | all-to-all | bytes 245760 | tf_op jit(solution)/shard_map/all_to_all | solution.py:117
  135.2 1.7 fusion.37
  137.5 3.8 all-to-all-start.3
  141.4 1.4 copy.270
  142.8 5.4 %all-to-all-done.3 = f32[32,128,1]{1,2,0:T(1,128)S(1)} async-done(((f32[32,128,1]{1,2,0:T(1,128)}), f32[32,128,1]{1,2,0:T(1,128)S(1)}, u32[]{:S(2)}, u32[]{:S(2)}) %all-to-all-start.3) | async-done | bytes 16416 | tf_op jit(solution)/shard_map/all_to_all | solution.py:26
  148.2 4.3 all-to-all-start.2
  152.8 11.8 %all-gather.10.cloned.1.call-done = bf16[16,20,3072]{2,1,0:T(8,128)(2,1)} async-done(((bf16[1,20,3072]{2,1,0:T(8,128)(2,1)}), bf16[16,20,3072]{2,1,0:T(8,128)(2,1)}) %all-gather.10.cloned.1.call-update) | async-done | bytes 1966096 | tf_op jit(solution)/shard_map/all_gather | solution.py:141
  164.6 4.0 reshape.195
  168.5 3.2 fusion.1
  171.8 65.0 %all-gather.8.cloned.1.call-done = bf16[16,20,3072]{2,1,0:T(8,128)(2,1)} async-done(((bf16[1,20,3072]{2,1,0:T(8,128)(2,1)}), bf16[16,20,3072]{2,1,0:T(8,128)(2,1)}) %all-gather.8.cloned.1.call-update) | async-done | bytes 1966096 | tf_op jit(solution)/shard_map/all_gather | solution.py:128
  236.7 4.0 reshape.193
  240.7 3.4 fusion.5
  245.8 2.1 stack.9
  248.0 2.3 fusion.7
  250.3 2.0 fusion
  252.3 4.1 stack.10
  256.4 2.2 maximum_bitcast_fusion
  258.6 2.6 copy.205
  261.2 7.6 %reshape.184 = bf16[16,960,128]{2,1,0:T(8,128)(2,1)} reshape(bf16[16,2,20,3072]{3,2,1,0:T(8,128)(2,1)} %copy.205) | data formatting | bytes 7864320 | tf_op jit(solution)/shard_map/reshape | solution.py:34
  269.0 75.8 %reduce-scatter.2.cloned.1.call-done = bf16[1,960,128]{2,1,0:T(8,128)(2,1)} async-done(((bf16[16,960,128]{2,1,0:T(8,128)(2,1)}), bf16[1,960,128]{2,1,0:T(8,128)(2,1)}) %reduce-scatter.2.cloned.1.call-update) | async-done | bytes 245776 | tf_op jit(solution)/shard_map/reduce_scatter | solution.py:35
  344.8 1.6 fusion.65
  347.9 18.4 %all-to-all-start.5 = ((bf16[20,32,98]{2,0,1:T(8,128)(2,1)}), bf16[20,32,98]{2,0,1:T(8,128)(2,1)S(1)}, u32[]{:S(2)}, u32[]{:S(2)}) async-start(bf16[20,32,98]{2,0,1:T(8,128)(2,1)} %copy.208), calls=%async_computation.6 | async-start | bytes 393216 | tf_op jit(solution)/shard_map/all_to_all | solution.py:160
  366.3 8.2 %all-to-all-done.5 = bf16[20,32,98]{2,0,1:T(8,128)(2,1)S(1)} async-done(((bf16[20,32,98]{2,0,1:T(8,128)(2,1)}), bf16[20,32,98]{2,0,1:T(8,128)(2,1)S(1)}, u32[]{:S(2)}, u32[]{:S(2)}) %all-to-all-start.5) | async-done | bytes 125472 | tf_op jit(solution)/shard_map/all_to_all | solution.py:160
  376.3 1.0 broadcast_in_dim.33
  377.3 3.8 all-to-all-start.6
  381.1 1.6 squeeze.16
  382.8 12.6 %all-to-all-done.6 = bf16[32,128,96]{1,2,0:T(8,128)(2,1)S(1)} async-done(((bf16[32,128,96]{1,2,0:T(8,128)(2,1)}), bf16[32,128,96]{1,2,0:T(8,128)(2,1)S(1)}, u32[]{:S(2)}, u32[]{:S(2)}) %all-to-all-start.6) | async-done | bytes 786464 | tf_op jit(solution)/shard_map/all_to_all | solution.py:26
  397.0 2.5 collective-permute-start.4
  401.6 4.4 all-to-all-start.7
  406.1 4.3 collective-permute-start.5
  410.5 6.0 %collective-permute-done.5 = f32[2,128,128]{2,1,0:T(8,128)S(1)} collective-permute-done((f32[2,128,128]{2,1,0:T(8,128)S(1)}, f32[2,128,128]{2,1,0:T(8,128)S(1)}, u32[]{:S(2)}, u32[]{:S(2)}) %collective-permute-start.5) | collective-permute-done | bytes 131104 | tf_op jit(solution)/shard_map/ppermute | solution.py:14
  416.6 6.4 %collective-permute-start.6 = (f32[2,128,128]{2,1,0:T(8,128)S(1)}, f32[2,128,128]{2,1,0:T(8,128)S(1)}, u32[]{:S(2)}, u32[]{:S(2)}) collective-permute-start(f32[2,128,128]{2,1,0:T(8,128)S(1)} %add.140), channel_id=1, source_target_pairs={{0,128},{32,160},{64,192},{96,224},{128,0},{160,32},{192,64},{224,... | collective-permute-start | bytes 393224 | tf_op jit(solution)/shard_map/ppermute | solution.py:14
  423.2 11.4 %collective-permute-done.6 = f32[2,128,128]{2,1,0:T(8,128)S(1)} collective-permute-done((f32[2,128,128]{2,1,0:T(8,128)S(1)}, f32[2,128,128]{2,1,0:T(8,128)S(1)}, u32[]{:S(2)}, u32[]{:S(2)}) %collective-permute-start.6) | collective-permute-done | bytes 131104 | tf_op jit(solution)/shard_map/ppermute | solution.py:14
  434.6 8.6 %collective-permute-start.7 = (f32[2,128,128]{2,1,0:T(8,128)S(1)}, f32[2,128,128]{2,1,0:T(8,128)S(1)}, u32[]{:S(2)}, u32[]{:S(2)}) collective-permute-start(f32[2,128,128]{2,1,0:T(8,128)S(1)} %add.142), channel_id=1, source_target_pairs={{0,256},{32,288},{64,320},{96,352},{128,384},{160,416},{192,448},{... | collective-permute-start | bytes 393224 | tf_op jit(solution)/shard_map/ppermute | solution.py:14
  443.2 1.0 fusion.26
  444.2 13.2 %collective-permute-done.7 = f32[2,128,128]{2,1,0:T(8,128)S(1)} collective-permute-done((f32[2,128,128]{2,1,0:T(8,128)S(1)}, f32[2,128,128]{2,1,0:T(8,128)S(1)}, u32[]{:S(2)}, u32[]{:S(2)}) %collective-permute-start.7) | collective-permute-done | bytes 131104 | tf_op jit(solution)/shard_map/ppermute | solution.py:14
  (194 shorter events, 24.0 us)
Async XLA Ops:
  7.2 161.4 %copy-start = (bf16[1,192,3072]{2,1,0:T(8,128)(2,1)S(1)}, bf16[1,192,3072]{2,1,0:T(8,128)(2,1)}, u32[]{:S(2)}) copy-start(bf16[1,192,3072]{2,1,0:T(8,128)(2,1)} %param.28) | copy-start | bytes 3538948
  7.2 15.4 %copy-start.38 = (bf16[128,96]{0,1:T(8,128)(2,1)S(1)}, bf16[128,96]{0,1:T(8,128)(2,1)}, u32[]{:S(2)}) copy-start(bf16[128,96]{0,1:T(8,128)(2,1)} %param.29) | copy-start | bytes 73732
  7.2 110.0 %all-gather.6.cloned.1.call-start = ((), (), s32[]{:S(2)}) async-start(), calls=%async_computation.9 | async-start | bytes 1671168 | tf_op jit(solution)/shard_map/all_gather | solution.py:78
  8.9 7.8 %copy-start.24 = (bf16[128,256]{0,1:T(8,128)(2,1)}, bf16[128,256]{0,1:T(8,128)(2,1)S(1)}, u32[]{:S(2)}) copy-start(bf16[128,256]{0,1:T(8,128)(2,1)S(1)} %copy.267) | copy-start | bytes 196612
  9.9 7.7 %collective-permute-start = (f32[2,128,128]{2,1,0:T(8,128)S(1)}, f32[2,128,128]{2,1,0:T(8,128)S(1)}, u32[]{:S(2)}, u32[]{:S(2)}) collective-permute-start(f32[2,128,128]{2,1,0:T(8,128)S(1)} %fusion.47), channel_id=1, source_target_pairs={{0,32},{32,0},{64,96},{96,64},{128,160},{160,128},{192,224},{224,1... | collective-permute-start | bytes 393224 | tf_op jit(solution)/shard_map/ppermute | solution.py:14
  15.7 16.6 %copy-start.40 = (bf16[128,256]{1,0:T(8,128)(2,1)S(1)}, bf16[128,256]{1,0:T(8,128)(2,1)}, u32[]{:S(2)}) copy-start(bf16[128,256]{1,0:T(8,128)(2,1)} %param.15) | copy-start | bytes 196612
  16.7 24.7 %copy-start.29 = (bf16[128,256]{1,0:T(8,128)(2,1)S(1)}, bf16[128,256]{1,0:T(8,128)(2,1)}, u32[]{:S(2)}) copy-start(bf16[128,256]{1,0:T(8,128)(2,1)} %param.16) | copy-start | bytes 196612
  17.6 49.7 %copy-start.26 = (bf16[128,256]{1,0:T(8,128)(2,1)S(1)}, bf16[128,256]{1,0:T(8,128)(2,1)}, u32[]{:S(2)}) copy-start(bf16[128,256]{1,0:T(8,128)(2,1)} %param.17) | copy-start | bytes 196612
  17.6 54.1 %copy-start.36 = (f32[2,128,128]{2,1,0:T(8,128)S(1)}, f32[2,128,128]{2,1,0:T(8,128)}, u32[]{:S(2)}) copy-start(f32[2,128,128]{2,1,0:T(8,128)} %param.18) | copy-start | bytes 393220
  17.7 14.8 %collective-permute-start.1 = (f32[2,128,128]{2,1,0:T(8,128)S(1)}, f32[2,128,128]{2,1,0:T(8,128)S(1)}, u32[]{:S(2)}, u32[]{:S(2)}) collective-permute-start(f32[2,128,128]{2,1,0:T(8,128)S(1)} %add.116), channel_id=1, source_target_pairs={{0,64},{32,96},{64,0},{96,32},{128,192},{160,224},{192,128},{224,1... | collective-permute-start | bytes 393224 | tf_op jit(solution)/shard_map/ppermute | solution.py:14
  22.9 49.8 %copy-start.44 = (f32[256]{0:T(256)S(1)}, f32[256]{0:T(256)}, u32[]{:S(2)}) copy-start(f32[256]{0:T(256)} %param.19) | copy-start | bytes 3076
  23.9 49.1 %all-to-all-start.4 = ((bf16[32,20,96]{2,1,0:T(8,128)(2,1)}), bf16[32,20,96]{2,1,0:T(8,128)(2,1)S(1)}, u32[]{:S(2)}, u32[]{:S(2)}) async-start(bf16[32,20,96]{2,1,0:T(8,128)(2,1)} %all_to_all.56), calls=%async_computation.4 | async-start | bytes 393216 | tf_op jit(solution)/shard_map/all_to_all | solution.py:140
  32.4 42.1 %copy-start.20 = (bf16[128,256]{0,1:T(8,128)(2,1)}, bf16[128,256]{0,1:T(8,128)(2,1)S(1)}, u32[]{:S(2)}) copy-start(bf16[128,256]{0,1:T(8,128)(2,1)S(1)} %copy.234) | copy-start | bytes 196612
  32.5 42.1 %copy-start.42 = (pred[128,128]{1,0:T(8,128)(4,1)}, pred[128,128]{1,0:T(8,128)(4,1)S(1)}, u32[]{:S(2)}) copy-start(pred[128,128]{1,0:T(8,128)(4,1)S(1)} %iota_compare_fusion) | copy-start | bytes 49156
  32.5 23.3 %collective-permute-start.2 = (f32[2,128,128]{2,1,0:T(8,128)S(1)}, f32[2,128,128]{2,1,0:T(8,128)S(1)}, u32[]{:S(2)}, u32[]{:S(2)}) collective-permute-start(f32[2,128,128]{2,1,0:T(8,128)S(1)} %add.118), channel_id=1, source_target_pairs={{0,128},{32,160},{64,192},{96,224},{128,0},{160,32},{192,64},{224,... | collective-permute-start | bytes 393224 | tf_op jit(solution)/shard_map/ppermute | solution.py:14
  41.6 33.0 %copy-start.31 = (bf16[2,128,128]{2,1,0:T(8,128)(2,1)}, bf16[2,128,128]{2,1,0:T(8,128)(2,1)S(1)}, u32[]{:S(2)}) copy-start(bf16[2,128,128]{2,1,0:T(8,128)(2,1)S(1)} %fusion.14) | copy-start | bytes 196612
  55.8 15.8 %collective-permute-start.3 = (f32[2,128,128]{2,1,0:T(8,128)S(1)}, f32[2,128,128]{2,1,0:T(8,128)S(1)}, u32[]{:S(2)}, u32[]{:S(2)}) collective-permute-start(f32[2,128,128]{2,1,0:T(8,128)S(1)} %add.120), channel_id=1, source_target_pairs={{0,256},{32,288},{64,320},{96,352},{128,384},{160,416},{192,448},{... | collective-permute-start | bytes 393224 | tf_op jit(solution)/shard_map/ppermute | solution.py:14
  74.5 42.7 %all-to-all-start = ((bf16[32,128,256]{2,1,0:T(8,128)(2,1)}), bf16[32,128,256]{2,1,0:T(8,128)(2,1)}, u32[]{:S(2)}, u32[]{:S(2)}) async-start(bf16[32,128,256]{2,1,0:T(8,128)(2,1)} %broadcast_in_dim.30), calls=%async_computation | async-start | bytes 4194304 | tf_op jit(solution)/shard_map/all_to_all | solution.py:26
  88.5 28.7 %copy-start.50 = (bf16[128,96]{0,1:T(8,128)(2,1)S(1)}, bf16[128,96]{0,1:T(8,128)(2,1)}, u32[]{:S(2)}) copy-start(bf16[128,96]{0,1:T(8,128)(2,1)} %param.21) | copy-start | bytes 73732
  88.5 76.1 %all-gather.10.cloned.1.call-start = ((), (), s32[]{:S(2)}) async-start(), calls=%async_computation.12 | async-start | bytes 2506752 | tf_op jit(solution)/shard_map/all_gather | solution.py:141
  89.5 147.2 %all-gather.8.cloned.1.call-start = ((), (), s32[]{:S(2)}) async-start(), calls=%async_computation.11 | async-start | bytes 2506752 | tf_op jit(solution)/shard_map/all_gather | solution.py:128
  89.8 31.1 %copy-start.4 = (f32[128,640]{0,1:T(8,128)}, f32[128,640]{0,1:T(8,128)S(1)}, u32[]{:S(2)}) copy-start(f32[128,640]{0,1:T(8,128)S(1)} %reshape.181) | copy-start | bytes 983044
  120.1 15.1 %copy-start.41 = (f32[3072]{0:T(1024)S(1)}, f32[3072]{0:T(1024)}, u32[]{:S(2)}) copy-start(f32[3072]{0:T(1024)} %param.22) | copy-start | bytes 36868
  120.9 20.4 %copy-start.15 = (bf16[8192,96]{0,1:T(8,128)(2,1)S(1)}, bf16[8192,96]{0,1:T(8,128)(2,1)}, u32[]{:S(2)}) copy-start(bf16[8192,96]{0,1:T(8,128)(2,1)} %all-gather.6.cloned.1.call-done) | copy-start | bytes 4718596
  133.9 8.9 %copy-start.6 = (bf16[32,20,96]{2,1,0:T(8,128)(2,1)}, bf16[32,20,96]{2,1,0:T(8,128)(2,1)S(1)}, u32[]{:S(2)}) copy-start(bf16[32,20,96]{2,1,0:T(8,128)(2,1)S(1)} %all_to_all.75) | copy-start | bytes 368644
  137.5 10.7 %all-to-all-start.3 = ((f32[32,128,1]{1,2,0:T(1,128)}), f32[32,128,1]{1,2,0:T(1,128)S(1)}, u32[]{:S(2)}, u32[]{:S(2)}) async-start(f32[32,128,1]{1,2,0:T(1,128)} %broadcast_in_dim.31), calls=%async_computation.3 | async-start | bytes 32768 | tf_op jit(solution)/shard_map/all_to_all | solution.py:26
  148.2 92.4 %all-to-all-start.2 = ((bf16[32,256,96]{1,2,0:T(8,128)(2,1)}), bf16[32,256,96]{1,2,0:T(8,128)(2,1)S(1)}, u32[]{:S(2)}, u32[]{:S(2)}) async-start(bf16[32,256,96]{1,2,0:T(8,128)(2,1)} %bitcast.172), calls=%async_computation.2 | async-start | bytes 3145728 | tf_op jit(solution)/shard_map/all_to_all | solution.py:127
  152.5 192.3 %reduce-scatter.2.cloned.1.call-start = ((), (), s32[]{:S(2)}) async-start(), calls=%async_computation.10 | async-start | bytes 4177920 | tf_op jit(solution)/shard_map/reduce_scatter | solution.py:35
  268.8 77.8 %copy-start.7 = (bf16[32,20,96]{2,1,0:T(8,128)(2,1)S(1)}, bf16[32,20,96]{2,1,0:T(8,128)(2,1)}, u32[]{:S(2)}) copy-start(bf16[32,20,96]{2,1,0:T(8,128)(2,1)} %copy-done.6) | copy-start | bytes 368644
  269.0 106.0 %copy-start.5 = (f32[128,640]{0,1:T(8,128)S(1)}, f32[128,640]{0,1:T(8,128)}, u32[]{:S(2)}) copy-start(f32[128,640]{0,1:T(8,128)} %copy-done.4) | copy-start | bytes 983044
  346.4 28.9 %copy-start.34 = (bf16[128,96]{0,1:T(8,128)(2,1)S(1)}, bf16[128,96]{0,1:T(8,128)(2,1)}, u32[]{:S(2)}) copy-start(bf16[128,96]{0,1:T(8,128)(2,1)} %copy-done.33) | copy-start | bytes 73732
  346.4 28.9 %copy-start.39 = (bf16[128,96]{0,1:T(8,128)(2,1)S(1)}, bf16[128,96]{0,1:T(8,128)(2,1)}, u32[]{:S(2)}) copy-start(bf16[128,96]{0,1:T(8,128)(2,1)} %param.29) | copy-start | bytes 73732
  347.9 26.6 %all-to-all-start.5 = ((bf16[20,32,98]{2,0,1:T(8,128)(2,1)}), bf16[20,32,98]{2,0,1:T(8,128)(2,1)S(1)}, u32[]{:S(2)}, u32[]{:S(2)}) async-start(bf16[20,32,98]{2,0,1:T(8,128)(2,1)} %copy.208), calls=%async_computation.6 | async-start | bytes 393216 | tf_op jit(solution)/shard_map/all_to_all | solution.py:160
  374.6 20.8 %copy-start.3 = (bf16[32,256,96]{1,2,0:T(8,128)(2,1)S(1)}, bf16[32,256,96]{1,2,0:T(8,128)(2,1)}, u32[]{:S(2)}) copy-start(bf16[32,256,96]{1,2,0:T(8,128)(2,1)} %copy-done.2) | copy-start | bytes 4718596
  377.3 18.1 %all-to-all-start.6 = ((bf16[32,128,96]{1,2,0:T(8,128)(2,1)}), bf16[32,128,96]{1,2,0:T(8,128)(2,1)S(1)}, u32[]{:S(2)}, u32[]{:S(2)}) async-start(bf16[32,128,96]{1,2,0:T(8,128)(2,1)} %broadcast_in_dim.33), calls=%async_computation.7 | async-start | bytes 1572864 | tf_op jit(solution)/shard_map/all_to_all | solution.py:26
  381.1 15.6 %copy-start.43 = (pred[128,128]{1,0:T(8,128)(4,1)S(1)}, pred[128,128]{1,0:T(8,128)(4,1)}, u32[]{:S(2)}) copy-start(pred[128,128]{1,0:T(8,128)(4,1)} %copy-done.42) | copy-start | bytes 49156
  396.2 4.5 copy-start.23
  396.2 14.2 %copy-start.32 = (bf16[2,128,128]{2,1,0:T(8,128)(2,1)S(1)}, bf16[2,128,128]{2,1,0:T(8,128)(2,1)}, u32[]{:S(2)}) copy-start(bf16[2,128,128]{2,1,0:T(8,128)(2,1)} %copy-done.31) | copy-start | bytes 196612
  396.3 26.7 %copy-start.22 = (bf16[128,256]{0,1:T(8,128)(2,1)S(1)}, bf16[128,256]{0,1:T(8,128)(2,1)}, u32[]{:S(2)}) copy-start(bf16[128,256]{0,1:T(8,128)(2,1)} %copy-done.20) | copy-start | bytes 196612
  396.6 46.7 %copy-start.9 = (f32[128,32,20]{0,1,2:T(8,128)S(1)}, f32[128,32,20]{0,1,2:T(8,128)}, u32[]{:S(2)}) copy-start(f32[128,32,20]{0,1,2:T(8,128)} %copy-done.8) | copy-start | bytes 983044
  396.6 46.7 %copy-start.35 = (bf16[128,96]{0,1:T(8,128)(2,1)S(1)}, bf16[128,96]{0,1:T(8,128)(2,1)}, u32[]{:S(2)}) copy-start(bf16[128,96]{0,1:T(8,128)(2,1)} %copy-done.33) | copy-start | bytes 73732
  397.0 9.0 %collective-permute-start.4 = (f32[2,128,128]{2,1,0:T(8,128)S(1)}, f32[2,128,128]{2,1,0:T(8,128)S(1)}, u32[]{:S(2)}, u32[]{:S(2)}) collective-permute-start(f32[2,128,128]{2,1,0:T(8,128)S(1)} %convolution_bitcast_fusion.4), channel_id=1, source_target_pairs={{0,32},{32,0},{64,96},{96,64},{128,160},{160,128},{192,224},{224,1... | collective-permute-start | bytes 393224 | tf_op jit(solution)/shard_map/ppermute | solution.py:14
  400.8 57.3 %copy-start.30 = (bf16[128,256]{1,0:T(8,128)(2,1)S(1)}, bf16[128,256]{1,0:T(8,128)(2,1)}, u32[]{:S(2)}) copy-start(bf16[128,256]{1,0:T(8,128)(2,1)} %param.16) | copy-start | bytes 196612
  401.6 57.6 %copy-start.28 = (bf16[128,256]{1,0:T(8,128)(2,1)S(1)}, bf16[128,256]{1,0:T(8,128)(2,1)}, u32[]{:S(2)}) copy-start(bf16[128,256]{1,0:T(8,128)(2,1)} %param.17) | copy-start | bytes 196612
  401.6 41.6 %all-to-all-start.7 = ((bf16[20,32,96]{2,0,1:T(8,128)(2,1)}), bf16[20,32,96]{2,0,1:T(8,128)(2,1)S(1)}, u32[]{:S(2)}, u32[]{:S(2)}) async-start(bf16[20,32,96]{2,0,1:T(8,128)(2,1)} %copy.212), calls=%async_computation.8 | async-start | bytes 393216 | tf_op jit(solution)/shard_map/all_to_all | solution.py:181
  406.1 10.5 %collective-permute-start.5 = (f32[2,128,128]{2,1,0:T(8,128)S(1)}, f32[2,128,128]{2,1,0:T(8,128)S(1)}, u32[]{:S(2)}, u32[]{:S(2)}) collective-permute-start(f32[2,128,128]{2,1,0:T(8,128)S(1)} %add.138), channel_id=1, source_target_pairs={{0,64},{32,96},{64,0},{96,32},{128,192},{160,224},{192,128},{224,1... | collective-permute-start | bytes 393224 | tf_op jit(solution)/shard_map/ppermute | solution.py:14
  416.6 18.1 %collective-permute-start.6 = (f32[2,128,128]{2,1,0:T(8,128)S(1)}, f32[2,128,128]{2,1,0:T(8,128)S(1)}, u32[]{:S(2)}, u32[]{:S(2)}) collective-permute-start(f32[2,128,128]{2,1,0:T(8,128)S(1)} %add.140), channel_id=1, source_target_pairs={{0,128},{32,160},{64,192},{96,224},{128,0},{160,32},{192,64},{224,... | collective-permute-start | bytes 393224 | tf_op jit(solution)/shard_map/ppermute | solution.py:14
  434.6 22.8 %collective-permute-start.7 = (f32[2,128,128]{2,1,0:T(8,128)S(1)}, f32[2,128,128]{2,1,0:T(8,128)S(1)}, u32[]{:S(2)}, u32[]{:S(2)}) collective-permute-start(f32[2,128,128]{2,1,0:T(8,128)S(1)} %add.142), channel_id=1, source_target_pairs={{0,256},{32,288},{64,320},{96,352},{128,384},{160,416},{192,448},{... | collective-permute-start | bytes 393224 | tf_op jit(solution)/shard_map/ppermute | solution.py:14
  (22 other events, 41.6 us)
Sparse Core Ops, SparseCore 0:
  10.1 84.2 all-gather.5
  96.5 68.0 all-gather.9
  166.7 70.0 all-gather.7
  269.0 75.7 reduce-scatter.1

commit v7 on v6

--- a/solution.py
+++ b/solution.py
@@ -26,14 +26,13 @@
     return lax.all_to_all(spread, axis, 0, 0, tiled=True)
 
 
-def scatter_sum(value, axis):
+def scatter_sum(values, axis):
     count = lax.axis_size(axis)
-    parts, rows, width = value.shape
+    rows, width = values[0].shape
     block = rows // count
-    dense = value.reshape(parts, count, block, width).transpose(1, 0, 2, 3)
-    dense = dense.reshape(count, parts * block * width // 128, 128)
-    part = lax.psum_scatter(dense, axis, scatter_dimension=0, tiled=True)
-    return part.reshape(parts, block, width)
+    joined = jnp.concatenate([value.reshape(count, block, width) for value in values], 1)
+    part = lax.psum_scatter(joined, axis, scatter_dimension=0, tiled=True)
+    return [part[0, i * block:(i + 1) * block] for i in range(len(values))]
 
 
 def head_normalize(attended, gain):
@@ -147,9 +146,7 @@
         jnp.dot(grad_gate_pre, w_gate, preferred_element_type=f32)
         + jnp.dot(grad_up_pre, w_up, preferred_element_type=f32)
     ).astype(jnp.bfloat16)
-    both_halves = scatter_sum(jnp.stack([out_terms, grad_terms]), "ctx")
-    half_out = both_halves[0]
-    grad_half = both_halves[1]
+    half_out, grad_half = scatter_sum([out_terms, grad_terms], "ctx")
     slot_inner = jnp.sum(slot_rows * model_gain * grad_half.astype(f32), -1, keepdims=True)
     inner_hi = slot_inner.astype(jnp.bfloat16)
     inner_lo = (slot_inner - inner_hi.astype(f32)).astype(jnp.bfloat16)

time: 468 us -> 465 us (level)
  local copies, waits for them, and re-layouts: 44.1 us -> 35.5 us
  waiting for transfers between devices: 256 us -> 263 us
  starting transfers between devices: 109 us -> 104 us
    ppermute x8, waiting for transfers between devices: 49 us -> 55.6 us  [butterfly_sums(): other = lax.ppermute(total, axis, [(i, i ^ step) for i in range(count)])]
    another operation x3 -> x1, local copies, waits for them, and re-layouts: 6.22 us -> 0.01 us  [the longest x2 6.21 us: local(): both_halves = scatter_sum(jnp.stack([out_terms, grad_terms]), 'ctx')]
    concatenate x0 -> x1, other arithmetic: none -> 5.22 us  [scatter_sum(): jnp.concatenate([value.reshape(count, block, width) for value in values], 1)]
    unnamed x107 -> x91, local copies, waits for them, and re-layouts: 9.9 us -> 9.99 us
  transfers between devices with their start and end apart: 19 -> 19, of which waited for: 12 -> 13; matrix products, arithmetic and copies ran while one was open for 7% -> 7% of each run, Pallas kernels for 0% -> 0%
where the time goes in v7:
time: 465 us; the launch traced here: 463 us
  waiting for transfers between devices  263 us (57%)
  starting transfers between devices  104 us (22%)
  local copies, waits for them, and re-layouts  35.5 us (8%)
  matrix products  21.6 us (5%)
  between operations  14.7 us (3%)
  blocking collectives  12.8 us (3%)
  other arithmetic  11.5 us (2%)
    reduce_scatter x1, waiting for transfers between devices, scatter_sum(): part = lax.psum_scatter(joined, axis, scatter_dimension=0, tiled=True)  76.2 us
    all_gather x1, waiting for transfers between devices, local(): portion = lax.all_gather(expert_in, 'ctx', axis=0, tiled=True)  65.1 us
    ppermute x8, waiting for transfers between devices, butterfly_sums(): other = lax.ppermute(total, axis, [(i, i ^ step) for i in range(count)])  55.6 us
    ppermute x8, starting transfers between devices, butterfly_sums(): other = lax.ppermute(total, axis, [(i, i ^ step) for i in range(count)])  47.9 us
    all_to_all x3, waiting for transfers between devices, gather_blocks(): return lax.all_to_all(spread, axis, 0, 0, tiled=True)  47.1 us
    all_to_all x3, starting transfers between devices, gather_blocks(): return lax.all_to_all(spread, axis, 0, 0, tiled=True)  21.4 us
    all_to_all x1, starting transfers between devices, local(): lax.all_to_all(payload, 'ep', split_axis=1, concat_axis=0, tiled=True)  17.9 us
    all_to_all x1, blocking collectives, local(): lax.all_to_all(picked.reshape(ep_count, capacity, columns), 'ep', 0, 0, t...  12.8 us
  transfers between devices with their start and end apart: 19, of which 13 were waited for; matrix products, arithmetic and copies ran while one was open for 7% of the time, Pallas kernels for 0%

profile of v7, /device:TPU:1, one launch (start us, length us, event | category | flops | bytes accessed | tf_op | source)
XLA Modules:
  0.0 463.1 jit_solution(6493879586921267584)
XLA Ops:
  8.9 1.0 fusion.47
  9.9 4.4 collective-permute-start
  17.7 4.9 %collective-permute-start.1 = (f32[2,128,128]{2,1,0:T(8,128)S(1)}, f32[2,128,128]{2,1,0:T(8,128)S(1)}, u32[]{:S(2)}, u32[]{:S(2)}) collective-permute-start(f32[2,128,128]{2,1,0:T(8,128)S(1)} %add.116), channel_id=1, source_target_pairs={{0,64},{32,96},{64,0},{96,32},{128,192},{160,224},{192,128},{224,1... | collective-permute-start | bytes 393224 | tf_op jit(solution)/shard_map/ppermute | solution.py:14
  23.9 8.4 %all-to-all-start.4 = ((bf16[32,20,96]{2,1,0:T(8,128)(2,1)}), bf16[32,20,96]{2,1,0:T(8,128)(2,1)S(1)}, u32[]{:S(2)}, u32[]{:S(2)}) async-start(bf16[32,20,96]{2,1,0:T(8,128)(2,1)} %all_to_all.56), calls=%async_computation.4 | async-start | bytes 393216 | tf_op jit(solution)/shard_map/all_to_all | solution.py:139
  32.5 8.8 %collective-permute-start.2 = (f32[2,128,128]{2,1,0:T(8,128)S(1)}, f32[2,128,128]{2,1,0:T(8,128)S(1)}, u32[]{:S(2)}, u32[]{:S(2)}) collective-permute-start(f32[2,128,128]{2,1,0:T(8,128)S(1)} %add.118), channel_id=1, source_target_pairs={{0,128},{32,160},{64,192},{96,224},{128,0},{160,32},{192,64},{224,... | collective-permute-start | bytes 393224 | tf_op jit(solution)/shard_map/ppermute | solution.py:14
  41.6 14.2 %collective-permute-done.2 = f32[2,128,128]{2,1,0:T(8,128)S(1)} collective-permute-done((f32[2,128,128]{2,1,0:T(8,128)S(1)}, f32[2,128,128]{2,1,0:T(8,128)S(1)}, u32[]{:S(2)}, u32[]{:S(2)}) %collective-permute-start.2) | collective-permute-done | bytes 131104 | tf_op jit(solution)/shard_map/ppermute | solution.py:14
  55.8 11.4 %collective-permute-start.3 = (f32[2,128,128]{2,1,0:T(8,128)S(1)}, f32[2,128,128]{2,1,0:T(8,128)S(1)}, u32[]{:S(2)}, u32[]{:S(2)}) collective-permute-start(f32[2,128,128]{2,1,0:T(8,128)S(1)} %add.120), channel_id=1, source_target_pairs={{0,256},{32,288},{64,320},{96,352},{128,384},{160,416},{192,448},{... | collective-permute-start | bytes 393224 | tf_op jit(solution)/shard_map/ppermute | solution.py:14
  67.4 4.4 collective-permute-done.3
  73.1 1.6 broadcast_in_dim.30
  74.7 13.8 %all-to-all-start = ((bf16[32,128,256]{2,1,0:T(8,128)(2,1)}), bf16[32,128,256]{2,1,0:T(8,128)(2,1)}, u32[]{:S(2)}, u32[]{:S(2)}) async-start(bf16[32,128,256]{2,1,0:T(8,128)(2,1)} %broadcast_in_dim.30), calls=%async_computation | async-start | bytes 4194304 | tf_op jit(solution)/shard_map/all_to_all | solution.py:26
  89.8 27.4 %all-to-all-done = bf16[32,128,256]{2,1,0:T(8,128)(2,1)} async-done(((bf16[32,128,256]{2,1,0:T(8,128)(2,1)}), bf16[32,128,256]{2,1,0:T(8,128)(2,1)}, u32[]{:S(2)}, u32[]{:S(2)}) %all-to-all-start) | async-done | bytes 2097184 | tf_op jit(solution)/shard_map/all_to_all | solution.py:26
  117.2 3.4 fusion.51
  121.1 12.8 %all_to_all.75 = bf16[32,20,96]{2,1,0:T(8,128)(2,1)S(1)} all-to-all(bf16[32,20,96]{2,1,0:T(8,128)(2,1)S(1)} %reshape.174), channel_id=1, replica_groups=mesh['ctx'=16,'ep'=32] {'ep'}, dimensions={0} | all-to-all | bytes 245760 | tf_op jit(solution)/shard_map/all_to_all | solution.py:116
  134.7 1.9 reshape.184
  136.8 1.7 fusion.37
  138.5 1.2 broadcast_in_dim.31
  139.8 3.8 all-to-all-start.3
  143.6 1.4 copy.265
  145.0 5.4 %all-to-all-done.3 = f32[32,128,1]{1,2,0:T(1,128)S(1)} async-done(((f32[32,128,1]{1,2,0:T(1,128)}), f32[32,128,1]{1,2,0:T(1,128)S(1)}, u32[]{:S(2)}, u32[]{:S(2)}) %all-to-all-start.3) | async-done | bytes 16416 | tf_op jit(solution)/shard_map/all_to_all | solution.py:26
  150.5 4.3 all-to-all-start.2
  155.0 9.8 %all-gather.10.cloned.1.call-done = bf16[16,20,3072]{2,1,0:T(8,128)(2,1)} async-done(((bf16[1,20,3072]{2,1,0:T(8,128)(2,1)}), bf16[16,20,3072]{2,1,0:T(8,128)(2,1)}) %all-gather.10.cloned.1.call-update) | async-done | bytes 1966096 | tf_op jit(solution)/shard_map/all_gather | solution.py:140
  164.8 4.0 reshape.188
  168.8 3.2 fusion.1
  172.0 65.1 %all-gather.8.cloned.1.call-done = bf16[16,20,3072]{2,1,0:T(8,128)(2,1)} async-done(((bf16[1,20,3072]{2,1,0:T(8,128)(2,1)}), bf16[16,20,3072]{2,1,0:T(8,128)(2,1)}) %all-gather.8.cloned.1.call-update) | async-done | bytes 1966096 | tf_op jit(solution)/shard_map/all_gather | solution.py:127
  237.1 4.0 reshape.186
  241.1 3.4 fusion.9
  247.6 2.0 fusion
  249.6 3.9 reshape.177
  253.6 2.1 reshape.175
  255.7 5.2 %pad_maximum_fusion = bf16[16,40,3072]{2,1,0:T(8,128)(2,1)} fusion(bf16[16,20,3072]{2,1,0:T(8,128)(2,1)} %reshape.177, bf16[16,20,3072]{2,1,0:T(8,128)(2,1)} %reshape.175), kind=kLoop, calls=%fused_computation.3 | loop fusion | flops 7864320 | bytes 7864320 | tf_op jit(solution)/shard_map/concatenate | solution.py:33
  261.1 76.2 %reduce-scatter.2.cloned.1.call-done = bf16[1,40,3072]{2,1,0:T(8,128)(2,1)} async-done(((bf16[16,40,3072]{2,1,0:T(8,128)(2,1)}), bf16[1,40,3072]{2,1,0:T(8,128)(2,1)}) %reduce-scatter.2.cloned.1.call-update) | async-done | bytes 245776 | tf_op jit(solution)/shard_map/reduce_scatter | solution.py:34
  337.3 1.7 fusion.65
  340.4 17.9 %all-to-all-start.5 = ((bf16[20,32,98]{2,0,1:T(8,128)(2,1)}), bf16[20,32,98]{2,0,1:T(8,128)(2,1)S(1)}, u32[]{:S(2)}, u32[]{:S(2)}) async-start(bf16[20,32,98]{2,0,1:T(8,128)(2,1)} %copy.203), calls=%async_computation.6 | async-start | bytes 393216 | tf_op jit(solution)/shard_map/all_to_all | solution.py:157
  358.3 8.2 %all-to-all-done.5 = bf16[20,32,98]{2,0,1:T(8,128)(2,1)S(1)} async-done(((bf16[20,32,98]{2,0,1:T(8,128)(2,1)}), bf16[20,32,98]{2,0,1:T(8,128)(2,1)S(1)}, u32[]{:S(2)}, u32[]{:S(2)}) %all-to-all-start.5) | async-done | bytes 125472 | tf_op jit(solution)/shard_map/all_to_all | solution.py:157
  367.9 1.3 fusion.25
  369.2 1.0 broadcast_in_dim.33
  370.2 3.8 all-to-all-start.6
  374.1 14.3 %all-to-all-done.6 = bf16[32,128,96]{1,2,0:T(8,128)(2,1)S(1)} async-done(((bf16[32,128,96]{1,2,0:T(8,128)(2,1)}), bf16[32,128,96]{1,2,0:T(8,128)(2,1)S(1)}, u32[]{:S(2)}, u32[]{:S(2)}) %all-to-all-start.6) | async-done | bytes 786464 | tf_op jit(solution)/shard_map/all_to_all | solution.py:26
  389.9 1.1 all_to_all.64
  391.8 4.0 all-to-all-start.7
  396.0 2.6 collective-permute-start.4
  399.6 3.0 collective-permute-done.4
  402.6 3.8 collective-permute-start.5
  406.6 6.5 %collective-permute-done.5 = f32[2,128,128]{2,1,0:T(8,128)S(1)} collective-permute-done((f32[2,128,128]{2,1,0:T(8,128)S(1)}, f32[2,128,128]{2,1,0:T(8,128)S(1)}, u32[]{:S(2)}, u32[]{:S(2)}) %collective-permute-start.5) | collective-permute-done | bytes 131104 | tf_op jit(solution)/shard_map/ppermute | solution.py:14
  413.2 5.4 %collective-permute-start.6 = (f32[2,128,128]{2,1,0:T(8,128)S(1)}, f32[2,128,128]{2,1,0:T(8,128)S(1)}, u32[]{:S(2)}, u32[]{:S(2)}) collective-permute-start(f32[2,128,128]{2,1,0:T(8,128)S(1)} %add.140), channel_id=1, source_target_pairs={{0,128},{32,160},{64,192},{96,224},{128,0},{160,32},{192,64},{224,... | collective-permute-start | bytes 393224 | tf_op jit(solution)/shard_map/ppermute | solution.py:14
  418.8 13.0 %collective-permute-done.6 = f32[2,128,128]{2,1,0:T(8,128)S(1)} collective-permute-done((f32[2,128,128]{2,1,0:T(8,128)S(1)}, f32[2,128,128]{2,1,0:T(8,128)S(1)}, u32[]{:S(2)}, u32[]{:S(2)}) %collective-permute-start.6) | collective-permute-done | bytes 131104 | tf_op jit(solution)/shard_map/ppermute | solution.py:14
  431.8 6.5 %collective-permute-start.7 = (f32[2,128,128]{2,1,0:T(8,128)S(1)}, f32[2,128,128]{2,1,0:T(8,128)S(1)}, u32[]{:S(2)}, u32[]{:S(2)}) collective-permute-start(f32[2,128,128]{2,1,0:T(8,128)S(1)} %add.142), channel_id=1, source_target_pairs={{0,256},{32,288},{64,320},{96,352},{128,384},{160,416},{192,448},{... | collective-permute-start | bytes 393224 | tf_op jit(solution)/shard_map/ppermute | solution.py:14
  439.3 14.5 %collective-permute-done.7 = f32[2,128,128]{2,1,0:T(8,128)S(1)} collective-permute-done((f32[2,128,128]{2,1,0:T(8,128)S(1)}, f32[2,128,128]{2,1,0:T(8,128)S(1)}, u32[]{:S(2)}, u32[]{:S(2)}) %collective-permute-start.7) | collective-permute-done | bytes 131104 | tf_op jit(solution)/shard_map/ppermute | solution.py:14
  (175 shorter events, 24.5 us)
Async XLA Ops:
  7.2 161.6 %copy-start = (bf16[1,192,3072]{2,1,0:T(8,128)(2,1)S(1)}, bf16[1,192,3072]{2,1,0:T(8,128)(2,1)}, u32[]{:S(2)}) copy-start(bf16[1,192,3072]{2,1,0:T(8,128)(2,1)} %param.28) | copy-start | bytes 3538948
  7.2 15.4 %copy-start.33 = (bf16[128,96]{0,1:T(8,128)(2,1)S(1)}, bf16[128,96]{0,1:T(8,128)(2,1)}, u32[]{:S(2)}) copy-start(bf16[128,96]{0,1:T(8,128)(2,1)} %param.29) | copy-start | bytes 73732
  7.2 110.1 %all-gather.6.cloned.1.call-start = ((), (), s32[]{:S(2)}) async-start(), calls=%async_computation.9 | async-start | bytes 1671168 | tf_op jit(solution)/shard_map/all_gather | solution.py:77
  8.9 7.8 %copy-start.20 = (bf16[128,256]{0,1:T(8,128)(2,1)}, bf16[128,256]{0,1:T(8,128)(2,1)S(1)}, u32[]{:S(2)}) copy-start(bf16[128,256]{0,1:T(8,128)(2,1)S(1)} %copy.262) | copy-start | bytes 196612
  9.9 7.8 %collective-permute-start = (f32[2,128,128]{2,1,0:T(8,128)S(1)}, f32[2,128,128]{2,1,0:T(8,128)S(1)}, u32[]{:S(2)}, u32[]{:S(2)}) collective-permute-start(f32[2,128,128]{2,1,0:T(8,128)S(1)} %fusion.47), channel_id=1, source_target_pairs={{0,32},{32,0},{64,96},{96,64},{128,160},{160,128},{192,224},{224,1... | collective-permute-start | bytes 393224 | tf_op jit(solution)/shard_map/ppermute | solution.py:14
  15.7 16.6 %copy-start.34 = (bf16[128,256]{1,0:T(8,128)(2,1)S(1)}, bf16[128,256]{1,0:T(8,128)(2,1)}, u32[]{:S(2)}) copy-start(bf16[128,256]{1,0:T(8,128)(2,1)} %param.15) | copy-start | bytes 196612
  16.7 24.7 %copy-start.25 = (bf16[128,256]{1,0:T(8,128)(2,1)S(1)}, bf16[128,256]{1,0:T(8,128)(2,1)}, u32[]{:S(2)}) copy-start(bf16[128,256]{1,0:T(8,128)(2,1)} %param.16) | copy-start | bytes 196612
  17.6 49.6 %copy-start.22 = (bf16[128,256]{1,0:T(8,128)(2,1)S(1)}, bf16[128,256]{1,0:T(8,128)(2,1)}, u32[]{:S(2)}) copy-start(bf16[128,256]{1,0:T(8,128)(2,1)} %param.17) | copy-start | bytes 196612
  17.6 54.2 %copy-start.31 = (f32[2,128,128]{2,1,0:T(8,128)S(1)}, f32[2,128,128]{2,1,0:T(8,128)}, u32[]{:S(2)}) copy-start(f32[2,128,128]{2,1,0:T(8,128)} %param.18) | copy-start | bytes 393220
  17.7 14.8 %collective-permute-start.1 = (f32[2,128,128]{2,1,0:T(8,128)S(1)}, f32[2,128,128]{2,1,0:T(8,128)S(1)}, u32[]{:S(2)}, u32[]{:S(2)}) collective-permute-start(f32[2,128,128]{2,1,0:T(8,128)S(1)} %add.116), channel_id=1, source_target_pairs={{0,64},{32,96},{64,0},{96,32},{128,192},{160,224},{192,128},{224,1... | collective-permute-start | bytes 393224 | tf_op jit(solution)/shard_map/ppermute | solution.py:14
  22.9 49.9 %copy-start.36 = (f32[256]{0:T(256)S(1)}, f32[256]{0:T(256)}, u32[]{:S(2)}) copy-start(f32[256]{0:T(256)} %param.19) | copy-start | bytes 3076
  23.9 49.2 %all-to-all-start.4 = ((bf16[32,20,96]{2,1,0:T(8,128)(2,1)}), bf16[32,20,96]{2,1,0:T(8,128)(2,1)S(1)}, u32[]{:S(2)}, u32[]{:S(2)}) async-start(bf16[32,20,96]{2,1,0:T(8,128)(2,1)} %all_to_all.56), calls=%async_computation.4 | async-start | bytes 393216 | tf_op jit(solution)/shard_map/all_to_all | solution.py:139
  32.4 42.3 %copy-start.17 = (bf16[128,256]{0,1:T(8,128)(2,1)}, bf16[128,256]{0,1:T(8,128)(2,1)S(1)}, u32[]{:S(2)}) copy-start(bf16[128,256]{0,1:T(8,128)(2,1)S(1)} %copy.229) | copy-start | bytes 196612
  32.5 23.3 %collective-permute-start.2 = (f32[2,128,128]{2,1,0:T(8,128)S(1)}, f32[2,128,128]{2,1,0:T(8,128)S(1)}, u32[]{:S(2)}, u32[]{:S(2)}) collective-permute-start(f32[2,128,128]{2,1,0:T(8,128)S(1)} %add.118), channel_id=1, source_target_pairs={{0,128},{32,160},{64,192},{96,224},{128,0},{160,32},{192,64},{224,... | collective-permute-start | bytes 393224 | tf_op jit(solution)/shard_map/ppermute | solution.py:14
  41.6 33.1 %copy-start.27 = (bf16[2,128,128]{2,1,0:T(8,128)(2,1)}, bf16[2,128,128]{2,1,0:T(8,128)(2,1)S(1)}, u32[]{:S(2)}) copy-start(bf16[2,128,128]{2,1,0:T(8,128)(2,1)S(1)} %fusion.14) | copy-start | bytes 196612
  55.8 16.0 %collective-permute-start.3 = (f32[2,128,128]{2,1,0:T(8,128)S(1)}, f32[2,128,128]{2,1,0:T(8,128)S(1)}, u32[]{:S(2)}, u32[]{:S(2)}) collective-permute-start(f32[2,128,128]{2,1,0:T(8,128)S(1)} %add.120), channel_id=1, source_target_pairs={{0,256},{32,288},{64,320},{96,352},{128,384},{160,416},{192,448},{... | collective-permute-start | bytes 393224 | tf_op jit(solution)/shard_map/ppermute | solution.py:14
  72.2 2.5 copy-start.40
  74.7 42.5 %all-to-all-start = ((bf16[32,128,256]{2,1,0:T(8,128)(2,1)}), bf16[32,128,256]{2,1,0:T(8,128)(2,1)}, u32[]{:S(2)}, u32[]{:S(2)}) async-start(bf16[32,128,256]{2,1,0:T(8,128)(2,1)} %broadcast_in_dim.30), calls=%async_computation | async-start | bytes 4194304 | tf_op jit(solution)/shard_map/all_to_all | solution.py:26
  88.5 28.7 %copy-start.42 = (bf16[128,96]{0,1:T(8,128)(2,1)S(1)}, bf16[128,96]{0,1:T(8,128)(2,1)}, u32[]{:S(2)}) copy-start(bf16[128,96]{0,1:T(8,128)(2,1)} %param.21) | copy-start | bytes 73732
  88.5 76.3 %all-gather.10.cloned.1.call-start = ((), (), s32[]{:S(2)}) async-start(), calls=%async_computation.12 | async-start | bytes 2506752 | tf_op jit(solution)/shard_map/all_gather | solution.py:140
  89.5 147.6 %all-gather.8.cloned.1.call-start = ((), (), s32[]{:S(2)}) async-start(), calls=%async_computation.11 | async-start | bytes 2506752 | tf_op jit(solution)/shard_map/all_gather | solution.py:127
  120.6 247.3 %copy-start.29 = (bf16[128,96]{0,1:T(8,128)(2,1)}, bf16[128,96]{0,1:T(8,128)(2,1)S(1)}, u32[]{:S(2)}) copy-start(bf16[128,96]{0,1:T(8,128)(2,1)S(1)} %get-tuple-element.63) | copy-start | bytes 73732
  120.6 16.2 %copy-start.35 = (f32[3072]{0:T(1024)S(1)}, f32[3072]{0:T(1024)}, u32[]{:S(2)}) copy-start(f32[3072]{0:T(1024)} %param.22) | copy-start | bytes 36868
  120.8 22.7 %copy-start.11 = (bf16[8192,96]{0,1:T(8,128)(2,1)S(1)}, bf16[8192,96]{0,1:T(8,128)(2,1)}, u32[]{:S(2)}) copy-start(bf16[8192,96]{0,1:T(8,128)(2,1)} %all-gather.6.cloned.1.call-done) | copy-start | bytes 4718596
  133.8 11.2 %copy-start.3 = (bf16[32,20,96]{2,1,0:T(8,128)(2,1)}, bf16[32,20,96]{2,1,0:T(8,128)(2,1)S(1)}, u32[]{:S(2)}) copy-start(bf16[32,20,96]{2,1,0:T(8,128)(2,1)S(1)} %all_to_all.75) | copy-start | bytes 368644
  139.8 10.7 %all-to-all-start.3 = ((f32[32,128,1]{1,2,0:T(1,128)}), f32[32,128,1]{1,2,0:T(1,128)S(1)}, u32[]{:S(2)}, u32[]{:S(2)}) async-start(f32[32,128,1]{1,2,0:T(1,128)} %broadcast_in_dim.31), calls=%async_computation.3 | async-start | bytes 32768 | tf_op jit(solution)/shard_map/all_to_all | solution.py:26
  150.5 90.6 %all-to-all-start.2 = ((bf16[32,256,96]{1,2,0:T(8,128)(2,1)}), bf16[32,256,96]{1,2,0:T(8,128)(2,1)S(1)}, u32[]{:S(2)}, u32[]{:S(2)}) async-start(bf16[32,256,96]{1,2,0:T(8,128)(2,1)} %bitcast.172), calls=%async_computation.2 | async-start | bytes 3145728 | tf_op jit(solution)/shard_map/all_to_all | solution.py:126
  154.7 182.6 %reduce-scatter.2.cloned.1.call-start = ((), (), s32[]{:S(2)}) async-start(), calls=%async_computation.10 | async-start | bytes 4177920 | tf_op jit(solution)/shard_map/reduce_scatter | solution.py:34
  241.0 3.4 copy-start.1
  241.0 3.4 copy-start.9
  241.1 3.4 copy-start.16
  260.9 78.2 %copy-start.4 = (bf16[32,20,96]{2,1,0:T(8,128)(2,1)S(1)}, bf16[32,20,96]{2,1,0:T(8,128)(2,1)}, u32[]{:S(2)}) copy-start(bf16[32,20,96]{2,1,0:T(8,128)(2,1)} %copy-done.3) | copy-start | bytes 368644
  340.4 26.1 %all-to-all-start.5 = ((bf16[20,32,98]{2,0,1:T(8,128)(2,1)}), bf16[20,32,98]{2,0,1:T(8,128)(2,1)S(1)}, u32[]{:S(2)}, u32[]{:S(2)}) async-start(bf16[20,32,98]{2,0,1:T(8,128)(2,1)} %copy.203), calls=%async_computation.6 | async-start | bytes 393216 | tf_op jit(solution)/shard_map/all_to_all | solution.py:157
  367.3 21.1 %copy-start.2 = (bf16[32,256,96]{1,2,0:T(8,128)(2,1)S(1)}, bf16[32,256,96]{1,2,0:T(8,128)(2,1)}, u32[]{:S(2)}) copy-start(bf16[32,256,96]{1,2,0:T(8,128)(2,1)} %copy-done.1) | copy-start | bytes 4718596
  370.2 18.1 %all-to-all-start.6 = ((bf16[32,128,96]{1,2,0:T(8,128)(2,1)}), bf16[32,128,96]{1,2,0:T(8,128)(2,1)S(1)}, u32[]{:S(2)}, u32[]{:S(2)}) async-start(bf16[32,128,96]{1,2,0:T(8,128)(2,1)} %broadcast_in_dim.33), calls=%async_computation.7 | async-start | bytes 1572864 | tf_op jit(solution)/shard_map/all_to_all | solution.py:26
  389.1 6.7 %copy-start.21 = (bf16[128,256]{0,1:T(8,128)(2,1)S(1)}, bf16[128,256]{0,1:T(8,128)(2,1)}, u32[]{:S(2)}) copy-start(bf16[128,256]{0,1:T(8,128)(2,1)} %copy-done.20) | copy-start | bytes 196612
  389.1 9.5 %copy-start.14 = (f32[2,128,128]{2,1,0:T(8,128)S(1)}, f32[2,128,128]{2,1,0:T(8,128)}, u32[]{:S(2)}) copy-start(f32[2,128,128]{2,1,0:T(8,128)} %copy-done.13) | copy-start | bytes 393220
  389.1 17.3 %copy-start.19 = (bf16[128,256]{0,1:T(8,128)(2,1)S(1)}, bf16[128,256]{0,1:T(8,128)(2,1)}, u32[]{:S(2)}) copy-start(bf16[128,256]{0,1:T(8,128)(2,1)} %copy-done.17) | copy-start | bytes 196612
  389.2 29.4 %copy-start.28 = (bf16[2,128,128]{2,1,0:T(8,128)(2,1)S(1)}, bf16[2,128,128]{2,1,0:T(8,128)(2,1)}, u32[]{:S(2)}) copy-start(bf16[2,128,128]{2,1,0:T(8,128)(2,1)} %copy-done.27) | copy-start | bytes 196612
  389.5 48.9 %copy-start.6 = (f32[128,32,20]{0,1,2:T(8,128)S(1)}, f32[128,32,20]{0,1,2:T(8,128)}, u32[]{:S(2)}) copy-start(f32[128,32,20]{0,1,2:T(8,128)} %copy-done.5) | copy-start | bytes 983044
  389.5 48.9 %copy-start.30 = (bf16[128,96]{0,1:T(8,128)(2,1)S(1)}, bf16[128,96]{0,1:T(8,128)(2,1)}, u32[]{:S(2)}) copy-start(bf16[128,96]{0,1:T(8,128)(2,1)} %copy-done.29) | copy-start | bytes 73732
  391.8 46.6 %all-to-all-start.7 = ((bf16[20,32,96]{2,0,1:T(8,128)(2,1)}), bf16[20,32,96]{2,0,1:T(8,128)(2,1)S(1)}, u32[]{:S(2)}, u32[]{:S(2)}) async-start(bf16[20,32,96]{2,0,1:T(8,128)(2,1)} %copy.207), calls=%async_computation.8 | async-start | bytes 393216 | tf_op jit(solution)/shard_map/all_to_all | solution.py:178
  395.8 58.7 %copy-start.24 = (bf16[128,256]{1,0:T(8,128)(2,1)S(1)}, bf16[128,256]{1,0:T(8,128)(2,1)}, u32[]{:S(2)}) copy-start(bf16[128,256]{1,0:T(8,128)(2,1)} %param.17) | copy-start | bytes 196612
  396.0 6.6 %collective-permute-start.4 = (f32[2,128,128]{2,1,0:T(8,128)S(1)}, f32[2,128,128]{2,1,0:T(8,128)S(1)}, u32[]{:S(2)}, u32[]{:S(2)}) collective-permute-start(f32[2,128,128]{2,1,0:T(8,128)S(1)} %convolution_bitcast_fusion.4), channel_id=1, source_target_pairs={{0,32},{32,0},{64,96},{96,64},{128,160},{160,128},{192,224},{224,1... | collective-permute-start | bytes 393224 | tf_op jit(solution)/shard_map/ppermute | solution.py:14
  398.8 56.7 %copy-start.26 = (bf16[128,256]{1,0:T(8,128)(2,1)S(1)}, bf16[128,256]{1,0:T(8,128)(2,1)}, u32[]{:S(2)}) copy-start(bf16[128,256]{1,0:T(8,128)(2,1)} %param.16) | copy-start | bytes 196612
  402.6 10.5 %collective-permute-start.5 = (f32[2,128,128]{2,1,0:T(8,128)S(1)}, f32[2,128,128]{2,1,0:T(8,128)S(1)}, u32[]{:S(2)}, u32[]{:S(2)}) collective-permute-start(f32[2,128,128]{2,1,0:T(8,128)S(1)} %add.138), channel_id=1, source_target_pairs={{0,64},{32,96},{64,0},{96,32},{128,192},{160,224},{192,128},{224,1... | collective-permute-start | bytes 393224 | tf_op jit(solution)/shard_map/ppermute | solution.py:14
  413.2 18.6 %collective-permute-start.6 = (f32[2,128,128]{2,1,0:T(8,128)S(1)}, f32[2,128,128]{2,1,0:T(8,128)S(1)}, u32[]{:S(2)}, u32[]{:S(2)}) collective-permute-start(f32[2,128,128]{2,1,0:T(8,128)S(1)} %add.140), channel_id=1, source_target_pairs={{0,128},{32,160},{64,192},{96,224},{128,0},{160,32},{192,64},{224,... | collective-permute-start | bytes 393224 | tf_op jit(solution)/shard_map/ppermute | solution.py:14
  431.8 22.0 %collective-permute-start.7 = (f32[2,128,128]{2,1,0:T(8,128)S(1)}, f32[2,128,128]{2,1,0:T(8,128)S(1)}, u32[]{:S(2)}, u32[]{:S(2)}) collective-permute-start(f32[2,128,128]{2,1,0:T(8,128)S(1)} %add.142), channel_id=1, source_target_pairs={{0,256},{32,288},{64,320},{96,352},{128,384},{160,416},{192,448},{... | collective-permute-start | bytes 393224 | tf_op jit(solution)/shard_map/ppermute | solution.py:14
  (14 other events, 15.3 us)
Sparse Core Ops, SparseCore 0:
  10.1 85.4 all-gather.5
  97.7 67.0 all-gather.9
  166.9 70.1 all-gather.7
  261.1 76.1 reduce-scatter.1

commit v8 on v7

--- a/solution.py
+++ b/solution.py
@@ -126,7 +126,6 @@
     w_rows = lax.all_to_all(w_blocks, "ep", 0, 0, tiled=True)
     portion = lax.all_gather(expert_in, "ctx", axis=0, tiled=True)
     square_sums = jnp.sum(gather_blocks(jnp.sum(stream_f * stream_f, -1, keepdims=True), "ep"), 0)
-    portion, w_rows, square_sums = lax.optimization_barrier((portion, w_rows, square_sums))
     row_scale = lax.rsqrt(square_sums / model_width + 1e-05)
     projected = jnp.concatenate([contract_last(portion, w_gate), contract_last(portion, w_up)], 1)
     pre_gate = projected[:, :hidden_block]
@@ -137,7 +136,12 @@
     grad_out = out_grad.astype(f32)
     grad_send = jnp.dot(dest_weights.T, grad_out, precision=high).astype(jnp.bfloat16)
     grad_in = lax.all_to_all(grad_send, "ep", split_axis=0, concat_axis=1, tiled=True)
-    grad_act = contract_last(lax.all_gather(grad_in, "ctx", axis=0, tiled=True), w_down)
+    grad_rows_all = lax.all_gather(grad_in, "ctx", axis=0, tiled=True)
+    portion, w_rows, square_sums, grad_rows_all = lax.optimization_barrier(
+        (portion, w_rows, square_sums, grad_rows_all)
+    )
+    row_scale = lax.rsqrt(square_sums / model_width + 1e-05)
+    grad_act = contract_last(grad_rows_all, w_down)
     grad_gate_pre = (grad_act * pre_up * gate_sig * (1.0 + pre_gate * (1.0 - gate_sig))).astype(
         jnp.bfloat16
     )

time: 465 us -> 462 us (level)
  starting transfers between devices: 104 us -> 109 us
  waiting for transfers between devices: 263 us -> 258 us
    ppermute x8, waiting for transfers between devices: 55.6 us -> 49.4 us  [butterfly_sums(): other = lax.ppermute(total, axis, [(i, i ^ step) for i in range(count)])]
    unnamed x91 -> x93, local copies, waits for them, and re-layouts: 9.99 us -> 10.4 us
  transfers between devices with their start and end apart: 19 -> 19, of which waited for: 13 -> 12; matrix products, arithmetic and copies ran while one was open for 7% -> 7% of each run, Pallas kernels for 0% -> 0%
where the time goes in v8:
time: 462 us; the launch traced here: 460 us
  waiting for transfers between devices  258 us (56%)
  starting transfers between devices  109 us (24%)
  local copies, waits for them, and re-layouts  35.1 us (8%)
  matrix products  19.3 us (4%)
  between operations  14.7 us (3%)
  blocking collectives  12.8 us (3%)
  other arithmetic  11.5 us (2%)
    reduce_scatter x1, waiting for transfers between devices, scatter_sum(): part = lax.psum_scatter(joined, axis, scatter_dimension=0, tiled=True)  75.8 us
    all_gather x1, waiting for transfers between devices, local(): portion = lax.all_gather(expert_in, 'ctx', axis=0, tiled=True)  68.1 us
    ppermute x8, starting transfers between devices, butterfly_sums(): other = lax.ppermute(total, axis, [(i, i ^ step) for i in range(count)])  50.9 us
    ppermute x8, waiting for transfers between devices, butterfly_sums(): other = lax.ppermute(total, axis, [(i, i ^ step) for i in range(count)])  49.4 us
    all_to_all x3, waiting for transfers between devices, gather_blocks(): return lax.all_to_all(spread, axis, 0, 0, tiled=True)  47.1 us
    all_to_all x3, starting transfers between devices, gather_blocks(): return lax.all_to_all(spread, axis, 0, 0, tiled=True)  22.2 us
    all_to_all x1, starting transfers between devices, local(): lax.all_to_all(payload, 'ep', split_axis=1, concat_axis=0, tiled=True)  18.3 us
    all_to_all x1, blocking collectives, local(): lax.all_to_all(picked.reshape(ep_count, capacity, columns), 'ep', 0, 0, t...  12.8 us
  transfers between devices with their start and end apart: 19, of which 12 were waited for; matrix products, arithmetic and copies ran while one was open for 7% of the time, Pallas kernels for 0%

profile of v8, /device:TPU:1, one launch (start us, length us, event | category | flops | bytes accessed | tf_op | source)
XLA Modules:
  0.0 460.4 jit_solution(4378941329821075117)
XLA Ops:
  7.9 1.0 copy.262
  8.9 1.0 fusion.47
  9.9 4.4 collective-permute-start
  17.7 4.9 %collective-permute-start.1 = (f32[2,128,128]{2,1,0:T(8,128)S(1)}, f32[2,128,128]{2,1,0:T(8,128)S(1)}, u32[]{:S(2)}, u32[]{:S(2)}) collective-permute-start(f32[2,128,128]{2,1,0:T(8,128)S(1)} %add.116), channel_id=1, source_target_pairs={{0,64},{32,96},{64,0},{96,32},{128,192},{160,224},{192,128},{224,1... | collective-permute-start | bytes 393224 | tf_op jit(solution)/shard_map/ppermute | solution.py:14
  23.9 8.4 %all-to-all-start.4 = ((bf16[32,20,96]{2,1,0:T(8,128)(2,1)}), bf16[32,20,96]{2,1,0:T(8,128)(2,1)S(1)}, u32[]{:S(2)}, u32[]{:S(2)}) async-start(bf16[32,20,96]{2,1,0:T(8,128)(2,1)} %all_to_all.56), calls=%async_computation.4 | async-start | bytes 393216 | tf_op jit(solution)/shard_map/all_to_all | solution.py:138
  32.5 8.8 %collective-permute-start.2 = (f32[2,128,128]{2,1,0:T(8,128)S(1)}, f32[2,128,128]{2,1,0:T(8,128)S(1)}, u32[]{:S(2)}, u32[]{:S(2)}) collective-permute-start(f32[2,128,128]{2,1,0:T(8,128)S(1)} %add.118), channel_id=1, source_target_pairs={{0,128},{32,160},{64,192},{96,224},{128,0},{160,32},{192,64},{224,... | collective-permute-start | bytes 393224 | tf_op jit(solution)/shard_map/ppermute | solution.py:14
  41.6 14.2 %collective-permute-done.2 = f32[2,128,128]{2,1,0:T(8,128)S(1)} collective-permute-done((f32[2,128,128]{2,1,0:T(8,128)S(1)}, f32[2,128,128]{2,1,0:T(8,128)S(1)}, u32[]{:S(2)}, u32[]{:S(2)}) %collective-permute-start.2) | collective-permute-done | bytes 131104 | tf_op jit(solution)/shard_map/ppermute | solution.py:14
  55.8 11.5 %collective-permute-start.3 = (f32[2,128,128]{2,1,0:T(8,128)S(1)}, f32[2,128,128]{2,1,0:T(8,128)S(1)}, u32[]{:S(2)}, u32[]{:S(2)}) collective-permute-start(f32[2,128,128]{2,1,0:T(8,128)S(1)} %add.120), channel_id=1, source_target_pairs={{0,256},{32,288},{64,320},{96,352},{128,384},{160,416},{192,448},{... | collective-permute-start | bytes 393224 | tf_op jit(solution)/shard_map/ppermute | solution.py:14
  67.5 4.1 collective-permute-done.3
  72.9 1.6 broadcast_in_dim.30
  74.5 14.6 %all-to-all-start = ((bf16[32,128,256]{2,1,0:T(8,128)(2,1)}), bf16[32,128,256]{2,1,0:T(8,128)(2,1)}, u32[]{:S(2)}, u32[]{:S(2)}) async-start(bf16[32,128,256]{2,1,0:T(8,128)(2,1)} %broadcast_in_dim.30), calls=%async_computation | async-start | bytes 4194304 | tf_op jit(solution)/shard_map/all_to_all | solution.py:26
  90.5 27.4 %all-to-all-done = bf16[32,128,256]{2,1,0:T(8,128)(2,1)} async-done(((bf16[32,128,256]{2,1,0:T(8,128)(2,1)}), bf16[32,128,256]{2,1,0:T(8,128)(2,1)}, u32[]{:S(2)}, u32[]{:S(2)}) %all-to-all-start) | async-done | bytes 2097184 | tf_op jit(solution)/shard_map/all_to_all | solution.py:26
  117.9 3.4 fusion.51
  121.7 12.8 %all_to_all.75 = bf16[32,20,96]{2,1,0:T(8,128)(2,1)S(1)} all-to-all(bf16[32,20,96]{2,1,0:T(8,128)(2,1)S(1)} %reshape.174), channel_id=1, replica_groups=mesh['ctx'=16,'ep'=32] {'ep'}, dimensions={0} | all-to-all | bytes 245760 | tf_op jit(solution)/shard_map/all_to_all | solution.py:116
  135.4 1.9 reshape.184
  137.5 1.7 fusion.37
  139.3 1.3 broadcast_in_dim.31
  140.5 3.8 all-to-all-start.3
  144.3 1.4 copy.265
  145.8 5.4 %all-to-all-done.3 = f32[32,128,1]{1,2,0:T(1,128)S(1)} async-done(((f32[32,128,1]{1,2,0:T(1,128)}), f32[32,128,1]{1,2,0:T(1,128)S(1)}, u32[]{:S(2)}, u32[]{:S(2)}) %all-to-all-start.3) | async-done | bytes 16416 | tf_op jit(solution)/shard_map/all_to_all | solution.py:26
  151.2 4.3 all-to-all-start.2
  155.8 8.7 %all-gather.10.cloned.1.call-done = bf16[16,20,3072]{2,1,0:T(8,128)(2,1)} async-done(((bf16[1,20,3072]{2,1,0:T(8,128)(2,1)}), bf16[16,20,3072]{2,1,0:T(8,128)(2,1)}) %all-gather.10.cloned.1.call-update) | async-done | bytes 1966096 | tf_op jit(solution)/shard_map/all_gather | solution.py:139
  164.5 4.0 reshape.188
  168.5 68.1 %all-gather.8.cloned.1.call-done = bf16[16,20,3072]{2,1,0:T(8,128)(2,1)} async-done(((bf16[1,20,3072]{2,1,0:T(8,128)(2,1)}), bf16[16,20,3072]{2,1,0:T(8,128)(2,1)}) %all-gather.8.cloned.1.call-update) | async-done | bytes 1966096 | tf_op jit(solution)/shard_map/all_gather | solution.py:127
  236.5 3.9 reshape.186
  240.5 3.4 fusion.5
  243.9 0.9 fusion.9
  248.4 2.0 fusion
  250.5 3.9 reshape.177
  254.4 2.1 reshape.175
  256.5 5.2 %pad_maximum_fusion = bf16[16,40,3072]{2,1,0:T(8,128)(2,1)} fusion(bf16[16,20,3072]{2,1,0:T(8,128)(2,1)} %reshape.177, bf16[16,20,3072]{2,1,0:T(8,128)(2,1)} %reshape.175), kind=kLoop, calls=%fused_computation.3 | loop fusion | flops 7864320 | bytes 7864320 | tf_op jit(solution)/shard_map/concatenate | solution.py:33
  261.9 75.8 %reduce-scatter.2.cloned.1.call-done = bf16[1,40,3072]{2,1,0:T(8,128)(2,1)} async-done(((bf16[16,40,3072]{2,1,0:T(8,128)(2,1)}), bf16[1,40,3072]{2,1,0:T(8,128)(2,1)}) %reduce-scatter.2.cloned.1.call-update) | async-done | bytes 245776 | tf_op jit(solution)/shard_map/reduce_scatter | solution.py:34
  337.7 1.7 fusion.65
  340.8 18.3 %all-to-all-start.5 = ((bf16[20,32,98]{2,0,1:T(8,128)(2,1)}), bf16[20,32,98]{2,0,1:T(8,128)(2,1)S(1)}, u32[]{:S(2)}, u32[]{:S(2)}) async-start(bf16[20,32,98]{2,0,1:T(8,128)(2,1)} %copy.203), calls=%async_computation.6 | async-start | bytes 393216 | tf_op jit(solution)/shard_map/all_to_all | solution.py:161
  359.1 8.2 %all-to-all-done.5 = bf16[20,32,98]{2,0,1:T(8,128)(2,1)S(1)} async-done(((bf16[20,32,98]{2,0,1:T(8,128)(2,1)}), bf16[20,32,98]{2,0,1:T(8,128)(2,1)S(1)}, u32[]{:S(2)}, u32[]{:S(2)}) %all-to-all-start.5) | async-done | bytes 125472 | tf_op jit(solution)/shard_map/all_to_all | solution.py:161
  368.8 1.3 fusion.25
  370.1 1.0 broadcast_in_dim.33
  371.1 3.8 all-to-all-start.6
  374.9 14.3 %all-to-all-done.6 = bf16[32,128,96]{1,2,0:T(8,128)(2,1)S(1)} async-done(((bf16[32,128,96]{1,2,0:T(8,128)(2,1)}), bf16[32,128,96]{1,2,0:T(8,128)(2,1)S(1)}, u32[]{:S(2)}, u32[]{:S(2)}) %all-to-all-start.6) | async-done | bytes 786464 | tf_op jit(solution)/shard_map/all_to_all | solution.py:26
  390.7 2.6 collective-permute-start.4
  395.4 4.5 all-to-all-start.7
  399.9 4.3 collective-permute-start.5
  404.4 6.1 %collective-permute-done.5 = f32[2,128,128]{2,1,0:T(8,128)S(1)} collective-permute-done((f32[2,128,128]{2,1,0:T(8,128)S(1)}, f32[2,128,128]{2,1,0:T(8,128)S(1)}, u32[]{:S(2)}, u32[]{:S(2)}) %collective-permute-start.5) | collective-permute-done | bytes 131104 | tf_op jit(solution)/shard_map/ppermute | solution.py:14
  410.6 6.0 %collective-permute-start.6 = (f32[2,128,128]{2,1,0:T(8,128)S(1)}, f32[2,128,128]{2,1,0:T(8,128)S(1)}, u32[]{:S(2)}, u32[]{:S(2)}) collective-permute-start(f32[2,128,128]{2,1,0:T(8,128)S(1)} %add.140), channel_id=1, source_target_pairs={{0,128},{32,160},{64,192},{96,224},{128,0},{160,32},{192,64},{224,... | collective-permute-start | bytes 393224 | tf_op jit(solution)/shard_map/ppermute | solution.py:14
  416.8 11.7 %collective-permute-done.6 = f32[2,128,128]{2,1,0:T(8,128)S(1)} collective-permute-done((f32[2,128,128]{2,1,0:T(8,128)S(1)}, f32[2,128,128]{2,1,0:T(8,128)S(1)}, u32[]{:S(2)}, u32[]{:S(2)}) %collective-permute-start.6) | collective-permute-done | bytes 131104 | tf_op jit(solution)/shard_map/ppermute | solution.py:14
  428.5 8.4 %collective-permute-start.7 = (f32[2,128,128]{2,1,0:T(8,128)S(1)}, f32[2,128,128]{2,1,0:T(8,128)S(1)}, u32[]{:S(2)}, u32[]{:S(2)}) collective-permute-start(f32[2,128,128]{2,1,0:T(8,128)S(1)} %add.142), channel_id=1, source_target_pairs={{0,256},{32,288},{64,320},{96,352},{128,384},{160,416},{192,448},{... | collective-permute-start | bytes 393224 | tf_op jit(solution)/shard_map/ppermute | solution.py:14
  437.0 1.0 fusion.26
  438.0 13.2 %collective-permute-done.7 = f32[2,128,128]{2,1,0:T(8,128)S(1)} collective-permute-done((f32[2,128,128]{2,1,0:T(8,128)S(1)}, f32[2,128,128]{2,1,0:T(8,128)S(1)}, u32[]{:S(2)}, u32[]{:S(2)}) %collective-permute-start.7) | collective-permute-done | bytes 131104 | tf_op jit(solution)/shard_map/ppermute | solution.py:14
  (177 shorter events, 23.3 us)
Async XLA Ops:
  7.2 237.7 %copy-start = (bf16[1,192,3072]{2,1,0:T(8,128)(2,1)S(1)}, bf16[1,192,3072]{2,1,0:T(8,128)(2,1)}, u32[]{:S(2)}) copy-start(bf16[1,192,3072]{2,1,0:T(8,128)(2,1)} %param.28) | copy-start | bytes 3538948
  7.2 15.4 %copy-start.34 = (bf16[128,96]{0,1:T(8,128)(2,1)S(1)}, bf16[128,96]{0,1:T(8,128)(2,1)}, u32[]{:S(2)}) copy-start(bf16[128,96]{0,1:T(8,128)(2,1)} %param.29) | copy-start | bytes 73732
  7.2 110.7 %all-gather.6.cloned.1.call-start = ((), (), s32[]{:S(2)}) async-start(), calls=%async_computation.9 | async-start | bytes 1671168 | tf_op jit(solution)/shard_map/all_gather | solution.py:77
  8.9 7.8 %copy-start.21 = (bf16[128,256]{0,1:T(8,128)(2,1)}, bf16[128,256]{0,1:T(8,128)(2,1)S(1)}, u32[]{:S(2)}) copy-start(bf16[128,256]{0,1:T(8,128)(2,1)S(1)} %copy.262) | copy-start | bytes 196612
  9.9 7.8 %collective-permute-start = (f32[2,128,128]{2,1,0:T(8,128)S(1)}, f32[2,128,128]{2,1,0:T(8,128)S(1)}, u32[]{:S(2)}, u32[]{:S(2)}) collective-permute-start(f32[2,128,128]{2,1,0:T(8,128)S(1)} %fusion.47), channel_id=1, source_target_pairs={{0,32},{32,0},{64,96},{96,64},{128,160},{160,128},{192,224},{224,1... | collective-permute-start | bytes 393224 | tf_op jit(solution)/shard_map/ppermute | solution.py:14
  15.7 16.6 %copy-start.35 = (bf16[128,256]{1,0:T(8,128)(2,1)S(1)}, bf16[128,256]{1,0:T(8,128)(2,1)}, u32[]{:S(2)}) copy-start(bf16[128,256]{1,0:T(8,128)(2,1)} %param.15) | copy-start | bytes 196612
  16.7 24.7 %copy-start.26 = (bf16[128,256]{1,0:T(8,128)(2,1)S(1)}, bf16[128,256]{1,0:T(8,128)(2,1)}, u32[]{:S(2)}) copy-start(bf16[128,256]{1,0:T(8,128)(2,1)} %param.16) | copy-start | bytes 196612
  17.6 49.7 %copy-start.23 = (bf16[128,256]{1,0:T(8,128)(2,1)S(1)}, bf16[128,256]{1,0:T(8,128)(2,1)}, u32[]{:S(2)}) copy-start(bf16[128,256]{1,0:T(8,128)(2,1)} %param.17) | copy-start | bytes 196612
  17.6 54.0 %copy-start.32 = (f32[2,128,128]{2,1,0:T(8,128)S(1)}, f32[2,128,128]{2,1,0:T(8,128)}, u32[]{:S(2)}) copy-start(f32[2,128,128]{2,1,0:T(8,128)} %param.18) | copy-start | bytes 393220
  17.7 14.8 %collective-permute-start.1 = (f32[2,128,128]{2,1,0:T(8,128)S(1)}, f32[2,128,128]{2,1,0:T(8,128)S(1)}, u32[]{:S(2)}, u32[]{:S(2)}) collective-permute-start(f32[2,128,128]{2,1,0:T(8,128)S(1)} %add.116), channel_id=1, source_target_pairs={{0,64},{32,96},{64,0},{96,32},{128,192},{160,224},{192,128},{224,1... | collective-permute-start | bytes 393224 | tf_op jit(solution)/shard_map/ppermute | solution.py:14
  23.0 49.7 %copy-start.37 = (f32[256]{0:T(256)S(1)}, f32[256]{0:T(256)}, u32[]{:S(2)}) copy-start(f32[256]{0:T(256)} %param.19) | copy-start | bytes 3076
  23.9 49.0 %all-to-all-start.4 = ((bf16[32,20,96]{2,1,0:T(8,128)(2,1)}), bf16[32,20,96]{2,1,0:T(8,128)(2,1)S(1)}, u32[]{:S(2)}, u32[]{:S(2)}) async-start(bf16[32,20,96]{2,1,0:T(8,128)(2,1)} %all_to_all.56), calls=%async_computation.4 | async-start | bytes 393216 | tf_op jit(solution)/shard_map/all_to_all | solution.py:138
  32.4 42.1 %copy-start.17 = (bf16[128,256]{0,1:T(8,128)(2,1)}, bf16[128,256]{0,1:T(8,128)(2,1)S(1)}, u32[]{:S(2)}) copy-start(bf16[128,256]{0,1:T(8,128)(2,1)S(1)} %copy.229) | copy-start | bytes 196612
  32.5 23.3 %collective-permute-start.2 = (f32[2,128,128]{2,1,0:T(8,128)S(1)}, f32[2,128,128]{2,1,0:T(8,128)S(1)}, u32[]{:S(2)}, u32[]{:S(2)}) collective-permute-start(f32[2,128,128]{2,1,0:T(8,128)S(1)} %add.118), channel_id=1, source_target_pairs={{0,128},{32,160},{64,192},{96,224},{128,0},{160,32},{192,64},{224,... | collective-permute-start | bytes 393224 | tf_op jit(solution)/shard_map/ppermute | solution.py:14
  41.6 33.0 %copy-start.28 = (bf16[2,128,128]{2,1,0:T(8,128)(2,1)}, bf16[2,128,128]{2,1,0:T(8,128)(2,1)S(1)}, u32[]{:S(2)}) copy-start(bf16[2,128,128]{2,1,0:T(8,128)(2,1)S(1)} %fusion.14) | copy-start | bytes 196612
  55.8 15.8 %collective-permute-start.3 = (f32[2,128,128]{2,1,0:T(8,128)S(1)}, f32[2,128,128]{2,1,0:T(8,128)S(1)}, u32[]{:S(2)}, u32[]{:S(2)}) collective-permute-start(f32[2,128,128]{2,1,0:T(8,128)S(1)} %add.120), channel_id=1, source_target_pairs={{0,256},{32,288},{64,320},{96,352},{128,384},{160,416},{192,448},{... | collective-permute-start | bytes 393224 | tf_op jit(solution)/shard_map/ppermute | solution.py:14
  74.5 43.4 %all-to-all-start = ((bf16[32,128,256]{2,1,0:T(8,128)(2,1)}), bf16[32,128,256]{2,1,0:T(8,128)(2,1)}, u32[]{:S(2)}, u32[]{:S(2)}) async-start(bf16[32,128,256]{2,1,0:T(8,128)(2,1)} %broadcast_in_dim.30), calls=%async_computation | async-start | bytes 4194304 | tf_op jit(solution)/shard_map/all_to_all | solution.py:26
  89.2 28.7 %copy-start.43 = (bf16[128,96]{0,1:T(8,128)(2,1)S(1)}, bf16[128,96]{0,1:T(8,128)(2,1)}, u32[]{:S(2)}) copy-start(bf16[128,96]{0,1:T(8,128)(2,1)} %param.21) | copy-start | bytes 73732
  89.2 75.3 %all-gather.10.cloned.1.call-start = ((), (), s32[]{:S(2)}) async-start(), calls=%async_computation.12 | async-start | bytes 2506752 | tf_op jit(solution)/shard_map/all_gather | solution.py:139
  90.2 146.4 %all-gather.8.cloned.1.call-start = ((), (), s32[]{:S(2)}) async-start(), calls=%async_computation.11 | async-start | bytes 2506752 | tf_op jit(solution)/shard_map/all_gather | solution.py:127
  121.3 247.5 %copy-start.30 = (bf16[128,96]{0,1:T(8,128)(2,1)}, bf16[128,96]{0,1:T(8,128)(2,1)S(1)}, u32[]{:S(2)}) copy-start(bf16[128,96]{0,1:T(8,128)(2,1)S(1)} %get-tuple-element.63) | copy-start | bytes 73732
  121.3 16.2 %copy-start.36 = (f32[3072]{0:T(1024)S(1)}, f32[3072]{0:T(1024)}, u32[]{:S(2)}) copy-start(f32[3072]{0:T(1024)} %param.22) | copy-start | bytes 36868
  121.5 22.8 %copy-start.11 = (bf16[8192,96]{0,1:T(8,128)(2,1)S(1)}, bf16[8192,96]{0,1:T(8,128)(2,1)}, u32[]{:S(2)}) copy-start(bf16[8192,96]{0,1:T(8,128)(2,1)} %all-gather.6.cloned.1.call-done) | copy-start | bytes 4718596
  134.6 11.2 %copy-start.3 = (bf16[32,20,96]{2,1,0:T(8,128)(2,1)}, bf16[32,20,96]{2,1,0:T(8,128)(2,1)S(1)}, u32[]{:S(2)}) copy-start(bf16[32,20,96]{2,1,0:T(8,128)(2,1)S(1)} %all_to_all.75) | copy-start | bytes 368644
  140.5 10.7 %all-to-all-start.3 = ((f32[32,128,1]{1,2,0:T(1,128)}), f32[32,128,1]{1,2,0:T(1,128)S(1)}, u32[]{:S(2)}, u32[]{:S(2)}) async-start(f32[32,128,1]{1,2,0:T(1,128)} %broadcast_in_dim.31), calls=%async_computation.3 | async-start | bytes 32768 | tf_op jit(solution)/shard_map/all_to_all | solution.py:26
  151.2 89.2 %all-to-all-start.2 = ((bf16[32,256,96]{1,2,0:T(8,128)(2,1)}), bf16[32,256,96]{1,2,0:T(8,128)(2,1)S(1)}, u32[]{:S(2)}, u32[]{:S(2)}) async-start(bf16[32,256,96]{1,2,0:T(8,128)(2,1)} %bitcast.172), calls=%async_computation.2 | async-start | bytes 3145728 | tf_op jit(solution)/shard_map/all_to_all | solution.py:126
  155.5 182.2 %reduce-scatter.2.cloned.1.call-start = ((), (), s32[]{:S(2)}) async-start(), calls=%async_computation.10 | async-start | bytes 4177920 | tf_op jit(solution)/shard_map/reduce_scatter | solution.py:34
  240.5 4.4 copy-start.1
  240.5 3.4 copy-start.10
  240.5 3.4 copy-start.15
  261.8 77.8 %copy-start.4 = (bf16[32,20,96]{2,1,0:T(8,128)(2,1)S(1)}, bf16[32,20,96]{2,1,0:T(8,128)(2,1)}, u32[]{:S(2)}) copy-start(bf16[32,20,96]{2,1,0:T(8,128)(2,1)} %copy-done.3) | copy-start | bytes 368644
  340.8 26.6 %all-to-all-start.5 = ((bf16[20,32,98]{2,0,1:T(8,128)(2,1)}), bf16[20,32,98]{2,0,1:T(8,128)(2,1)S(1)}, u32[]{:S(2)}, u32[]{:S(2)}) async-start(bf16[20,32,98]{2,0,1:T(8,128)(2,1)} %copy.203), calls=%async_computation.6 | async-start | bytes 393216 | tf_op jit(solution)/shard_map/all_to_all | solution.py:161
  368.1 21.0 %copy-start.2 = (bf16[32,256,96]{1,2,0:T(8,128)(2,1)S(1)}, bf16[32,256,96]{1,2,0:T(8,128)(2,1)}, u32[]{:S(2)}) copy-start(bf16[32,256,96]{1,2,0:T(8,128)(2,1)} %copy-done.1) | copy-start | bytes 4718596
  371.1 18.1 %all-to-all-start.6 = ((bf16[32,128,96]{1,2,0:T(8,128)(2,1)}), bf16[32,128,96]{1,2,0:T(8,128)(2,1)S(1)}, u32[]{:S(2)}, u32[]{:S(2)}) async-start(bf16[32,128,96]{1,2,0:T(8,128)(2,1)} %broadcast_in_dim.33), calls=%async_computation.7 | async-start | bytes 1572864 | tf_op jit(solution)/shard_map/all_to_all | solution.py:26
  389.2 4.2 copy-start.22
  389.2 4.3 copy-start.14
  389.9 4.5 copy-start.20
  390.0 14.3 %copy-start.29 = (bf16[2,128,128]{2,1,0:T(8,128)(2,1)S(1)}, bf16[2,128,128]{2,1,0:T(8,128)(2,1)}, u32[]{:S(2)}) copy-start(bf16[2,128,128]{2,1,0:T(8,128)(2,1)} %copy-done.28) | copy-start | bytes 196612
  390.1 26.6 %copy-start.19 = (bf16[128,256]{0,1:T(8,128)(2,1)S(1)}, bf16[128,256]{0,1:T(8,128)(2,1)}, u32[]{:S(2)}) copy-start(bf16[128,256]{0,1:T(8,128)(2,1)} %copy-done.17) | copy-start | bytes 196612
  390.3 46.7 %copy-start.6 = (f32[128,32,20]{0,1,2:T(8,128)S(1)}, f32[128,32,20]{0,1,2:T(8,128)}, u32[]{:S(2)}) copy-start(f32[128,32,20]{0,1,2:T(8,128)} %copy-done.5) | copy-start | bytes 983044
  390.3 46.7 %copy-start.31 = (bf16[128,96]{0,1:T(8,128)(2,1)S(1)}, bf16[128,96]{0,1:T(8,128)(2,1)}, u32[]{:S(2)}) copy-start(bf16[128,96]{0,1:T(8,128)(2,1)} %copy-done.30) | copy-start | bytes 73732
  390.7 9.1 %collective-permute-start.4 = (f32[2,128,128]{2,1,0:T(8,128)S(1)}, f32[2,128,128]{2,1,0:T(8,128)S(1)}, u32[]{:S(2)}, u32[]{:S(2)}) collective-permute-start(f32[2,128,128]{2,1,0:T(8,128)S(1)} %convolution_bitcast_fusion.4), channel_id=1, source_target_pairs={{0,32},{32,0},{64,96},{96,64},{128,160},{160,128},{192,224},{224,1... | collective-permute-start | bytes 393224 | tf_op jit(solution)/shard_map/ppermute | solution.py:14
  394.7 57.2 %copy-start.27 = (bf16[128,256]{1,0:T(8,128)(2,1)S(1)}, bf16[128,256]{1,0:T(8,128)(2,1)}, u32[]{:S(2)}) copy-start(bf16[128,256]{1,0:T(8,128)(2,1)} %param.16) | copy-start | bytes 196612
  395.4 57.5 %copy-start.25 = (bf16[128,256]{1,0:T(8,128)(2,1)S(1)}, bf16[128,256]{1,0:T(8,128)(2,1)}, u32[]{:S(2)}) copy-start(bf16[128,256]{1,0:T(8,128)(2,1)} %param.17) | copy-start | bytes 196612
  395.4 41.6 %all-to-all-start.7 = ((bf16[20,32,96]{2,0,1:T(8,128)(2,1)}), bf16[20,32,96]{2,0,1:T(8,128)(2,1)S(1)}, u32[]{:S(2)}, u32[]{:S(2)}) async-start(bf16[20,32,96]{2,0,1:T(8,128)(2,1)} %copy.207), calls=%async_computation.8 | async-start | bytes 393216 | tf_op jit(solution)/shard_map/all_to_all | solution.py:182
  399.9 10.6 %collective-permute-start.5 = (f32[2,128,128]{2,1,0:T(8,128)S(1)}, f32[2,128,128]{2,1,0:T(8,128)S(1)}, u32[]{:S(2)}, u32[]{:S(2)}) collective-permute-start(f32[2,128,128]{2,1,0:T(8,128)S(1)} %add.138), channel_id=1, source_target_pairs={{0,64},{32,96},{64,0},{96,32},{128,192},{160,224},{192,128},{224,1... | collective-permute-start | bytes 393224 | tf_op jit(solution)/shard_map/ppermute | solution.py:14
  410.6 17.9 %collective-permute-start.6 = (f32[2,128,128]{2,1,0:T(8,128)S(1)}, f32[2,128,128]{2,1,0:T(8,128)S(1)}, u32[]{:S(2)}, u32[]{:S(2)}) collective-permute-start(f32[2,128,128]{2,1,0:T(8,128)S(1)} %add.140), channel_id=1, source_target_pairs={{0,128},{32,160},{64,192},{96,224},{128,0},{160,32},{192,64},{224,... | collective-permute-start | bytes 393224 | tf_op jit(solution)/shard_map/ppermute | solution.py:14
  428.5 22.6 %collective-permute-start.7 = (f32[2,128,128]{2,1,0:T(8,128)S(1)}, f32[2,128,128]{2,1,0:T(8,128)S(1)}, u32[]{:S(2)}, u32[]{:S(2)}) collective-permute-start(f32[2,128,128]{2,1,0:T(8,128)S(1)} %add.142), channel_id=1, source_target_pairs={{0,256},{32,288},{64,320},{96,352},{128,384},{160,416},{192,448},{... | collective-permute-start | bytes 393224 | tf_op jit(solution)/shard_map/ppermute | solution.py:14
  (15 other events, 18.3 us)
Sparse Core Ops, SparseCore 0:
  10.1 84.8 all-gather.5
  97.1 67.3 all-gather.9
  166.6 69.8 all-gather.7
  261.9 75.7 reduce-scatter.1
